TPU v7x, 32 devices: a whole 2x2x4 slice. The times are simulated.
32 devices in a mesh: grp: 2 (over y), row: 4 (over z), head: 2 (over x), rep: 2 (over core).
Axes of the slice: x: 2, y: 2, z: 4, core: 2. Of those that a mesh axis runs over, the one named last changes fastest.
Arguments:
- queries: float32 [2048, 8192], P(('grp', 'row', 'rep'), 'head'), parts along dimension 0
- key_max: float32 [4096, 1024], P(('grp', 'row', 'rep'), 'head'), parts along dimension 0
- key_min: float32 [4096, 1024], P(('grp', 'row', 'rep'), 'head'), parts along dimension 0, as said below
- limits: int32 [2048], P(('grp', 'row', 'rep')), parts along dimension 0, may hold values from 0 to 2047, as said below
Outputs:
- page_mass: float32 [2048, 2048], P(('grp', 'row', 'rep'), 'head'), parts along dimension 0
There are 2 independent parts, one for each index of `grp`. A program takes and returns all parts, laid end to end along the dimension named above; each array names one. Nothing has to cross between parts.
Inputs may be any that keep to these rules, and one draw needn't show every extreme that they name: key_min <= key_max in every entry. Rows of the i-th aligned block of 128 rows have limits within the i-th block of 256 pages, not falling within a block; the first block's first row has the first page and the last block's last row the last page.
All inputs are finite; a program needn't handle non-finite values.
Results may differ from a plain program's by a relative error of at most 0.00013.
Values sent between devices are 32-bit elements; how exact they have to be, the bound alone decides.
No kernel may reach another device: no remote copies, remote signals or barrier semaphores. Data moves between devices by JAX's collectives and lax.ppermute only.
A program may use at most 64 MiB of HBM per device.

v0:
```python
import math

import jax
import jax.numpy as jnp
from jax import lax
from jax.sharding import PartitionSpec as P

DH = 128


def per_device(queries, key_max, key_min, limits):
    head_count = queries.shape[1] // DH
    kv_count = key_max.shape[1] // DH
    group_size = head_count // kv_count
    score_scale = 1.0 / math.sqrt(DH)
    bounds = jnp.stack((key_max, key_min))
    query_rows, row_limits = (queries, limits)
    gathered = lax.all_gather(bounds, ("row", "rep"), axis=1, tiled=True)
    page_ids = jnp.arange(gathered.shape[1], dtype=jnp.int32)
    row_count = query_rows.shape[0]
    page_count = gathered.shape[1]
    head_rows = query_rows.reshape(row_count, head_count, DH).transpose(1, 0, 2)
    positive = jnp.maximum(head_rows, 0.0)
    negative = jnp.minimum(head_rows, 0.0)
    sheets = gathered.reshape(2, page_count, kv_count, DH).transpose(2, 0, 1, 3)
    visible = page_ids[None, :] <= row_limits[:, None]

    def head_scores(head_index, kv_index):
        upper_part = jnp.dot(
            positive[head_index], sheets[kv_index, 0].T, precision=lax.Precision.HIGHEST
        )
        return upper_part + jnp.dot(
            negative[head_index], sheets[kv_index, 1].T, precision=lax.Precision.HIGHEST
        )

    def head_step(accumulated, head_index):
        raw_scores = head_scores(head_index, head_index // group_size)
        masked = jnp.where(visible, raw_scores * score_scale, -1e30)
        row_top = jnp.max(masked, axis=1, keepdims=True)
        weights = jnp.exp(masked - row_top)
        row_total = jnp.sum(weights, axis=1, keepdims=True)
        return (accumulated + weights / row_total, None)

    start = jnp.zeros((row_count, page_count), jnp.float32)
    accumulated, unused = lax.scan(head_step, start, jnp.arange(head_count, dtype=jnp.int32))
    return lax.psum_scatter(accumulated, "head", scatter_dimension=1, tiled=True)


def solution(mesh):
    placed = (
        P(("grp", "row", "rep"), "head"),
        P(("grp", "row", "rep"), "head"),
        P(("grp", "row", "rep"), "head"),
        P(("grp", "row", "rep")),
    )
    return jax.shard_map(
        per_device,
        mesh=mesh,
        in_specs=placed,
        out_specs=P(("grp", "row", "rep"), "head"),
        check_vma=False,
    )
```

profile of v0, /device:TPU:16, one launch (start us, length us, event | category | flops | bytes accessed | tf_op | source)
XLA Modules:
  0.0 446.9 jit_solution(9973003947528456110)
XLA Ops:
  14.3 77.6 %all-gather.2.cloned.1.call-done = f32[2,2048,512]{1,2,0:T(8,128)} async-done(((f32[2,256,512]{1,2,0:T(8,128)}), f32[2,2048,512]{1,2,0:T(8,128)}) %all-gather.2.cloned.1.call-update) | async-done | bytes 8388624 | tf_op jit(solution)/shard_map/all_gather | solution.py:18
  91.9 8.7 %copy.10 = f32[4,2,2048,128]{3,2,1,0:T(8,128)} copy(f32[4,2,2048,128]{2,3,0,1:T(8,128)} %bitcast.40) | data formatting | bytes 16777216
  100.7 318.0 %while.13 = (s32[]{:T(128)}, f32[128,2048]{1,0:T(8,128)S(1)}, s32[32]{0:T(128)S(1)}, f32[32,128,128]{1,2,0:T(8,128)}, f32[4,2,2048,128]{3,2,1,0:T(8,128)}, /*ind...) while((s32[]{:T(128)}, f32[128,2048]{1,0:T(8,128)S(1)}, ...), condition=%wide.region_3.4_spmd.clone, body=%wide.region_0.3_spmd.clone.sunk | while | flops 808189696 | bytes 9571716 | solution.py:45
  107.4 2.6 fusion.26
  117.3 2.6 fusion.26
  127.2 2.6 fusion.26
  137.2 2.6 fusion.26
  147.1 2.6 fusion.26
  157.0 2.6 fusion.26
  167.0 2.6 fusion.26
  176.9 2.6 fusion.26
  186.8 2.6 fusion.26
  196.8 2.6 fusion.26
  206.7 2.6 fusion.26
  216.7 2.6 fusion.26
  226.6 2.6 fusion.26
  286.2 2.6 fusion.26
  296.2 2.6 fusion.26
  306.1 2.6 fusion.26
  375.6 2.6 fusion.26
  385.6 2.6 fusion.26
  395.5 2.6 fusion.26
  405.5 2.6 fusion.26
  419.6 20.4 %reduce-scatter.2.cloned.1.call-done = f32[128,1024]{1,0:T(8,128)} async-done(((f32[128,2048]{1,0:T(8,128)}), f32[128,1024]{1,0:T(8,128)}) %reduce-scatter.2.cloned.1.call-update) | async-done | bytes 524304 | tf_op jit(solution)/shard_map/reduce_scatter | solution.py:46
  (155 shorter events, 154.2 us)
Async XLA Ops:
  6.5 85.4 %all-gather.2.cloned.1.call-start = ((), (), s32[]{:S(2)}) async-start(), calls=%async_computation.1 | async-start | bytes 9437184 | tf_op jit(solution)/shard_map/all_gather | solution.py:18
  10.1 430.0 %reduce-scatter.2.cloned.1.call-start = ((), (), s32[]{:S(2)}) async-start(), calls=%async_computation.2 | async-start | bytes 1572864 | tf_op jit(solution)/shard_map/reduce_scatter | solution.py:46
  91.9 8.8 %copy-start.1 = (s32[128]{0:T(128)S(1)}, s32[128]{0:T(128)}, u32[]{:S(2)}) copy-start(s32[128]{0:T(128)} %param.9) | copy-start | bytes 1540
  418.6 1.0 copy-start
Sparse Core Ops, SparseCore 0:
  10.2 81.6 all-gather.1
  419.8 20.2 reduce-scatter.1
where the time goes:
time: 452 us; the launch traced here: 447 us
  matrix products  157 us (35%)
  loops' own time  121 us (27%)
  waiting for transfers between devices  98.1 us (22%)
  local copies, waits for them, and re-layouts  33.2 us (7%)
  other arithmetic  24.4 us (5%)
  between operations  13.4 us (3%)
    another operation x1, loops' own time, per_device(): lax.scan(head_step, start, jnp.arange(head_count, dtype=jnp.int32))  121 us
    dot_general x32, matrix products, head_scores(): jnp.dot(negative[head_index], sheets[kv_index, 1].T, precision=lax.Precis...  82.2 us
    all_gather x1, waiting for transfers between devices, per_device(): gathered = lax.all_gather(bounds, ('row', 'rep'), axis=1, tiled=True)  77.6 us
    dot_general x32, matrix products, head_scores(): jnp.dot(positive[head_index], sheets[kv_index, 0].T, precision=lax.Precis...  74.5 us
    reduce_scatter x1, waiting for transfers between devices, per_device(): lax.psum_scatter(accumulated, 'head', scatter_dimension=1, tiled=True)  20.4 us
    dynamic_slice x32, local copies, waits for them, and re-layouts, per_device(): lax.scan(head_step, start, jnp.arange(head_count, dtype=jnp.int32))  19.1 us
    unnamed x8, local copies, waits for them, and re-layouts  14.1 us
    add x32, other arithmetic, head_step(): return (accumulated + weights / row_total, None)  11.5 us
  transfers between devices with their start and end apart: 2, of which 2 were waited for; matrix products, arithmetic and copies ran while one was open for 1% of the time, Pallas kernels for 0%

commit v1 on v0

v1 whole, which is shorter than its diff:
```python
import functools
import math

import jax
import jax.numpy as jnp
from jax import lax
from jax.experimental import pallas as pl
from jax.experimental.pallas import tpu as pltpu
from jax.sharding import PartitionSpec as P

DH = 128
CHUNK = 256
ROW_STRIP = 8


def _split(x):
    hi = x.astype(jnp.bfloat16)
    lo = (x - hi.astype(jnp.float32)).astype(jnp.bfloat16)
    return hi, lo


def _mass_kernel(nb_ref, q_ref, k_ref, lim_ref, out_ref, khi_ref, klo_ref, s_ref,
                 *, group_size, chunk_count, score_scale):
    h = pl.program_id(0)
    nb = nb_ref[0]
    row_count, page_count = s_ref.shape

    @pl.when(h == 0)
    def _():
        out_ref[...] = jnp.zeros_like(out_ref)

    @pl.when(h % group_size == 0)
    def _():
        for c in range(chunk_count):
            @pl.when(c < nb)
            def _():
                kc = k_ref[c * CHUNK:(c + 1) * CHUNK, :].T
                hi, lo = _split(kc)
                khi_ref[:, c * CHUNK:(c + 1) * CHUNK] = hi
                klo_ref[:, c * CHUNK:(c + 1) * CHUNK] = lo

    q = q_ref[...]
    x = jnp.concatenate([jnp.maximum(q, 0.0), jnp.minimum(q, 0.0)], axis=1) * score_scale
    xhi, xlo = _split(x)

    for c in range(chunk_count):
        @pl.when(c < nb)
        def _():
            khi = khi_ref[:, c * CHUNK:(c + 1) * CHUNK]
            klo = klo_ref[:, c * CHUNK:(c + 1) * CHUNK]
            s = jnp.dot(xhi, khi, preferred_element_type=jnp.float32)
            s = s + jnp.dot(xhi, klo, preferred_element_type=jnp.float32)
            s = s + jnp.dot(xlo, khi, preferred_element_type=jnp.float32)
            s_ref[:, c * CHUNK:(c + 1) * CHUNK] = s

    def strip(i, carry):
        r0 = pl.multiple_of(i * ROW_STRIP, ROW_STRIP)
        sv = s_ref[pl.ds(r0, ROW_STRIP), :]
        lim = lim_ref[pl.ds(r0, ROW_STRIP), :]
        pages = lax.broadcasted_iota(jnp.int32, sv.shape, 1)
        sm = jnp.where(pages <= lim, sv, -1e30)
        top = jnp.max(sm, axis=1, keepdims=True)
        e = jnp.exp(sm - top)
        total = jnp.sum(e, axis=1, keepdims=True)
        out_ref[pl.ds(r0, ROW_STRIP), :] += e * (1.0 / total)
        return carry

    lax.fori_loop(0, row_count // ROW_STRIP, strip, 0)


def page_mass_local(queries, keys, limits):
    row_count = queries.shape[0]
    head_count = queries.shape[1] // DH
    page_count = keys.shape[0]
    kv_count = keys.shape[1] // (2 * DH)
    group_size = head_count // kv_count
    chunk_count = page_count // CHUNK
    nb = (jnp.max(limits) // CHUNK + 1).astype(jnp.int32).reshape(1)
    kernel = functools.partial(
        _mass_kernel, group_size=group_size, chunk_count=chunk_count,
        score_scale=1.0 / math.sqrt(DH))
    grid_spec = pltpu.PrefetchScalarGridSpec(
        num_scalar_prefetch=1,
        grid=(head_count,),
        in_specs=[
            pl.BlockSpec((row_count, DH), lambda h, nb: (0, h)),
            pl.BlockSpec((page_count, 2 * DH), lambda h, nb: (0, h // group_size)),
            pl.BlockSpec((row_count, 1), lambda h, nb: (0, 0)),
        ],
        out_specs=pl.BlockSpec((row_count, page_count), lambda h, nb: (0, 0)),
        scratch_shapes=[
            pltpu.VMEM((2 * DH, page_count), jnp.bfloat16),
            pltpu.VMEM((2 * DH, page_count), jnp.bfloat16),
            pltpu.VMEM((row_count, page_count), jnp.float32),
        ],
    )
    return pl.pallas_call(
        kernel,
        grid_spec=grid_spec,
        out_shape=jax.ShapeDtypeStruct((row_count, page_count), jnp.float32),
        compiler_params=pltpu.CompilerParams(dimension_semantics=("arbitrary",)),
    )(nb, queries, keys, limits.reshape(row_count, 1))


def per_device(queries, key_max, key_min, limits):
    local_pages = key_max.shape[0]
    kv_count = key_max.shape[1] // DH
    bounds = jnp.stack(
        (key_max.reshape(local_pages, kv_count, DH), key_min.reshape(local_pages, kv_count, DH)),
        axis=2,
    ).reshape(local_pages, kv_count * 2 * DH)
    keys = lax.all_gather(bounds, ("row", "rep"), axis=0, tiled=True)
    accumulated = page_mass_local(queries, keys, limits)
    return lax.psum_scatter(accumulated, "head", scatter_dimension=1, tiled=True)


def solution(mesh):
    placed = (
        P(("grp", "row", "rep"), "head"),
        P(("grp", "row", "rep"), "head"),
        P(("grp", "row", "rep"), "head"),
        P(("grp", "row", "rep")),
    )
    return jax.shard_map(
        per_device,
        mesh=mesh,
        in_specs=placed,
        out_specs=P(("grp", "row", "rep"), "head"),
        check_vma=False,
    )
```

time: 452 us -> 323 us (0.71)
  Pallas kernels: 0 us -> 178 us
  matrix products: 157 us -> 0 us
  loops' own time: 121 us -> 0 us
  local copies, waits for them, and re-layouts: 33.2 us -> 5.72 us
  other arithmetic: 24.4 us -> 2.24 us
  waiting for transfers between devices: 98.1 us -> 119 us
    pallas_call x0 -> x1, Pallas kernels: none -> 178 us  [page_mass_local(): pl.pallas_call(kernel, grid_spec=grid_spec, out_shape=jax.ShapeDtypeStruc...]
    dot_general x64 -> x0, matrix products: 157 us -> none  [the longest x32 82.2 us: head_scores(): jnp.dot(negative[head_index], sheets[kv_index, 1].T, precision=lax.Precis...]
    another operation x1 -> x0, loops' own time: 121 us -> none  [per_device(): lax.scan(head_step, start, jnp.arange(head_count, dtype=jnp.int32))]
    reduce_scatter x1, waiting for transfers between devices: 20.4 us -> 42.7 us  [per_device(): lax.psum_scatter(accumulated, 'head', scatter_dimension=1, tiled=True)]
    dynamic_slice x32 -> x0, local copies, waits for them, and re-layouts: 19.1 us -> none  [per_device(): lax.scan(head_step, start, jnp.arange(head_count, dtype=jnp.int32))]
    unnamed x8 -> x0, local copies, waits for them, and re-layouts: 14.1 us -> none
    add x32 -> x0, other arithmetic: 11.5 us -> none  [head_step(): return (accumulated + weights / row_total, None)]
    reduce_sum x32 -> x0, other arithmetic: 9.7 us -> none  [head_step(): row_total = jnp.sum(weights, axis=1, keepdims=True)]
where the time goes in v1:
time: 323 us; the launch traced here: 321 us
  Pallas kernels  178 us (55%)
  waiting for transfers between devices  119 us (37%)
  between operations  16 us (5%)
  local copies, waits for them, and re-layouts  5.72 us (2%)
    pallas_call x1, Pallas kernels, page_mass_local(): pl.pallas_call(kernel, grid_spec=grid_spec, out_shape=jax.ShapeDtypeStruc...  178 us
    all_gather x1, waiting for transfers between devices, per_device(): keys = lax.all_gather(bounds, ('row', 'rep'), axis=0, tiled=True)  76.5 us
    reduce_scatter x1, waiting for transfers between devices, per_device(): lax.psum_scatter(accumulated, 'head', scatter_dimension=1, tiled=True)  42.7 us
  transfers between devices with their start and end apart: 2, of which 2 were waited for; matrix products, arithmetic and copies ran while one was open for 1% of the time, Pallas kernels for 0%

profile of v1, /device:TPU:16, one launch (start us, length us, event | category | flops | bytes accessed | tf_op | source)
XLA Modules:
  0.0 321.4 jit_solution(3021150321041764528)
XLA Ops:
  6.5 0.0 all-gather.2.cloned.1.call-start
  6.5 1.2 stack_reshape.6
  7.8 1.2 stack_reshape.7
  9.0 0.9 pad_maximum_fusion
  9.9 1.9 reshape.10
  11.8 0.0 all-gather.2.cloned.1.call-update
  11.9 0.0 reduce-scatter.2.cloned.1.call-start
  11.9 1.3 reduce_max.9
  15.8 1.4 copy.7.lim_ref
  17.2 76.5 %all-gather.2.cloned.1.call-done.k_ref = f32[2048,1024]{1,0:T(8,128)} async-done(((f32[256,1024]{1,0:T(8,128)}), f32[2048,1024]{1,0:T(8,128)}) %all-gather.2.cloned.1.call-update) | async-done | bytes 8388624 | tf_op jit(solution)/shard_map/all_gather | solution.py:112
  93.7 178.1 %shard_map.46 = f32[128,2048]{1,0:T(8,128)} custom-call(s32[1]{0:T(128)} %bitcast.nb_ref, f32[128,4096]{1,0:T(8,128)} %q_ref.1, f32[2048,1024]{1,0:T(8,128)} %all-gather.2.cloned.1.call-done.k_ref, s32[128,1]{1,0:T(8,128)} %copy.7.lim_ref), custom_call_target="tpu_custom_call" | custom-call | tf_op jit(solution)/shard_map/pallas_call | solution.py:97
  271.8 0.0 reduce-scatter.2.cloned.1.call-update
  271.8 42.7 %reduce-scatter.2.cloned.1.call-done = f32[128,1024]{1,0:T(8,128)} async-done(((f32[128,2048]{1,0:T(8,128)}), f32[128,1024]{1,0:T(8,128)}) %reduce-scatter.2.cloned.1.call-update) | async-done | bytes 524304 | tf_op jit(solution)/shard_map/reduce_scatter | solution.py:114
Async XLA Ops:
  6.5 87.1 %all-gather.2.cloned.1.call-start = ((), (), s32[]{:S(2)}) async-start(), calls=%async_computation.1 | async-start | bytes 9437184 | tf_op jit(solution)/shard_map/all_gather | solution.py:112
  11.9 302.7 %reduce-scatter.2.cloned.1.call-start = ((), (), s32[]{:S(2)}) async-start(), calls=%async_computation.2 | async-start | bytes 1572864 | tf_op jit(solution)/shard_map/reduce_scatter | solution.py:114
Sparse Core Ops, SparseCore 0:
  12.0 81.6 all-gather.1
  272.0 42.5 reduce-scatter.1

commit v2 on v1

v2 whole, which is shorter than its diff:
```python
import functools
import math

import jax
import jax.numpy as jnp
from jax import lax
from jax.experimental import pallas as pl
from jax.experimental.pallas import tpu as pltpu
from jax.sharding import PartitionSpec as P

DH = 128
CHUNK = 256


def _split(x):
    hi = x.astype(jnp.bfloat16)
    lo = (x - hi.astype(jnp.float32)).astype(jnp.bfloat16)
    return hi, lo


def _mass_kernel(nb_ref, q_ref, k_ref, lim_ref, out_ref, khi_ref, klo_ref, s_ref, acc_ref,
                 *, group_size, chunk_count, score_scale):
    h = pl.program_id(0)
    nb = nb_ref[0]
    row_count = q_ref.shape[0]

    @pl.when(h == 0)
    def _():
        acc_ref[...] = jnp.zeros_like(acc_ref)

    @pl.when(h % group_size == 0)
    def _():
        for c in range(chunk_count):
            @pl.when(c < nb)
            def _():
                hi, lo = _split(k_ref[c * CHUNK:(c + 1) * CHUNK, :])
                khi_ref[c * CHUNK:(c + 1) * CHUNK, :] = hi
                klo_ref[c * CHUNK:(c + 1) * CHUNK, :] = lo

    q = q_ref[...]
    x = jnp.concatenate([jnp.maximum(q, 0.0), jnp.minimum(q, 0.0)], axis=1) * score_scale
    xhi, xlo = _split(x.T)
    lim = lim_ref[...]
    page_in_chunk = lax.broadcasted_iota(jnp.int32, (CHUNK, row_count), 0)

    def vreg_fold(v, op):
        return op(v.reshape(CHUNK // 8, 8, row_count), axis=0)

    top = jnp.full((8, row_count), -jnp.inf, jnp.float32)
    for c in range(chunk_count):
        def pass_scores(top, c=c):
            khi = khi_ref[c * CHUNK:(c + 1) * CHUNK, :]
            klo = klo_ref[c * CHUNK:(c + 1) * CHUNK, :]
            s = jnp.dot(khi, xhi, preferred_element_type=jnp.float32)
            s = s + jnp.dot(khi, xlo, preferred_element_type=jnp.float32)
            s = s + jnp.dot(klo, xhi, preferred_element_type=jnp.float32)
            s = jnp.where(page_in_chunk + c * CHUNK <= lim, s, -1e30)
            s_ref[c * CHUNK:(c + 1) * CHUNK, :] = s
            return jnp.maximum(top, vreg_fold(s, jnp.max))
        top = lax.cond(c < nb, pass_scores, lambda t: t, top)
    top = jnp.max(top, axis=0, keepdims=True)

    total = jnp.zeros((8, row_count), jnp.float32)
    for c in range(chunk_count):
        def pass_exp(total, c=c):
            e = jnp.exp(s_ref[c * CHUNK:(c + 1) * CHUNK, :] - top)
            s_ref[c * CHUNK:(c + 1) * CHUNK, :] = e
            return total + vreg_fold(e, jnp.sum)
        total = lax.cond(c < nb, pass_exp, lambda t: t, total)
    inv = 1.0 / jnp.sum(total, axis=0, keepdims=True)

    for c in range(chunk_count):
        @pl.when(c < nb)
        def _():
            acc_ref[c * CHUNK:(c + 1) * CHUNK, :] += s_ref[c * CHUNK:(c + 1) * CHUNK, :] * inv

    @pl.when(h == pl.num_programs(0) - 1)
    def _():
        for c in range(chunk_count):
            out_ref[:, c * CHUNK:(c + 1) * CHUNK] = acc_ref[c * CHUNK:(c + 1) * CHUNK, :].T


def page_mass_local(queries, keys, limits):
    row_count = queries.shape[0]
    head_count = queries.shape[1] // DH
    page_count = keys.shape[0]
    kv_count = keys.shape[1] // (2 * DH)
    group_size = head_count // kv_count
    chunk_count = page_count // CHUNK
    nb = (jnp.max(limits) // CHUNK + 1).astype(jnp.int32).reshape(1)
    kernel = functools.partial(
        _mass_kernel, group_size=group_size, chunk_count=chunk_count,
        score_scale=1.0 / math.sqrt(DH))
    grid_spec = pltpu.PrefetchScalarGridSpec(
        num_scalar_prefetch=1,
        grid=(head_count,),
        in_specs=[
            pl.BlockSpec((row_count, DH), lambda h, nb: (0, h)),
            pl.BlockSpec((page_count, 2 * DH), lambda h, nb: (0, h // group_size)),
            pl.BlockSpec((1, row_count), lambda h, nb: (0, 0)),
        ],
        out_specs=pl.BlockSpec((row_count, page_count), lambda h, nb: (0, 0)),
        scratch_shapes=[
            pltpu.VMEM((page_count, 2 * DH), jnp.bfloat16),
            pltpu.VMEM((page_count, 2 * DH), jnp.bfloat16),
            pltpu.VMEM((page_count, row_count), jnp.float32),
            pltpu.VMEM((page_count, row_count), jnp.float32),
        ],
    )
    return pl.pallas_call(
        kernel,
        grid_spec=grid_spec,
        out_shape=jax.ShapeDtypeStruct((row_count, page_count), jnp.float32),
        compiler_params=pltpu.CompilerParams(dimension_semantics=("arbitrary",)),
    )(nb, queries, keys, limits.reshape(1, row_count))


def per_device(queries, key_max, key_min, limits):
    local_pages = key_max.shape[0]
    kv_count = key_max.shape[1] // DH
    bounds = jnp.stack(
        (key_max.reshape(local_pages, kv_count, DH), key_min.reshape(local_pages, kv_count, DH)),
        axis=2,
    ).reshape(local_pages, kv_count * 2 * DH)
    keys = lax.all_gather(bounds, ("row", "rep"), axis=0, tiled=True)
    accumulated = page_mass_local(queries, keys, limits)
    return lax.psum_scatter(accumulated, "head", scatter_dimension=1, tiled=True)


def solution(mesh):
    placed = (
        P(("grp", "row", "rep"), "head"),
        P(("grp", "row", "rep"), "head"),
        P(("grp", "row", "rep"), "head"),
        P(("grp", "row", "rep")),
    )
    return jax.shard_map(
        per_device,
        mesh=mesh,
        in_specs=placed,
        out_specs=P(("grp", "row", "rep"), "head"),
        check_vma=False,
    )
```

time: 323 us -> 213 us (0.66)
  Pallas kernels: 178 us -> 59.4 us
  waiting for transfers between devices: 119 us -> 128 us
    pallas_call x1, Pallas kernels: 178 us -> 59.4 us  [page_mass_local(): pl.pallas_call(kernel, grid_spec=grid_spec, out_shape=jax.ShapeDtypeStruc...]
    reduce_scatter x1, waiting for transfers between devices: 42.7 us -> 49.8 us  [per_device(): lax.psum_scatter(accumulated, 'head', scatter_dimension=1, tiled=True)]
where the time goes in v2:
time: 213 us; the launch traced here: 210 us
  waiting for transfers between devices  128 us (60%)
  Pallas kernels  59.4 us (28%)
  between operations  16 us (8%)
  local copies, waits for them, and re-layouts  4.33 us (2%)
  other arithmetic  2.24 us (1%)
    all_gather x1, waiting for transfers between devices, per_device(): keys = lax.all_gather(bounds, ('row', 'rep'), axis=0, tiled=True)  77.9 us
    pallas_call x1, Pallas kernels, page_mass_local(): pl.pallas_call(kernel, grid_spec=grid_spec, out_shape=jax.ShapeDtypeStruc...  59.4 us
    reduce_scatter x1, waiting for transfers between devices, per_device(): lax.psum_scatter(accumulated, 'head', scatter_dimension=1, tiled=True)  49.8 us
  transfers between devices with their start and end apart: 2, of which 2 were waited for; matrix products, arithmetic and copies ran while one was open for 1% of the time, Pallas kernels for 0%

profile of v2, /device:TPU:16, one launch (start us, length us, event | category | flops | bytes accessed | tf_op | source)
XLA Modules:
  0.0 209.7 jit_solution(5702924094227432744)
XLA Ops:
  6.5 0.0 all-gather.2.cloned.1.call-start
  6.5 1.2 stack_reshape.6
  7.8 1.2 stack_reshape.7
  9.0 0.9 pad_maximum_fusion
  9.9 1.9 reshape.10
  11.8 0.0 all-gather.2.cloned.1.call-update
  11.9 0.0 reduce-scatter.2.cloned.1.call-start
  11.9 1.3 reduce_max.9
  15.8 77.9 %all-gather.2.cloned.1.call-done.k_ref = f32[2048,1024]{1,0:T(8,128)} async-done(((f32[256,1024]{1,0:T(8,128)}), f32[2048,1024]{1,0:T(8,128)}) %all-gather.2.cloned.1.call-update) | async-done | bytes 8388624 | tf_op jit(solution)/shard_map/all_gather | solution.py:125
  93.7 59.4 %shard_map.46 = f32[128,2048]{1,0:T(8,128)} custom-call(s32[1]{0:T(128)} %bitcast.nb_ref, f32[128,4096]{1,0:T(8,128)} %q_ref.1, f32[2048,1024]{1,0:T(8,128)} %all-gather.2.cloned.1.call-done.k_ref, s32[1,128]{1,0:T(1,128)} %bitcast.6), custom_call_target="tpu_custom_call" | custom-call | tf_op jit(solution)/shard_map/pallas_call | solution.py:110
  153.1 0.0 reduce-scatter.2.cloned.1.call-update
  153.1 49.8 %reduce-scatter.2.cloned.1.call-done = f32[128,1024]{1,0:T(8,128)} async-done(((f32[128,2048]{1,0:T(8,128)}), f32[128,1024]{1,0:T(8,128)}) %reduce-scatter.2.cloned.1.call-update) | async-done | bytes 524304 | tf_op jit(solution)/shard_map/reduce_scatter | solution.py:127
Async XLA Ops:
  6.5 87.1 %all-gather.2.cloned.1.call-start = ((), (), s32[]{:S(2)}) async-start(), calls=%async_computation.1 | async-start | bytes 9437184 | tf_op jit(solution)/shard_map/all_gather | solution.py:125
  11.9 191.1 %reduce-scatter.2.cloned.1.call-start = ((), (), s32[]{:S(2)}) async-start(), calls=%async_computation.2 | async-start | bytes 1572864 | tf_op jit(solution)/shard_map/reduce_scatter | solution.py:127
Sparse Core Ops, SparseCore 0:
  12.0 81.6 all-gather.1
  153.3 49.5 reduce-scatter.1

commit v3 on v2

v3 whole, which is shorter than its diff:
```python
import functools
import math

import jax
import jax.numpy as jnp
from jax import lax
from jax.experimental import pallas as pl
from jax.experimental.pallas import tpu as pltpu
from jax.sharding import PartitionSpec as P

DH = 128
CHUNK = 256


def _split(x):
    hi = x.astype(jnp.bfloat16)
    lo = (x - hi.astype(jnp.float32)).astype(jnp.bfloat16)
    return hi, lo


def _mass_kernel(nb_ref, q_ref, k_ref, lim_ref, out_ref, kcat_ref, s_ref, acc_ref,
                 *, pairs_per_group, chunk_count, score_scale):
    hp = pl.program_id(0)
    nb = nb_ref[0]
    row_count = q_ref.shape[0] // 1
    lanes = 2 * row_count

    @pl.when(hp == 0)
    def _():
        acc_ref[...] = jnp.zeros_like(acc_ref)

    @pl.when(hp % pairs_per_group == 0)
    def _():
        for c in range(chunk_count):
            @pl.when(c < nb)
            def _():
                hi, lo = _split(k_ref[c * CHUNK:(c + 1) * CHUNK, :])
                kcat_ref[c * CHUNK:(c + 1) * CHUNK, :] = jnp.concatenate([hi, hi, lo], axis=1)

    q = q_ref[...]
    xs = []
    for j in range(2):
        qj = q[:, j * DH:(j + 1) * DH]
        xs.append(jnp.concatenate([jnp.maximum(qj, 0.0), jnp.minimum(qj, 0.0)], axis=1).T)
    w = jnp.concatenate(xs, axis=1) * score_scale
    whi, wlo = _split(w)
    wcat = jnp.concatenate([whi, wlo, whi], axis=0)
    lim = lim_ref[...]
    lim2 = jnp.concatenate([lim, lim], axis=1)
    page_in_chunk = lax.broadcasted_iota(jnp.int32, (CHUNK, lanes), 0)

    def vreg_fold(v, op):
        return op(v.reshape(CHUNK // 8, 8, lanes), axis=0)

    top = jnp.full((8, lanes), -jnp.inf, jnp.float32)
    for c in range(chunk_count):
        def pass_scores(top, c=c):
            s = jnp.dot(kcat_ref[c * CHUNK:(c + 1) * CHUNK, :], wcat,
                        preferred_element_type=jnp.float32)
            s = jnp.where(page_in_chunk + c * CHUNK <= lim2, s, -1e30)
            s_ref[c * CHUNK:(c + 1) * CHUNK, :] = s
            return jnp.maximum(top, vreg_fold(s, jnp.max))
        top = lax.cond(c < nb, pass_scores, lambda t: t, top)
    top = jnp.max(top, axis=0, keepdims=True)

    total = jnp.zeros((8, lanes), jnp.float32)
    for c in range(chunk_count):
        def pass_exp(total, c=c):
            e = jnp.exp(s_ref[c * CHUNK:(c + 1) * CHUNK, :] - top)
            s_ref[c * CHUNK:(c + 1) * CHUNK, :] = e
            return total + vreg_fold(e, jnp.sum)
        total = lax.cond(c < nb, pass_exp, lambda t: t, total)
    inv = 1.0 / jnp.sum(total, axis=0, keepdims=True)
    inv_a = inv[:, :row_count]
    inv_b = inv[:, row_count:]

    for c in range(chunk_count):
        @pl.when(c < nb)
        def _():
            e = s_ref[c * CHUNK:(c + 1) * CHUNK, :]
            acc_ref[c * CHUNK:(c + 1) * CHUNK, :] += (
                e[:, :row_count] * inv_a + e[:, row_count:] * inv_b)

    @pl.when(hp == pl.num_programs(0) - 1)
    def _():
        for c in range(chunk_count):
            out_ref[:, c * CHUNK:(c + 1) * CHUNK] = acc_ref[c * CHUNK:(c + 1) * CHUNK, :].T


def page_mass_local(queries, keys, limits):
    row_count = queries.shape[0]
    head_count = queries.shape[1] // DH
    page_count = keys.shape[0]
    kv_count = keys.shape[1] // (2 * DH)
    pairs_per_group = head_count // kv_count // 2
    chunk_count = page_count // CHUNK
    nb = (jnp.max(limits) // CHUNK + 1).astype(jnp.int32).reshape(1)
    kernel = functools.partial(
        _mass_kernel, pairs_per_group=pairs_per_group, chunk_count=chunk_count,
        score_scale=1.0 / math.sqrt(DH))
    grid_spec = pltpu.PrefetchScalarGridSpec(
        num_scalar_prefetch=1,
        grid=(head_count // 2,),
        in_specs=[
            pl.BlockSpec((row_count, 2 * DH), lambda hp, nb: (0, hp)),
            pl.BlockSpec((page_count, 2 * DH), lambda hp, nb: (0, hp // pairs_per_group)),
            pl.BlockSpec((1, row_count), lambda hp, nb: (0, 0)),
        ],
        out_specs=pl.BlockSpec((row_count, page_count), lambda hp, nb: (0, 0)),
        scratch_shapes=[
            pltpu.VMEM((page_count, 6 * DH), jnp.bfloat16),
            pltpu.VMEM((page_count, 2 * row_count), jnp.float32),
            pltpu.VMEM((page_count, row_count), jnp.float32),
        ],
    )
    return pl.pallas_call(
        kernel,
        grid_spec=grid_spec,
        out_shape=jax.ShapeDtypeStruct((row_count, page_count), jnp.float32),
        compiler_params=pltpu.CompilerParams(dimension_semantics=("arbitrary",)),
    )(nb, queries, keys, limits.reshape(1, row_count))


def per_device(queries, key_max, key_min, limits):
    local_pages = key_max.shape[0]
    kv_count = key_max.shape[1] // DH
    bounds = jnp.stack(
        (key_max.reshape(local_pages, kv_count, DH), key_min.reshape(local_pages, kv_count, DH)),
        axis=2,
    ).reshape(local_pages, kv_count * 2 * DH)
    keys = lax.all_gather(bounds, ("row", "rep"), axis=0, tiled=True)
    accumulated = page_mass_local(queries, keys, limits)
    return lax.psum_scatter(accumulated, "head", scatter_dimension=1, tiled=True)


def solution(mesh):
    placed = (
        P(("grp", "row", "rep"), "head"),
        P(("grp", "row", "rep"), "head"),
        P(("grp", "row", "rep"), "head"),
        P(("grp", "row", "rep")),
    )
    return jax.shard_map(
        per_device,
        mesh=mesh,
        in_specs=placed,
        out_specs=P(("grp", "row", "rep"), "head"),
        check_vma=False,
    )
```

time: 213 us -> 174 us (0.82)
  Pallas kernels: 59.4 us -> 34.8 us
  waiting for transfers between devices: 128 us -> 114 us
    pallas_call x1, Pallas kernels: 59.4 us -> 34.8 us  [page_mass_local(): pl.pallas_call(kernel, grid_spec=grid_spec, out_shape=jax.ShapeDtypeStruc...]
    reduce_scatter x1, waiting for transfers between devices: 49.8 us -> 36.4 us  [per_device(): lax.psum_scatter(accumulated, 'head', scatter_dimension=1, tiled=True)]
where the time goes in v3:
time: 174 us; the launch traced here: 172 us
  waiting for transfers between devices  114 us (66%)
  Pallas kernels  34.8 us (20%)
  between operations  16 us (9%)
  local copies, waits for them, and re-layouts  4.33 us (2%)
  other arithmetic  2.24 us (1%)
    all_gather x1, waiting for transfers between devices, per_device(): keys = lax.all_gather(bounds, ('row', 'rep'), axis=0, tiled=True)  77.9 us
    reduce_scatter x1, waiting for transfers between devices, per_device(): lax.psum_scatter(accumulated, 'head', scatter_dimension=1, tiled=True)  36.4 us
    pallas_call x1, Pallas kernels, page_mass_local(): pl.pallas_call(kernel, grid_spec=grid_spec, out_shape=jax.ShapeDtypeStruc...  34.8 us
  transfers between devices with their start and end apart: 2, of which 2 were waited for; matrix products, arithmetic and copies ran while one was open for 1% of the time, Pallas kernels for 0%

profile of v3, /device:TPU:16, one launch (start us, length us, event | category | flops | bytes accessed | tf_op | source)
XLA Modules:
  0.0 171.7 jit_solution(16615410703109527002)
XLA Ops:
  6.5 0.0 all-gather.2.cloned.1.call-start
  6.5 1.2 stack_reshape.6
  7.8 1.2 stack_reshape.7
  9.0 0.9 pad_maximum_fusion
  9.9 1.9 %reshape.10 = f32[256,1024]{1,0:T(8,128)} reshape(f32[256,4,2,128]{3,2,1,0:T(2,128)S(1)} %pad_maximum_fusion) | data formatting | bytes 2097152 | tf_op jit(solution)/shard_map/reshape | solution.py:130
  11.8 0.0 all-gather.2.cloned.1.call-update
  11.9 0.0 reduce-scatter.2.cloned.1.call-start
  11.9 1.3 reduce_max.9
  15.8 77.9 %all-gather.2.cloned.1.call-done.k_ref = f32[2048,1024]{1,0:T(8,128)} async-done(((f32[256,1024]{1,0:T(8,128)}), f32[2048,1024]{1,0:T(8,128)}) %all-gather.2.cloned.1.call-update) | async-done | bytes 8388624 | tf_op jit(solution)/shard_map/all_gather | solution.py:131
  93.7 34.8 %shard_map.46 = f32[128,2048]{1,0:T(8,128)} custom-call(s32[1]{0:T(128)} %bitcast.nb_ref, f32[128,4096]{1,0:T(8,128)} %q_ref.1, f32[2048,1024]{1,0:T(8,128)} %all-gather.2.cloned.1.call-done.k_ref, s32[1,128]{1,0:T(1,128)} %bitcast.6), custom_call_target="tpu_custom_call" | custom-call | tf_op jit(solution)/shard_map/pallas_call | solution.py:116
  128.5 0.0 reduce-scatter.2.cloned.1.call-update
  128.5 36.4 %reduce-scatter.2.cloned.1.call-done = f32[128,1024]{1,0:T(8,128)} async-done(((f32[128,2048]{1,0:T(8,128)}), f32[128,1024]{1,0:T(8,128)}) %reduce-scatter.2.cloned.1.call-update) | async-done | bytes 524304 | tf_op jit(solution)/shard_map/reduce_scatter | solution.py:133
Async XLA Ops:
  6.5 87.1 %all-gather.2.cloned.1.call-start = ((), (), s32[]{:S(2)}) async-start(), calls=%async_computation.1 | async-start | bytes 9437184 | tf_op jit(solution)/shard_map/all_gather | solution.py:131
  11.9 153.0 %reduce-scatter.2.cloned.1.call-start = ((), (), s32[]{:S(2)}) async-start(), calls=%async_computation.2 | async-start | bytes 1572864 | tf_op jit(solution)/shard_map/reduce_scatter | solution.py:133
Sparse Core Ops, SparseCore 0:
  12.0 81.6 all-gather.1
  128.6 36.2 reduce-scatter.1

commit v4 on v3

--- a/solution.py
+++ b/solution.py
@@ -18,19 +18,22 @@
     return hi, lo
 
 
-def _mass_kernel(nb_ref, q_ref, k_ref, lim_ref, out_ref, kcat_ref, s_ref, acc_ref,
-                 *, pairs_per_group, chunk_count, score_scale):
+def _mass_kernel(nb_ref, q_ref, k_ref, lim_ref, *refs, chunk_count, score_scale, first, last):
+    if first:
+        out_ref, kcat_ref, s_ref, acc_ref = refs
+    else:
+        acc_in_ref, out_ref, kcat_ref, s_ref, acc_ref = refs
     hp = pl.program_id(0)
     nb = nb_ref[0]
-    row_count = q_ref.shape[0] // 1
+    row_count = q_ref.shape[0]
     lanes = 2 * row_count
 
     @pl.when(hp == 0)
     def _():
-        acc_ref[...] = jnp.zeros_like(acc_ref)
-
-    @pl.when(hp % pairs_per_group == 0)
-    def _():
+        if first:
+            acc_ref[...] = jnp.zeros_like(acc_ref)
+        else:
+            acc_ref[...] = acc_in_ref[...]
         for c in range(chunk_count):
             @pl.when(c < nb)
             def _():
@@ -84,29 +87,40 @@
     @pl.when(hp == pl.num_programs(0) - 1)
     def _():
         for c in range(chunk_count):
-            out_ref[:, c * CHUNK:(c + 1) * CHUNK] = acc_ref[c * CHUNK:(c + 1) * CHUNK, :].T
+            if last:
+                out_ref[:, c * CHUNK:(c + 1) * CHUNK] = acc_ref[c * CHUNK:(c + 1) * CHUNK, :].T
+            else:
+                out_ref[c * CHUNK:(c + 1) * CHUNK, :] = acc_ref[c * CHUNK:(c + 1) * CHUNK, :]
 
 
-def page_mass_local(queries, keys, limits):
+def page_mass_group(nb, queries, keys, limits, acc, last):
     row_count = queries.shape[0]
-    head_count = queries.shape[1] // DH
+    pair_count = queries.shape[1] // (2 * DH)
     page_count = keys.shape[0]
-    kv_count = keys.shape[1] // (2 * DH)
-    pairs_per_group = head_count // kv_count // 2
     chunk_count = page_count // CHUNK
-    nb = (jnp.max(limits) // CHUNK + 1).astype(jnp.int32).reshape(1)
+    first = acc is None
     kernel = functools.partial(
-        _mass_kernel, pairs_per_group=pairs_per_group, chunk_count=chunk_count,
-        score_scale=1.0 / math.sqrt(DH))
+        _mass_kernel, chunk_count=chunk_count, score_scale=1.0 / math.sqrt(DH),
+        first=first, last=last)
+    in_specs = [
+        pl.BlockSpec((row_count, 2 * DH), lambda hp, nb: (0, hp)),
+        pl.BlockSpec((page_count, 2 * DH), lambda hp, nb: (0, 0)),
+        pl.BlockSpec((1, row_count), lambda hp, nb: (0, 0)),
+    ]
+    operands = [nb, queries, keys, limits.reshape(1, row_count)]
+    if not first:
+        in_specs.append(pl.BlockSpec((page_count, row_count), lambda hp, nb: (0, 0)))
+        operands.append(acc)
+    if last:
+        out_shape = (row_count, page_count)
+    else:
+        out_shape = (page_count, row_count)
+    aliases = {4: 0} if (not first and not last) else {}
     grid_spec = pltpu.PrefetchScalarGridSpec(
         num_scalar_prefetch=1,
-        grid=(head_count // 2,),
-        in_specs=[
-            pl.BlockSpec((row_count, 2 * DH), lambda hp, nb: (0, hp)),
-            pl.BlockSpec((page_count, 2 * DH), lambda hp, nb: (0, hp // pairs_per_group)),
-            pl.BlockSpec((1, row_count), lambda hp, nb: (0, 0)),
-        ],
-        out_specs=pl.BlockSpec((row_count, page_count), lambda hp, nb: (0, 0)),
+        grid=(pair_count,),
+        in_specs=in_specs,
+        out_specs=pl.BlockSpec(out_shape, lambda hp, nb: (0, 0)),
         scratch_shapes=[
             pltpu.VMEM((page_count, 6 * DH), jnp.bfloat16),
             pltpu.VMEM((page_count, 2 * row_count), jnp.float32),
@@ -116,21 +130,26 @@
     return pl.pallas_call(
         kernel,
         grid_spec=grid_spec,
-        out_shape=jax.ShapeDtypeStruct((row_count, page_count), jnp.float32),
+        out_shape=jax.ShapeDtypeStruct(out_shape, jnp.float32),
+        input_output_aliases=aliases,
         compiler_params=pltpu.CompilerParams(dimension_semantics=("arbitrary",)),
-    )(nb, queries, keys, limits.reshape(1, row_count))
+    )(*operands)
 
 
 def per_device(queries, key_max, key_min, limits):
     local_pages = key_max.shape[0]
     kv_count = key_max.shape[1] // DH
-    bounds = jnp.stack(
-        (key_max.reshape(local_pages, kv_count, DH), key_min.reshape(local_pages, kv_count, DH)),
-        axis=2,
-    ).reshape(local_pages, kv_count * 2 * DH)
-    keys = lax.all_gather(bounds, ("row", "rep"), axis=0, tiled=True)
-    accumulated = page_mass_local(queries, keys, limits)
-    return lax.psum_scatter(accumulated, "head", scatter_dimension=1, tiled=True)
+    group_cols = queries.shape[1] // kv_count
+    nb = (jnp.max(limits) // CHUNK + 1).astype(jnp.int32).reshape(1)
+    acc = None
+    for kv in range(kv_count):
+        bounds = jnp.concatenate(
+            (key_max[:, kv * DH:(kv + 1) * DH], key_min[:, kv * DH:(kv + 1) * DH]), axis=1)
+        keys = lax.all_gather(bounds, ("row", "rep"), axis=0, tiled=True)
+        acc = page_mass_group(
+            nb, queries[:, kv * group_cols:(kv + 1) * group_cols], keys, limits, acc,
+            last=kv == kv_count - 1)
+    return lax.psum_scatter(acc, "head", scatter_dimension=1, tiled=True)
 
 
 def solution(mesh):

time: 174 us -> 173 us (level)
  waiting for transfers between devices: 114 us -> 105 us
  Pallas kernels: 34.8 us -> 43.7 us
    reduce_scatter x1, waiting for transfers between devices: 36.4 us -> 24.3 us  [per_device(): return lax.psum_scatter(acc, 'head', scatter_dimension=1, tiled=True)]
    pallas_call x1 -> x4, Pallas kernels: 34.8 us -> 43.7 us  [page_mass_group(): pl.pallas_call(kernel, grid_spec=grid_spec, out_shape=jax.ShapeDtypeStruc...]
    all_gather x1 -> x4, waiting for transfers between devices: 77.9 us -> 80.9 us  [per_device(): keys = lax.all_gather(bounds, ('row', 'rep'), axis=0, tiled=True)]
    concatenate x0 -> x4, other arithmetic: none -> 2.89 us  [per_device(): jnp.concatenate((key_max[:, kv * DH:(kv + 1) * DH], key_min[:, kv * DH:(k...]
    slice x0 -> x2, local copies, waits for them, and re-layouts: none -> 2.73 us  [the longest x1 1.37 us: per_device(): key_max[:, kv * DH:(kv + 1) * DH]]
    another operation x2 -> x0, local copies, waits for them, and re-layouts: 2.42 us -> none  [per_device(): jnp.stack((key_max.reshape(local_pages, kv_count, DH), key_min.reshape(lo...]
    reshape x1 -> x0, local copies, waits for them, and re-layouts: 1.91 us -> none  [per_device(): bounds = jnp.stack((key_max.reshape(local_pages, kv_count, DH), key_min.r...]
  transfers between devices with their start and end apart: 2 -> 5, of which waited for: 2 -> 5; matrix products, arithmetic and copies ran while one was open for 1% -> 2% of each run, Pallas kernels for 0% -> 19%
where the time goes in v4:
time: 173 us; the launch traced here: 171 us
  waiting for transfers between devices  105 us (61%)
  Pallas kernels  43.7 us (25%)
  between operations  15.8 us (9%)
  other arithmetic  3.53 us (2%)
  local copies, waits for them, and re-layouts  2.74 us (2%)
    all_gather x4, waiting for transfers between devices, per_device(): keys = lax.all_gather(bounds, ('row', 'rep'), axis=0, tiled=True)  80.9 us
    pallas_call x4, Pallas kernels, page_mass_group(): pl.pallas_call(kernel, grid_spec=grid_spec, out_shape=jax.ShapeDtypeStruc...  43.7 us
    reduce_scatter x1, waiting for transfers between devices, per_device(): return lax.psum_scatter(acc, 'head', scatter_dimension=1, tiled=True)  24.3 us
  transfers between devices with their start and end apart: 5, of which 5 were waited for; matrix products, arithmetic and copies ran while one was open for 2% of the time, Pallas kernels for 19%

profile of v4, /device:TPU:16, one launch (start us, length us, event | category | flops | bytes accessed | tf_op | source)
XLA Modules:
  0.0 171.2 jit_solution(10880353878757170319)
XLA Ops:
  6.5 1.4 fusion.1
  7.9 0.7 pad_maximum_fusion.3
  8.7 0.0 all-gather.11.cloned.1.call-update
  8.7 0.0 all-gather.9.cloned.1.call-start
  8.8 0.7 pad_maximum_fusion.2
  9.5 0.0 all-gather.9.cloned.1.call-update
  9.5 0.0 all-gather.7.cloned.1.call-start
  9.5 0.7 pad_maximum_fusion.1
  10.3 0.0 all-gather.7.cloned.1.call-update
  10.3 0.0 all-gather.5.cloned.1.call-start
  10.3 0.7 pad_maximum_fusion
  11.1 0.0 reduce-scatter.2.cloned.1.call-start
  11.1 0.6 reduce_max.9
  14.4 1.4 fusion
  15.7 22.9 %all-gather.11.cloned.1.call-done.k_ref = f32[2048,256]{1,0:T(8,128)} async-done(((f32[256,256]{1,0:T(8,128)}), f32[2048,256]{1,0:T(8,128)}) %all-gather.11.cloned.1.call-update) | async-done | bytes 2097168 | tf_op jit(solution)/shard_map/all_gather | solution.py:148
  38.7 10.7 %shard_map.46.refs_0_ = f32[2048,128]{1,0:T(8,128)} custom-call(s32[1]{0:T(128)} %bitcast.nb_ref, f32[128,1024]{1,0:T(8,128)} %get-tuple-element.5.q_ref, f32[2048,256]{1,0:T(8,128)} %all-gather.11.cloned.1.call-done.k_ref, s32[1,128]{1,0:T(1,128)} %bitcast.2), custom_call_target="tpu_custom_call" | custom-call | tf_op jit(solution)/shard_map/pallas_call | solution.py:130
  49.3 19.6 %all-gather.9.cloned.1.call-done.k_ref = f32[2048,256]{1,0:T(8,128)} async-done(((f32[256,256]{1,0:T(8,128)}), f32[2048,256]{1,0:T(8,128)}) %all-gather.9.cloned.1.call-update) | async-done | bytes 2097168 | tf_op jit(solution)/shard_map/all_gather | solution.py:148
  68.9 11.0 %shard_map.47.refs_0_ = f32[2048,128]{1,0:T(8,128)} custom-call(s32[1]{0:T(128)} %bitcast.nb_ref, f32[128,1024]{1,0:T(8,128)} %get-tuple-element.8.q_ref, f32[2048,256]{1,0:T(8,128)} %all-gather.9.cloned.1.call-done.k_ref, s32[1,128]{1,0:T(1,128)} %bitcast.3, f32[2048,128]{1,0:T(8,128)} %shard_map.46.refs_0_), custom_call_target="tpu_custom_call", output_to_operand_aliasing={{}: (4, {})} | custom-call | tf_op jit(solution)/shard_map/pallas_call | solution.py:130
  79.8 19.3 %all-gather.7.cloned.1.call-done.k_ref = f32[2048,256]{1,0:T(8,128)} async-done(((f32[256,256]{1,0:T(8,128)}), f32[2048,256]{1,0:T(8,128)}) %all-gather.7.cloned.1.call-update) | async-done | bytes 2097168 | tf_op jit(solution)/shard_map/all_gather | solution.py:148
  99.1 11.0 %shard_map.48.refs_0_ = f32[2048,128]{1,0:T(8,128)} custom-call(s32[1]{0:T(128)} %bitcast.nb_ref, f32[128,1024]{1,0:T(8,128)} %get-tuple-element.6.q_ref, f32[2048,256]{1,0:T(8,128)} %all-gather.7.cloned.1.call-done.k_ref, s32[1,128]{1,0:T(1,128)} %bitcast.4, f32[2048,128]{1,0:T(8,128)} %shard_map.47.refs_0_), custom_call_target="tpu_custom_call", output_to_operand_aliasing={{}: (4, {})} | custom-call | tf_op jit(solution)/shard_map/pallas_call | solution.py:130
  110.1 19.1 %all-gather.5.cloned.1.call-done.k_ref = f32[2048,256]{1,0:T(8,128)} async-done(((f32[256,256]{1,0:T(8,128)}), f32[2048,256]{1,0:T(8,128)}) %all-gather.5.cloned.1.call-update) | async-done | bytes 2097168 | tf_op jit(solution)/shard_map/all_gather | solution.py:148
  129.2 11.1 %shard_map.49 = f32[128,2048]{1,0:T(8,128)} custom-call(s32[1]{0:T(128)} %bitcast.nb_ref, f32[128,1024]{1,0:T(8,128)} %get-tuple-element.7.q_ref, f32[2048,256]{1,0:T(8,128)} %all-gather.5.cloned.1.call-done.k_ref, s32[1,128]{1,0:T(1,128)} %bitcast.5, f32[2048,128]{1,0:T(8,128)} %shard_map.48.refs_0_), custom_call_target="tpu_custom_call" | custom-call | tf_op jit(solution)/shard_map/pallas_call | solution.py:130
  140.3 0.0 reduce-scatter.2.cloned.1.call-update
  140.4 24.3 %reduce-scatter.2.cloned.1.call-done = f32[128,1024]{1,0:T(8,128)} async-done(((f32[128,2048]{1,0:T(8,128)}), f32[128,1024]{1,0:T(8,128)}) %reduce-scatter.2.cloned.1.call-update) | async-done | bytes 524304 | tf_op jit(solution)/shard_map/reduce_scatter | solution.py:152
  (6 shorter events, 0.0 us)
Async XLA Ops:
  6.5 32.1 %all-gather.11.cloned.1.call-start = ((), (), s32[]{:S(2)}) async-start(), calls=%async_computation.4 | async-start | bytes 2359296 | tf_op jit(solution)/shard_map/all_gather | solution.py:148
  7.9 3.2 %copy-start.1 = (s32[128]{0:T(128)S(1)}, s32[128]{0:T(128)}, u32[]{:S(2)}) copy-start(s32[128]{0:T(128)} %param.7) | copy-start | bytes 1540
  7.9 6.5 %copy-start = (f32[128,4096]{1,0:T(8,128)S(1)}, f32[128,4096]{1,0:T(8,128)}, u32[]{:S(2)}) copy-start(f32[128,4096]{1,0:T(8,128)} %param.4) | copy-start | bytes 6291460
  8.7 60.2 %all-gather.9.cloned.1.call-start = ((), (), s32[]{:S(2)}) async-start(), calls=%async_computation.3 | async-start | bytes 2359296 | tf_op jit(solution)/shard_map/all_gather | solution.py:148
  9.5 89.6 %all-gather.7.cloned.1.call-start = ((), (), s32[]{:S(2)}) async-start(), calls=%async_computation.2 | async-start | bytes 2359296 | tf_op jit(solution)/shard_map/all_gather | solution.py:148
  10.3 118.9 %all-gather.5.cloned.1.call-start = ((), (), s32[]{:S(2)}) async-start(), calls=%async_computation.1 | async-start | bytes 2359296 | tf_op jit(solution)/shard_map/all_gather | solution.py:148
  11.1 153.6 %reduce-scatter.2.cloned.1.call-start = ((), (), s32[]{:S(2)}) async-start(), calls=%async_computation.5 | async-start | bytes 1572864 | tf_op jit(solution)/shard_map/reduce_scatter | solution.py:152
Sparse Core Ops, SparseCore 0:
  9.0 29.6 all-gather.10
  40.3 28.5 all-gather.8
  70.5 28.5 all-gather.6
  100.6 28.5 all-gather.4
  140.5 24.1 reduce-scatter.1

commit v5 on v4

--- a/solution.py
+++ b/solution.py
@@ -10,6 +10,7 @@
 
 DH = 128
 CHUNK = 256
+GATHERS = 2
 
 
 def _split(x):
@@ -18,7 +19,8 @@
     return hi, lo
 
 
-def _mass_kernel(nb_ref, q_ref, k_ref, lim_ref, *refs, chunk_count, score_scale, first, last):
+def _mass_kernel(nb_ref, q_ref, k_ref, lim_ref, *refs, chunk_count, score_scale, first, last,
+                 pairs_per_kv):
     if first:
         out_ref, kcat_ref, s_ref, acc_ref = refs
     else:
@@ -34,6 +36,9 @@
             acc_ref[...] = jnp.zeros_like(acc_ref)
         else:
             acc_ref[...] = acc_in_ref[...]
+
+    @pl.when(hp % pairs_per_kv == 0)
+    def _():
         for c in range(chunk_count):
             @pl.when(c < nb)
             def _():
@@ -96,15 +101,16 @@
 def page_mass_group(nb, queries, keys, limits, acc, last):
     row_count = queries.shape[0]
     pair_count = queries.shape[1] // (2 * DH)
+    pairs_per_kv = pair_count // (keys.shape[1] // (2 * DH))
     page_count = keys.shape[0]
     chunk_count = page_count // CHUNK
     first = acc is None
     kernel = functools.partial(
         _mass_kernel, chunk_count=chunk_count, score_scale=1.0 / math.sqrt(DH),
-        first=first, last=last)
+        first=first, last=last, pairs_per_kv=pairs_per_kv)
     in_specs = [
         pl.BlockSpec((row_count, 2 * DH), lambda hp, nb: (0, hp)),
-        pl.BlockSpec((page_count, 2 * DH), lambda hp, nb: (0, 0)),
+        pl.BlockSpec((page_count, 2 * DH), lambda hp, nb: (0, hp // pairs_per_kv)),
         pl.BlockSpec((1, row_count), lambda hp, nb: (0, 0)),
     ]
     operands = [nb, queries, keys, limits.reshape(1, row_count)]
@@ -139,16 +145,19 @@
 def per_device(queries, key_max, key_min, limits):
     local_pages = key_max.shape[0]
     kv_count = key_max.shape[1] // DH
-    group_cols = queries.shape[1] // kv_count
+    call_count = min(kv_count, GATHERS)
+    kv_per_call = kv_count // call_count
+    group_cols = queries.shape[1] // call_count
     nb = (jnp.max(limits) // CHUNK + 1).astype(jnp.int32).reshape(1)
     acc = None
-    for kv in range(kv_count):
-        bounds = jnp.concatenate(
-            (key_max[:, kv * DH:(kv + 1) * DH], key_min[:, kv * DH:(kv + 1) * DH]), axis=1)
-        keys = lax.all_gather(bounds, ("row", "rep"), axis=0, tiled=True)
+    for g in range(call_count):
+        parts = []
+        for kv in range(g * kv_per_call, (g + 1) * kv_per_call):
+            parts += [key_max[:, kv * DH:(kv + 1) * DH], key_min[:, kv * DH:(kv + 1) * DH]]
+        keys = lax.all_gather(jnp.concatenate(parts, axis=1), ("row", "rep"), axis=0, tiled=True)
         acc = page_mass_group(
-            nb, queries[:, kv * group_cols:(kv + 1) * group_cols], keys, limits, acc,
-            last=kv == kv_count - 1)
+            nb, queries[:, g * group_cols:(g + 1) * group_cols], keys, limits, acc,
+            last=g == call_count - 1)
     return lax.psum_scatter(acc, "head", scatter_dimension=1, tiled=True)
 
 

time: 173 us -> 160 us (0.925)
  waiting for transfers between devices: 105 us -> 98.6 us
  Pallas kernels: 43.7 us -> 37.7 us
    all_gather x4 -> x2, waiting for transfers between devices: 80.9 us -> 70 us  [per_device(): lax.all_gather(jnp.concatenate(parts, axis=1), ('row', 'rep'), axis=0, ti...]
    pallas_call x4 -> x2, Pallas kernels: 43.7 us -> 37.7 us  [page_mass_group(): pl.pallas_call(kernel, grid_spec=grid_spec, out_shape=jax.ShapeDtypeStruc...]
    reduce_scatter x1, waiting for transfers between devices: 24.3 us -> 28.5 us  [per_device(): return lax.psum_scatter(acc, 'head', scatter_dimension=1, tiled=True)]
  transfers between devices with their start and end apart: 5 -> 3, of which waited for: 5 -> 3; matrix products, arithmetic and copies ran while one was open for 2% -> 2% of each run, Pallas kernels for 19% -> 12%
where the time goes in v5:
time: 160 us; the launch traced here: 158 us
  waiting for transfers between devices  98.6 us (62%)
  Pallas kernels  37.7 us (24%)
  between operations  15.8 us (10%)
  local copies, waits for them, and re-layouts  3.04 us (2%)
  other arithmetic  2.35 us (1%)
    all_gather x2, waiting for transfers between devices, per_device(): lax.all_gather(jnp.concatenate(parts, axis=1), ('row', 'rep'), axis=0, ti...  70 us
    pallas_call x2, Pallas kernels, page_mass_group(): pl.pallas_call(kernel, grid_spec=grid_spec, out_shape=jax.ShapeDtypeStruc...  37.7 us
    reduce_scatter x1, waiting for transfers between devices, per_device(): return lax.psum_scatter(acc, 'head', scatter_dimension=1, tiled=True)  28.5 us
  transfers between devices with their start and end apart: 3, of which 3 were waited for; matrix products, arithmetic and copies ran while one was open for 2% of the time, Pallas kernels for 12%

profile of v5, /device:TPU:16, one launch (start us, length us, event | category | flops | bytes accessed | tf_op | source)
XLA Modules:
  0.0 157.6 jit_solution(1278829946218032652)
XLA Ops:
  6.5 0.0 copy-start.1
  6.5 0.0 copy-start
  6.5 0.0 all-gather.5.cloned.1.call-start
  6.5 1.5 fusion.1
  8.1 0.8 pad_maximum_fusion.1
  8.9 0.0 all-gather.5.cloned.1.call-update
  8.9 0.0 all-gather.3.cloned.1.call-start
  9.0 0.8 pad_maximum_fusion
  9.8 0.0 all-gather.3.cloned.1.call-update
  9.8 0.0 reduce-scatter.2.cloned.1.call-start
  9.9 0.0 copy-done.1
  9.9 0.7 reduce_max.9
  13.3 0.0 copy-done
  13.3 1.5 fusion
  14.8 41.1 %all-gather.5.cloned.1.call-done.k_ref = f32[2048,512]{1,0:T(8,128)} async-done(((f32[256,512]{1,0:T(8,128)}), f32[2048,512]{1,0:T(8,128)}) %all-gather.5.cloned.1.call-update) | async-done | bytes 4194320 | tf_op jit(solution)/shard_map/all_gather | solution.py:157
  55.9 18.6 %shard_map.46.refs_0_ = f32[2048,128]{1,0:T(8,128)} custom-call(s32[1]{0:T(128)} %bitcast.nb_ref, f32[128,2048]{1,0:T(8,128)} %get-tuple-element.5.q_ref, f32[2048,512]{1,0:T(8,128)} %all-gather.5.cloned.1.call-done.k_ref, s32[1,128]{1,0:T(1,128)} %bitcast.2), custom_call_target="tpu_custom_call" | custom-call | tf_op jit(solution)/shard_map/pallas_call | solution.py:136
  74.5 28.9 %all-gather.3.cloned.1.call-done.k_ref = f32[2048,512]{1,0:T(8,128)} async-done(((f32[256,512]{1,0:T(8,128)}), f32[2048,512]{1,0:T(8,128)}) %all-gather.3.cloned.1.call-update) | async-done | bytes 4194320 | tf_op jit(solution)/shard_map/all_gather | solution.py:157
  103.4 19.1 %shard_map.47 = f32[128,2048]{1,0:T(8,128)} custom-call(s32[1]{0:T(128)} %bitcast.nb_ref, f32[128,2048]{1,0:T(8,128)} %get-tuple-element.6.q_ref, f32[2048,512]{1,0:T(8,128)} %all-gather.3.cloned.1.call-done.k_ref, s32[1,128]{1,0:T(1,128)} %bitcast.3, f32[2048,128]{1,0:T(8,128)} %shard_map.46.refs_0_), custom_call_target="tpu_custom_call" | custom-call | tf_op jit(solution)/shard_map/pallas_call | solution.py:136
  122.5 0.0 reduce-scatter.2.cloned.1.call-update
  122.6 28.5 %reduce-scatter.2.cloned.1.call-done = f32[128,1024]{1,0:T(8,128)} async-done(((f32[128,2048]{1,0:T(8,128)}), f32[128,1024]{1,0:T(8,128)}) %reduce-scatter.2.cloned.1.call-update) | async-done | bytes 524304 | tf_op jit(solution)/shard_map/reduce_scatter | solution.py:161
Async XLA Ops:
  6.5 3.3 %copy-start.1 = (s32[128]{0:T(128)S(1)}, s32[128]{0:T(128)}, u32[]{:S(2)}) copy-start(s32[128]{0:T(128)} %param.7) | copy-start | bytes 1540
  6.5 6.7 %copy-start = (f32[128,4096]{1,0:T(8,128)S(1)}, f32[128,4096]{1,0:T(8,128)}, u32[]{:S(2)}) copy-start(f32[128,4096]{1,0:T(8,128)} %param.4) | copy-start | bytes 6291460
  6.5 49.4 %all-gather.5.cloned.1.call-start = ((), (), s32[]{:S(2)}) async-start(), calls=%async_computation.2 | async-start | bytes 4718592 | tf_op jit(solution)/shard_map/all_gather | solution.py:157
  8.9 94.5 %all-gather.3.cloned.1.call-start = ((), (), s32[]{:S(2)}) async-start(), calls=%async_computation.1 | async-start | bytes 4718592 | tf_op jit(solution)/shard_map/all_gather | solution.py:157
  9.8 141.2 %reduce-scatter.2.cloned.1.call-start = ((), (), s32[]{:S(2)}) async-start(), calls=%async_computation.3 | async-start | bytes 1572864 | tf_op jit(solution)/shard_map/reduce_scatter | solution.py:161
Sparse Core Ops, SparseCore 0:
  9.0 46.8 all-gather.4
  57.5 45.8 all-gather.2
  122.7 28.3 reduce-scatter.1

commit v6 on v5

--- a/solution.py
+++ b/solution.py
@@ -142,7 +142,17 @@
     )(*operands)
 
 
-def per_device(queries, key_max, key_min, limits):
+def head_sum_scatter(acc, head_devices):
+    if head_devices != 2:
+        return lax.psum_scatter(acc, "head", scatter_dimension=1, tiled=True)
+    half = acc.shape[1] // 2
+    first_half = lax.axis_index("head") == 0
+    own = jnp.where(first_half, acc[:, :half], acc[:, half:])
+    other = jnp.where(first_half, acc[:, half:], acc[:, :half])
+    return own + lax.ppermute(other, "head", [(0, 1), (1, 0)])
+
+
+def per_device(queries, key_max, key_min, limits, head_devices):
     local_pages = key_max.shape[0]
     kv_count = key_max.shape[1] // DH
     call_count = min(kv_count, GATHERS)
@@ -158,7 +168,7 @@
         acc = page_mass_group(
             nb, queries[:, g * group_cols:(g + 1) * group_cols], keys, limits, acc,
             last=g == call_count - 1)
-    return lax.psum_scatter(acc, "head", scatter_dimension=1, tiled=True)
+    return head_sum_scatter(acc, head_devices)
 
 
 def solution(mesh):
@@ -169,7 +179,7 @@
         P(("grp", "row", "rep")),
     )
     return jax.shard_map(
-        per_device,
+        functools.partial(per_device, head_devices=mesh.shape["head"]),
         mesh=mesh,
         in_specs=placed,
         out_specs=P(("grp", "row", "rep"), "head"),

time: 160 us -> 152 us (0.950)
  the two profiles are of different devices: /device:TPU:16 before, /device:TPU:25 now
where the time goes in v6:
time: 152 us
  waiting for transfers between devices  72.3 us (48%)
  Pallas kernels  53.8 us (35%)
  between operations  16 us (11%)
  other arithmetic  5.68 us (4%)
  local copies, waits for them, and re-layouts  3.03 us (2%)
    all_gather x2, waiting for transfers between devices, per_device(): lax.all_gather(jnp.concatenate(parts, axis=1), ('row', 'rep'), axis=0, ti...  61.7 us
    pallas_call x2, Pallas kernels, page_mass_group(): pl.pallas_call(kernel, grid_spec=grid_spec, out_shape=jax.ShapeDtypeStruc...  53.8 us
    ppermute x1, waiting for transfers between devices, head_sum_scatter(): return own + lax.ppermute(other, 'head', [(0, 1), (1, 0)])  10.6 us
  transfers between devices with their start and end apart: 3, of which 3 were waited for; matrix products, arithmetic and copies ran while one was open for 2% of the time, Pallas kernels for 18%

profile of v6, /device:TPU:25, one launch (start us, length us, event | category | flops | bytes accessed | tf_op | source)
XLA Modules:
  0.0 152.0 jit_solution(17542720318019622674)
XLA Ops:
  6.5 0.0 copy-start.1
  6.5 0.0 copy-start
  6.5 0.0 all-gather.5.cloned.1.call-start
  6.5 1.5 fusion.1
  8.1 0.8 pad_maximum_fusion.1
  8.9 0.0 all-gather.5.cloned.1.call-update
  8.9 0.0 all-gather.3.cloned.1.call-start
  9.0 0.8 pad_maximum_fusion
  9.8 0.0 all-gather.3.cloned.1.call-update
  9.8 0.0 copy-done.1
  9.8 0.7 reduce_max.9
  13.0 0.0 copy-done
  13.1 1.5 fusion
  14.6 40.8 %all-gather.5.cloned.1.call-done.k_ref = f32[2048,512]{1,0:T(8,128)} async-done(((f32[256,512]{1,0:T(8,128)}), f32[2048,512]{1,0:T(8,128)}) %all-gather.5.cloned.1.call-update) | async-done | bytes 4194320 | tf_op jit(solution)/shard_map/all_gather | solution.py:167
  55.4 26.6 %shard_map.46.refs_0_ = f32[2048,128]{1,0:T(8,128)} custom-call(s32[1]{0:T(128)} %bitcast.nb_ref, f32[128,2048]{1,0:T(8,128)} %get-tuple-element.5.q_ref, f32[2048,512]{1,0:T(8,128)} %all-gather.5.cloned.1.call-done.k_ref, s32[1,128]{1,0:T(1,128)} %bitcast.2), custom_call_target="tpu_custom_call" | custom-call | tf_op jit(solution)/shard_map/pallas_call | solution.py:136
  82.1 20.9 %all-gather.3.cloned.1.call-done.k_ref = f32[2048,512]{1,0:T(8,128)} async-done(((f32[256,512]{1,0:T(8,128)}), f32[2048,512]{1,0:T(8,128)}) %all-gather.3.cloned.1.call-update) | async-done | bytes 4194320 | tf_op jit(solution)/shard_map/all_gather | solution.py:167
  102.9 27.2 %shard_map.47 = f32[128,2048]{1,0:T(8,128)} custom-call(s32[1]{0:T(128)} %bitcast.nb_ref, f32[128,2048]{1,0:T(8,128)} %get-tuple-element.6.q_ref, f32[2048,512]{1,0:T(8,128)} %all-gather.3.cloned.1.call-done.k_ref, s32[1,128]{1,0:T(1,128)} %bitcast.3, f32[2048,128]{1,0:T(8,128)} %shard_map.46.refs_0_), custom_call_target="tpu_custom_call" | custom-call | tf_op jit(solution)/shard_map/pallas_call | solution.py:136
  130.1 1.3 slice_select_fusion
  131.4 1.2 collective-permute-start
  132.6 10.6 %collective-permute-done = f32[128,1024]{1,0:T(8,128)S(1)} collective-permute-done((f32[128,1024]{1,0:T(8,128)S(1)}, f32[128,1024]{1,0:T(8,128)S(1)}, u32[]{:S(2)}, u32[]{:S(2)}) %collective-permute-start) | collective-permute-done | bytes 524320 | tf_op jit(solution)/shard_map/ppermute | solution.py:152
  143.1 2.1 %select_add_fusion = f32[128,1024]{1,0:T(8,128)} fusion(f32[128,1024]{1,0:T(8,128)S(1)} %collective-permute-done, f32[128,2048]{1,0:T(8,128)} %shard_map.47, pred[]{:T(512)S(6)} %eq.3), kind=kLoop, calls=%fused_computation.2 | loop fusion | flops 262144 | bytes 2097153 | tf_op jit(solution)/shard_map/add | solution.py:152
Async XLA Ops:
  6.5 3.3 %copy-start.1 = (s32[128]{0:T(128)S(1)}, s32[128]{0:T(128)}, u32[]{:S(2)}) copy-start(s32[128]{0:T(128)} %param.7) | copy-start | bytes 1540
  6.5 6.5 %copy-start = (f32[128,4096]{1,0:T(8,128)S(1)}, f32[128,4096]{1,0:T(8,128)}, u32[]{:S(2)}) copy-start(f32[128,4096]{1,0:T(8,128)} %param.4) | copy-start | bytes 6291460
  6.5 48.9 %all-gather.5.cloned.1.call-start = ((), (), s32[]{:S(2)}) async-start(), calls=%async_computation.1 | async-start | bytes 4718592 | tf_op jit(solution)/shard_map/all_gather | solution.py:167
  8.9 94.0 %all-gather.3.cloned.1.call-start = ((), (), s32[]{:S(2)}) async-start(), calls=%async_computation | async-start | bytes 4718592 | tf_op jit(solution)/shard_map/all_gather | solution.py:167
  131.4 11.7 %collective-permute-start = (f32[128,1024]{1,0:T(8,128)S(1)}, f32[128,1024]{1,0:T(8,128)S(1)}, u32[]{:S(2)}, u32[]{:S(2)}) collective-permute-start(f32[128,1024]{1,0:T(8,128)S(1)} %slice_select_fusion), channel_id=1, source_target_pairs={{0,2},{2,0},{1,3},{3,1},{4,6},{6,4},{5,7},{7,5},{8,10},{10,8},{9,1... | collective-permute-start | bytes 1572872 | tf_op jit(solution)/shard_map/ppermute | solution.py:152
Sparse Core Ops, SparseCore 0:
  9.0 46.3 all-gather.4
  57.0 45.8 all-gather.2

commit v7 on v6

--- a/solution.py
+++ b/solution.py
@@ -11,6 +11,7 @@
 DH = 128
 CHUNK = 256
 GATHERS = 2
+MM_CHUNK = 1024
 
 
 def _split(x):
@@ -27,6 +28,7 @@
         acc_in_ref, out_ref, kcat_ref, s_ref, acc_ref = refs
     hp = pl.program_id(0)
     nb = nb_ref[0]
+    nfull = nb_ref[1]
     row_count = q_ref.shape[0]
     lanes = 2 * row_count
 
@@ -60,15 +62,30 @@
     def vreg_fold(v, op):
         return op(v.reshape(CHUNK // 8, 8, lanes), axis=0)
 
+    mm_pages = min(MM_CHUNK, chunk_count * CHUNK)
+    for mc in range(chunk_count * CHUNK // mm_pages):
+        @pl.when(mc * mm_pages < nb * CHUNK)
+        def _():
+            s_ref[mc * mm_pages:(mc + 1) * mm_pages, :] = jnp.dot(
+                kcat_ref[mc * mm_pages:(mc + 1) * mm_pages, :], wcat,
+                preferred_element_type=jnp.float32)
+
     top = jnp.full((8, lanes), -jnp.inf, jnp.float32)
     for c in range(chunk_count):
-        def pass_scores(top, c=c):
-            s = jnp.dot(kcat_ref[c * CHUNK:(c + 1) * CHUNK, :], wcat,
-                        preferred_element_type=jnp.float32)
-            s = jnp.where(page_in_chunk + c * CHUNK <= lim2, s, -1e30)
+        def keep(top):
+            return top
+
+        def open_chunk(top, c=c):
+            return jnp.maximum(top, vreg_fold(s_ref[c * CHUNK:(c + 1) * CHUNK, :], jnp.max))
+
+        def masked_chunk(top, c=c):
+            s = s_ref[c * CHUNK:(c + 1) * CHUNK, :]
+            s = jnp.where(page_in_chunk <= lim2 - c * CHUNK, s, -1e30)
             s_ref[c * CHUNK:(c + 1) * CHUNK, :] = s
             return jnp.maximum(top, vreg_fold(s, jnp.max))
-        top = lax.cond(c < nb, pass_scores, lambda t: t, top)
+
+        branch = jnp.where(c < nb, jnp.where(c < nfull, 1, 2), 0)
+        top = lax.switch(branch, [keep, open_chunk, masked_chunk], top)
     top = jnp.max(top, axis=0, keepdims=True)
 
     total = jnp.zeros((8, lanes), jnp.float32)
@@ -158,7 +175,7 @@
     call_count = min(kv_count, GATHERS)
     kv_per_call = kv_count // call_count
     group_cols = queries.shape[1] // call_count
-    nb = (jnp.max(limits) // CHUNK + 1).astype(jnp.int32).reshape(1)
+    nb = jnp.stack([jnp.max(limits) // CHUNK + 1, (jnp.min(limits) + 1) // CHUNK]).astype(jnp.int32)
     acc = None
     for g in range(call_count):
         parts = []

time: 152 us -> 149 us (0.980)
  the two profiles are of different devices: /device:TPU:25 before, /device:TPU:16 now
where the time goes in v7:
time: 149 us; the launch traced here: 148 us
  waiting for transfers between devices  81.7 us (55%)
  Pallas kernels  38.8 us (26%)
  between operations  16.7 us (11%)
  other arithmetic  6.32 us (4%)
  local copies, waits for them, and re-layouts  3.06 us (2%)
  starting transfers between devices  1.57 us (1%)
    all_gather x2, waiting for transfers between devices, per_device(): lax.all_gather(jnp.concatenate(parts, axis=1), ('row', 'rep'), axis=0, ti...  68.4 us
    pallas_call x2, Pallas kernels, page_mass_group(): pl.pallas_call(kernel, grid_spec=grid_spec, out_shape=jax.ShapeDtypeStruc...  38.8 us
    ppermute x1, waiting for transfers between devices, head_sum_scatter(): return own + lax.ppermute(other, 'head', [(0, 1), (1, 0)])  13.3 us
  transfers between devices with their start and end apart: 3, of which 3 were waited for; matrix products, arithmetic and copies ran while one was open for 2% of the time, Pallas kernels for 13%

profile of v7, /device:TPU:16, one launch (start us, length us, event | category | flops | bytes accessed | tf_op | source)
XLA Modules:
  0.0 148.2 jit_solution(4187301556984318412)
XLA Ops:
  6.5 0.0 copy-start.1
  6.5 0.0 copy-start
  6.5 0.0 all-gather.5.cloned.1.call-start
  6.5 1.5 %fusion.2 = (f32[256,128]{1,0:T(8,128)S(1)}, f32[256,128]{1,0:T(8,128)S(1)}, f32[256,128]{1,0:T(8,128)S(1)}, f32[256,128]{1,0:T(8,128)S(1)}, f32[256,128]{1,0:T(...) fusion(f32[256,512]{1,0:T(8,128)} %param.5, f32[256,512]{1,0:T(8,128)} %param.6), kind=kLoop, calls=%fused_computation.7 | loop fusion | bytes 2097152 | tf_op jit(solution)/shard_map/slice | solution.py:183
  8.1 0.8 pad_maximum_fusion.1
  8.9 0.0 all-gather.5.cloned.1.call-update
  8.9 0.0 all-gather.3.cloned.1.call-start
  9.0 0.8 pad_maximum_fusion
  9.8 0.0 all-gather.3.cloned.1.call-update
  9.8 0.0 copy-done.1
  9.8 0.7 fusion
  13.8 0.6 pad_add_fusion.nb_ref
  14.4 0.0 copy-done
  14.4 1.5 %fusion.1 = (f32[128,2048]{1,0:T(8,128)}, f32[128,2048]{1,0:T(8,128)}) fusion(f32[128,4096]{1,0:T(8,128)S(1)} %copy-done), kind=kLoop, calls=%fused_computation.6 | loop fusion | bytes 4194304 | tf_op jit(solution)/shard_map/slice | solution.py:186
  15.9 40.0 %all-gather.5.cloned.1.call-done.k_ref = f32[2048,512]{1,0:T(8,128)} async-done(((f32[256,512]{1,0:T(8,128)}), f32[2048,512]{1,0:T(8,128)}) %all-gather.5.cloned.1.call-update) | async-done | bytes 4194320 | tf_op jit(solution)/shard_map/all_gather | solution.py:184
  55.9 19.1 %shard_map.46.refs_0_ = f32[2048,128]{1,0:T(8,128)} custom-call(s32[2]{0:T(128)} %pad_add_fusion.nb_ref, f32[128,2048]{1,0:T(8,128)} %get-tuple-element.7.q_ref, f32[2048,512]{1,0:T(8,128)} %all-gather.5.cloned.1.call-done.k_ref, s32[1,128]{1,0:T(1,128)} %bitcast.3), custom_call_target="tpu_custom_call" | custom-call | tf_op jit(solution)/shard_map/pallas_call | solution.py:153
  75.1 28.4 %all-gather.3.cloned.1.call-done.k_ref = f32[2048,512]{1,0:T(8,128)} async-done(((f32[256,512]{1,0:T(8,128)}), f32[2048,512]{1,0:T(8,128)}) %all-gather.3.cloned.1.call-update) | async-done | bytes 4194320 | tf_op jit(solution)/shard_map/all_gather | solution.py:184
  103.4 19.7 %shard_map.47 = f32[128,2048]{1,0:T(8,128)} custom-call(s32[2]{0:T(128)} %pad_add_fusion.nb_ref, f32[128,2048]{1,0:T(8,128)} %get-tuple-element.8.q_ref, f32[2048,512]{1,0:T(8,128)} %all-gather.3.cloned.1.call-done.k_ref, s32[1,128]{1,0:T(1,128)} %bitcast.4, f32[2048,128]{1,0:T(8,128)} %shard_map.46.refs_0_), custom_call_target="tpu_custom_call" | custom-call | tf_op jit(solution)/shard_map/pallas_call | solution.py:153
  123.1 1.3 slice_select_fusion
  124.4 1.5 %collective-permute-start = (f32[128,1024]{1,0:T(8,128)S(1)}, f32[128,1024]{1,0:T(8,128)S(1)}, u32[]{:S(2)}, u32[]{:S(2)}) collective-permute-start(f32[128,1024]{1,0:T(8,128)S(1)} %slice_select_fusion), channel_id=1, source_target_pairs={{0,2},{2,0},{1,3},{3,1},{4,6},{6,4},{5,7},{7,5},{8,10},{10,8},{9,1... | collective-permute-start | bytes 1572872 | tf_op jit(solution)/shard_map/ppermute | solution.py:169
  125.9 13.3 %collective-permute-done = f32[128,1024]{1,0:T(8,128)S(1)} collective-permute-done((f32[128,1024]{1,0:T(8,128)S(1)}, f32[128,1024]{1,0:T(8,128)S(1)}, u32[]{:S(2)}, u32[]{:S(2)}) %collective-permute-start) | collective-permute-done | bytes 524320 | tf_op jit(solution)/shard_map/ppermute | solution.py:169
  139.2 2.1 %select_add_fusion = f32[128,1024]{1,0:T(8,128)} fusion(f32[128,1024]{1,0:T(8,128)S(1)} %collective-permute-done, f32[128,2048]{1,0:T(8,128)} %shard_map.47, pred[]{:T(512)S(6)} %eq.3), kind=kLoop, calls=%fused_computation.2 | loop fusion | flops 262144 | bytes 2097153 | tf_op jit(solution)/shard_map/add | solution.py:169
Async XLA Ops:
  6.5 3.3 %copy-start.1 = (s32[128]{0:T(128)S(1)}, s32[128]{0:T(128)}, u32[]{:S(2)}) copy-start(s32[128]{0:T(128)} %param.7) | copy-start | bytes 1540
  6.5 7.8 %copy-start = (f32[128,4096]{1,0:T(8,128)S(1)}, f32[128,4096]{1,0:T(8,128)}, u32[]{:S(2)}) copy-start(f32[128,4096]{1,0:T(8,128)} %param.4) | copy-start | bytes 6291460
  6.5 49.4 %all-gather.5.cloned.1.call-start = ((), (), s32[]{:S(2)}) async-start(), calls=%async_computation.1 | async-start | bytes 4718592 | tf_op jit(solution)/shard_map/all_gather | solution.py:184
  8.9 94.5 %all-gather.3.cloned.1.call-start = ((), (), s32[]{:S(2)}) async-start(), calls=%async_computation | async-start | bytes 4718592 | tf_op jit(solution)/shard_map/all_gather | solution.py:184
  124.4 14.8 %collective-permute-start = (f32[128,1024]{1,0:T(8,128)S(1)}, f32[128,1024]{1,0:T(8,128)S(1)}, u32[]{:S(2)}, u32[]{:S(2)}) collective-permute-start(f32[128,1024]{1,0:T(8,128)S(1)} %slice_select_fusion), channel_id=1, source_target_pairs={{0,2},{2,0},{1,3},{3,1},{4,6},{6,4},{5,7},{7,5},{8,10},{10,8},{9,1... | collective-permute-start | bytes 1572872 | tf_op jit(solution)/shard_map/ppermute | solution.py:169
Sparse Core Ops, SparseCore 0:
  9.0 46.8 all-gather.4
  57.5 45.8 all-gather.2

commit v8 on v7

--- a/solution.py
+++ b/solution.py
@@ -169,7 +169,26 @@
     return own + lax.ppermute(other, "head", [(0, 1), (1, 0)])
 
 
-def per_device(queries, key_max, key_min, limits, head_devices):
+def causal_gather(block, row_devices):
+    z = lax.axis_index("row")
+    r = lax.axis_index("rep")
+    block_pages = block.shape[0]
+    forward = [(i, i + 1) for i in range(row_devices - 1)]
+    mine = [block]
+    for _ in range(1, row_devices):
+        mine.append(lax.ppermute(mine[-1], "row", forward))
+    mine = jnp.stack(mine)
+    sibling = lax.ppermute(mine, "rep", [(0, 1), (1, 0)])
+    slots = 2 * row_devices
+    out = jnp.zeros((slots * block_pages, block.shape[1]), block.dtype)
+    for k in range(row_devices):
+        for part, rep_index in ((mine[k], r), (sibling[k], 1 - r)):
+            slot = jnp.where(z >= k, 2 * (z - k) + rep_index, slots - 1)
+            out = lax.dynamic_update_slice(out, part, (slot * block_pages, 0))
+    return out
+
+
+def per_device(queries, key_max, key_min, limits, head_devices, row_devices):
     local_pages = key_max.shape[0]
     kv_count = key_max.shape[1] // DH
     call_count = min(kv_count, GATHERS)
@@ -181,7 +200,11 @@
         parts = []
         for kv in range(g * kv_per_call, (g + 1) * kv_per_call):
             parts += [key_max[:, kv * DH:(kv + 1) * DH], key_min[:, kv * DH:(kv + 1) * DH]]
-        keys = lax.all_gather(jnp.concatenate(parts, axis=1), ("row", "rep"), axis=0, tiled=True)
+        bounds = jnp.concatenate(parts, axis=1)
+        if g == 0:
+            keys = lax.all_gather(bounds, ("row", "rep"), axis=0, tiled=True)
+        else:
+            keys = causal_gather(bounds, row_devices)
         acc = page_mass_group(
             nb, queries[:, g * group_cols:(g + 1) * group_cols], keys, limits, acc,
             last=g == call_count - 1)
@@ -196,7 +219,8 @@
         P(("grp", "row", "rep")),
     )
     return jax.shard_map(
-        functools.partial(per_device, head_devices=mesh.shape["head"]),
+        functools.partial(
+            per_device, head_devices=mesh.shape["head"], row_devices=mesh.shape["row"]),
         mesh=mesh,
         in_specs=placed,
         out_specs=P(("grp", "row", "rep"), "head"),

time: 149 us -> 172 us (1.15)
  the two profiles are of different devices: /device:TPU:16 before, /device:TPU:31 now
where the time goes in v8:
time: 172 us
  waiting for transfers between devices  82.1 us (48%)
  Pallas kernels  43.1 us (25%)
  between operations  16.3 us (9%)
  local copies, waits for them, and re-layouts  15.4 us (9%)
  other arithmetic  7.98 us (5%)
  starting transfers between devices  6.59 us (4%)
    ppermute x3, waiting for transfers between devices, causal_gather(): mine.append(lax.ppermute(mine[-1], 'row', forward))  69.6 us
    pallas_call x2, Pallas kernels, page_mass_group(): pl.pallas_call(kernel, grid_spec=grid_spec, out_shape=jax.ShapeDtypeStruc...  43.1 us
    ppermute x1, waiting for transfers between devices, head_sum_scatter(): return own + lax.ppermute(other, 'head', [(0, 1), (1, 0)])  12.5 us
    dynamic_update_slice x7, local copies, waits for them, and re-layouts, causal_gather(): out = lax.dynamic_update_slice(out, part, (slot * block_pages, 0))  10 us
    ppermute x3, starting transfers between devices, causal_gather(): mine.append(lax.ppermute(mine[-1], 'row', forward))  3.84 us
  transfers between devices with their start and end apart: 6, of which 4 were waited for; matrix products, arithmetic and copies ran while one was open for 10% of the time, Pallas kernels for 0%

profile of v8, /device:TPU:31, one launch (start us, length us, event | category | flops | bytes accessed | tf_op | source)
XLA Modules:
  0.0 171.6 jit_solution(7004511910501221621)
XLA Ops:
  6.5 1.4 fusion.7
  7.9 0.8 pad_maximum_fusion.2
  8.8 2.5 %broadcast_in_dim.3 = f32[2048,512]{1,0:T(8,128)} broadcast(f32[]{:T(128)} %constant.46.clone.1), dimensions={} | broadcast | bytes 4194308 | tf_op jit(solution)/shard_map/broadcast_in_dim | solution.py:183
  11.3 1.0 fusion.4
  12.2 1.3 collective-permute-start
  13.5 28.4 %collective-permute-done = f32[256,512]{1,0:T(8,128)S(1)} collective-permute-done((f32[256,512]{1,0:T(8,128)S(1)}, f32[256,512]{1,0:T(8,128)S(1)}, u32[]{:S(2)}, u32[]{:S(2)}) %collective-permute-start) | collective-permute-done | bytes 524320 | tf_op jit(solution)/shard_map/ppermute | solution.py:179
  41.9 1.3 collective-permute-start.1
  43.2 28.7 %collective-permute-done.1 = f32[256,512]{1,0:T(8,128)S(1)} collective-permute-done((f32[256,512]{1,0:T(8,128)S(1)}, f32[256,512]{1,0:T(8,128)S(1)}, u32[]{:S(2)}, u32[]{:S(2)}) %collective-permute-start.1) | collective-permute-done | bytes 524320 | tf_op jit(solution)/shard_map/ppermute | solution.py:179
  71.9 1.3 collective-permute-start.2
  73.2 12.5 %collective-permute-done.2 = f32[256,512]{1,0:T(8,128)S(1)} collective-permute-done((f32[256,512]{1,0:T(8,128)S(1)}, f32[256,512]{1,0:T(8,128)S(1)}, u32[]{:S(2)}, u32[]{:S(2)}) %collective-permute-start.2) | collective-permute-done | bytes 524320 | tf_op jit(solution)/shard_map/ppermute | solution.py:179
  85.7 1.5 pad_maximum_fusion
  87.2 2.4 %collective-permute-start.3 = (f32[4,256,512]{2,1,0:T(8,128)}, f32[4,256,512]{2,1,0:T(8,128)}, u32[]{:S(2)}, u32[]{:S(2)}) collective-permute-start(f32[4,256,512]{2,1,0:T(8,128)} %pad_maximum_fusion), channel_id=1, source_target_pairs={{0,1},{1,0},{2,3},{3,2},{4,5},{5,4},{6,7},{7,6},{8,9},{9,8},{10,11... | collective-permute-start | bytes 6291464 | tf_op jit(solution)/shard_map/ppermute | solution.py:181
  93.9 1.5 fusion.6
  95.4 1.9 %fusion.3 = f32[2048,512]{1,0:T(8,128)} fusion(f32[2048,512]{1,0:T(8,128)} %get-tuple-element.18, s32[]{:T(128)S(6)} %select_n.75, f32[4,256,512]{2,1,0:T(8,128)} %collective-permute-done.3), kind=kLoop, calls=%fused_computation.8 | loop fusion | bytes 1048580 | tf_op jit(solution)/shard_map/dynamic_update_slice | solution.py:187
  97.2 0.8 constant_dynamic-update-slice_fusion.2
  98.1 1.9 %fusion.2 = f32[2048,512]{1,0:T(8,128)} fusion(f32[2048,512]{1,0:T(8,128)} %constant_dynamic-update-slice_fusion.2, s32[]{:T(128)S(6)} %select_n.79, f32[4,256,512]{2,1,0:T(8,128)} %collective-permute-done.3), kind=kLoop, calls=%fused_computation.6 | loop fusion | bytes 1048580 | tf_op jit(solution)/shard_map/dynamic_update_slice | solution.py:187
  100.8 1.9 %fusion.1 = f32[2048,512]{1,0:T(8,128)} fusion(f32[2048,512]{1,0:T(8,128)} %constant_dynamic-update-slice_fusion.1, s32[]{:T(128)S(6)} %select_n.83, f32[4,256,512]{2,1,0:T(8,128)} %collective-permute-done.3), kind=kLoop, calls=%fused_computation.4 | loop fusion | bytes 1048580 | tf_op jit(solution)/shard_map/dynamic_update_slice | solution.py:187
  102.7 0.8 constant_dynamic-update-slice_fusion
  103.5 1.9 %fusion.k_ref = f32[2048,512]{1,0:T(8,128)} fusion(f32[2048,512]{1,0:T(8,128)} %constant_dynamic-update-slice_fusion, s32[]{:T(128)S(6)} %select_n.87, f32[4,256,512]{2,1,0:T(8,128)} %collective-permute-done.3), kind=kLoop, calls=%fused_computation.2 | loop fusion | bytes 1048580 | tf_op jit(solution)/shard_map/dynamic_update_slice | solution.py:187
  105.4 21.3 %shard_map.46.refs_0_ = f32[2048,128]{1,0:T(8,128)} custom-call(s32[2]{0:T(128)} %pad_add_fusion.nb_ref, f32[128,2048]{1,0:T(8,128)} %get-tuple-element.7.q_ref, f32[2048,512]{1,0:T(8,128)} %all-gather.2.cloned.1.call-done.k_ref, s32[1,128]{1,0:T(1,128)} %bitcast.27), custom_call_target="tpu_custom_call" | custom-call | tf_op jit(solution)/shard_map/pallas_call | solution.py:153
  126.8 21.8 %shard_map.47 = f32[128,2048]{1,0:T(8,128)} custom-call(s32[2]{0:T(128)} %pad_add_fusion.nb_ref, f32[128,2048]{1,0:T(8,128)} %get-tuple-element.8.q_ref, f32[2048,512]{1,0:T(8,128)} %fusion.k_ref, s32[1,128]{1,0:T(1,128)} %bitcast.28, f32[2048,128]{1,0:T(8,128)} %shard_map.46.refs_0_), custom_call_target="tpu_custom_call" | custom-call | tf_op jit(solution)/shard_map/pallas_call | solution.py:153
  148.6 1.3 slice_select_fusion
  150.1 12.5 %collective-permute-done.4 = f32[128,1024]{1,0:T(8,128)S(1)} collective-permute-done((f32[128,1024]{1,0:T(8,128)S(1)}, f32[128,1024]{1,0:T(8,128)S(1)}, u32[]{:S(2)}, u32[]{:S(2)}) %collective-permute-start.4) | collective-permute-done | bytes 524320 | tf_op jit(solution)/shard_map/ppermute | solution.py:169
  162.6 2.1 %select_add_fusion = f32[128,1024]{1,0:T(8,128)} fusion(f32[128,1024]{1,0:T(8,128)S(1)} %collective-permute-done.4, f32[128,2048]{1,0:T(8,128)} %shard_map.47, pred[]{:T(512)S(6)} %eq.3), kind=kLoop, calls=%fused_computation.11 | loop fusion | flops 262144 | bytes 2097153 | tf_op jit(solution)/shard_map/add | solution.py:169
  (16 shorter events, 2.5 us)
Async XLA Ops:
  6.5 98.9 %all-gather.2.cloned.1.call-start = ((), (), s32[]{:S(2)}) async-start(), calls=%async_computation | async-start | bytes 4718592 | tf_op jit(solution)/shard_map/all_gather | solution.py:205
  11.3 78.4 %copy-start.3 = (s32[128]{0:T(128)S(1)}, s32[128]{0:T(128)}, u32[]{:S(2)}) copy-start(s32[128]{0:T(128)} %param.7) | copy-start | bytes 1540
  11.3 82.6 %copy-start = (f32[128,4096]{1,0:T(8,128)S(1)}, f32[128,4096]{1,0:T(8,128)}, u32[]{:S(2)}) copy-start(f32[128,4096]{1,0:T(8,128)} %param.4) | copy-start | bytes 6291460
  12.2 29.7 %collective-permute-start = (f32[256,512]{1,0:T(8,128)S(1)}, f32[256,512]{1,0:T(8,128)S(1)}, u32[]{:S(2)}, u32[]{:S(2)}) collective-permute-start(f32[256,512]{1,0:T(8,128)S(1)} %get-tuple-element.19), channel_id=1, source_target_pairs={{0,4},{4,8},{8,12},{1,5},{5,9},{9,13},{2,6},{6,10},{10,14},{3,7},{... | collective-permute-start | bytes 1572872 | tf_op jit(solution)/shard_map/ppermute | solution.py:179
  41.9 30.0 %collective-permute-start.1 = (f32[256,512]{1,0:T(8,128)S(1)}, f32[256,512]{1,0:T(8,128)S(1)}, u32[]{:S(2)}, u32[]{:S(2)}) collective-permute-start(f32[256,512]{1,0:T(8,128)S(1)} %collective-permute-done), channel_id=1, source_target_pairs={{0,4},{4,8},{8,12},{1,5},{5,9},{9,13},{2,6},{6,10},{10,14},{3,7},{... | collective-permute-start | bytes 1572872 | tf_op jit(solution)/shard_map/ppermute | solution.py:179
  71.9 13.8 %collective-permute-start.2 = (f32[256,512]{1,0:T(8,128)S(1)}, f32[256,512]{1,0:T(8,128)S(1)}, u32[]{:S(2)}, u32[]{:S(2)}) collective-permute-start(f32[256,512]{1,0:T(8,128)S(1)} %collective-permute-done.1), channel_id=1, source_target_pairs={{0,4},{4,8},{8,12},{1,5},{5,9},{9,13},{2,6},{6,10},{10,14},{3,7},{... | collective-permute-start | bytes 1572872 | tf_op jit(solution)/shard_map/ppermute | solution.py:179
  85.7 1.5 copy-start.1
  87.2 8.2 %collective-permute-start.3 = (f32[4,256,512]{2,1,0:T(8,128)}, f32[4,256,512]{2,1,0:T(8,128)}, u32[]{:S(2)}, u32[]{:S(2)}) collective-permute-start(f32[4,256,512]{2,1,0:T(8,128)} %pad_maximum_fusion), channel_id=1, source_target_pairs={{0,1},{1,0},{2,3},{3,2},{4,5},{5,4},{6,7},{7,6},{8,9},{9,8},{10,11... | collective-permute-start | bytes 6291464 | tf_op jit(solution)/shard_map/ppermute | solution.py:181
  93.9 8.9 %copy-start.2 = (f32[256,512]{1,0:T(8,128)S(1)}, f32[256,512]{1,0:T(8,128)}, u32[]{:S(2)}) copy-start(f32[256,512]{1,0:T(8,128)} %copy-done.1) | copy-start | bytes 1572868
  149.8 12.8 %collective-permute-start.4 = (f32[128,1024]{1,0:T(8,128)S(1)}, f32[128,1024]{1,0:T(8,128)S(1)}, u32[]{:S(2)}, u32[]{:S(2)}) collective-permute-start(f32[128,1024]{1,0:T(8,128)S(1)} %slice_select_fusion), channel_id=1, source_target_pairs={{0,2},{2,0},{1,3},{3,1},{4,6},{6,4},{5,7},{7,5},{8,10},{10,8},{9,1... | collective-permute-start | bytes 1572872 | tf_op jit(solution)/shard_map/ppermute | solution.py:169
Sparse Core Ops, SparseCore 0:
  9.0 61.0 all-gather.1

commit v9 on v7

--- a/solution.py
+++ b/solution.py
@@ -10,7 +10,6 @@
 
 DH = 128
 CHUNK = 256
-GATHERS = 2
 MM_CHUNK = 1024
 
 
@@ -172,19 +171,19 @@
 def per_device(queries, key_max, key_min, limits, head_devices):
     local_pages = key_max.shape[0]
     kv_count = key_max.shape[1] // DH
-    call_count = min(kv_count, GATHERS)
-    kv_per_call = kv_count // call_count
-    group_cols = queries.shape[1] // call_count
+    head_cols = queries.shape[1] // kv_count
+    sizes = [kv_count - 1, 1] if kv_count > 1 else [kv_count]
     nb = jnp.stack([jnp.max(limits) // CHUNK + 1, (jnp.min(limits) + 1) // CHUNK]).astype(jnp.int32)
     acc = None
-    for g in range(call_count):
+    kv0 = 0
+    for g, size in enumerate(sizes):
         parts = []
-        for kv in range(g * kv_per_call, (g + 1) * kv_per_call):
+        for kv in range(kv0, kv0 + size):
             parts += [key_max[:, kv * DH:(kv + 1) * DH], key_min[:, kv * DH:(kv + 1) * DH]]
         keys = lax.all_gather(jnp.concatenate(parts, axis=1), ("row", "rep"), axis=0, tiled=True)
-        acc = page_mass_group(
-            nb, queries[:, g * group_cols:(g + 1) * group_cols], keys, limits, acc,
-            last=g == call_count - 1)
+        cols = slice(kv0 * head_cols, (kv0 + size) * head_cols)
+        acc = page_mass_group(nb, queries[:, cols], keys, limits, acc, last=g == len(sizes) - 1)
+        kv0 += size
     return head_sum_scatter(acc, head_devices)
 
 

time: 149 us -> 144 us (0.966)
  waiting for transfers between devices: 81.7 us -> 73.3 us
  local copies, waits for them, and re-layouts: 3.06 us -> 8.84 us
  other arithmetic: 6.32 us -> 4.24 us
    all_gather x2, waiting for transfers between devices: 68.4 us -> 60.4 us  [per_device(): lax.all_gather(jnp.concatenate(parts, axis=1), ('row', 'rep'), axis=0, ti...]
    unnamed x4 -> x13, local copies, waits for them, and re-layouts: 0.01 us -> 5.71 us
  transfers between devices with their start and end apart: 3 -> 3, of which waited for: 3 -> 3; matrix products, arithmetic and copies ran while one was open for 2% -> 3% of each run, Pallas kernels for 13% -> 19%
where the time goes in v9:
time: 144 us
  waiting for transfers between devices  73.3 us (51%)
  Pallas kernels  38.9 us (27%)
  between operations  16.7 us (12%)
  local copies, waits for them, and re-layouts  8.84 us (6%)
  other arithmetic  4.24 us (3%)
  starting transfers between devices  1.58 us (1%)
    all_gather x2, waiting for transfers between devices, per_device(): lax.all_gather(jnp.concatenate(parts, axis=1), ('row', 'rep'), axis=0, ti...  60.4 us
    pallas_call x2, Pallas kernels, page_mass_group(): pl.pallas_call(kernel, grid_spec=grid_spec, out_shape=jax.ShapeDtypeStruc...  38.9 us
    ppermute x1, waiting for transfers between devices, head_sum_scatter(): return own + lax.ppermute(other, 'head', [(0, 1), (1, 0)])  12.9 us
    unnamed x13, local copies, waits for them, and re-layouts  5.71 us
  transfers between devices with their start and end apart: 3, of which 3 were waited for; matrix products, arithmetic and copies ran while one was open for 3% of the time, Pallas kernels for 19%

profile of v9, /device:TPU:16, one launch (start us, length us, event | category | flops | bytes accessed | tf_op | source)
XLA Modules:
  0.0 143.6 jit_solution(10808748856950822312)
XLA Ops:
  6.5 0.0 all-gather.5.cloned.1.call-start
  6.5 1.1 slice_dynamic-update-slice_fusion.5
  7.6 0.9 slice_dynamic-update-slice_fusion.4
  8.5 0.9 slice_dynamic-update-slice_fusion.3
  9.4 0.9 slice_dynamic-update-slice_fusion.2
  10.4 1.0 slice_dynamic-update-slice_fusion.1
  11.4 1.0 slice_dynamic-update-slice_fusion
  12.4 0.9 copy-done.2
  13.3 0.0 all-gather.5.cloned.1.call-update
  13.3 0.0 all-gather.3.cloned.1.call-start
  13.3 0.7 pad_maximum_fusion
  14.1 0.0 all-gather.3.cloned.1.call-update
  14.1 0.7 fusion
  18.0 1.3 slice.41.q_ref
  19.3 0.8 slice.38.q_ref
  20.1 0.6 pad_add_fusion.nb_ref
  20.8 57.2 %all-gather.5.cloned.1.call-done.k_ref = f32[2048,768]{1,0:T(8,128)} async-done(((f32[256,768]{1,0:T(8,128)}), f32[2048,768]{1,0:T(8,128)}) %all-gather.5.cloned.1.call-update) | async-done | bytes 6291472 | tf_op jit(solution)/shard_map/all_gather | solution.py:183
  77.9 27.0 %shard_map.46.refs_0_ = f32[2048,128]{1,0:T(8,128)} custom-call(s32[2]{0:T(128)} %pad_add_fusion.nb_ref, f32[128,3072]{1,0:T(8,128)} %slice.41.q_ref, f32[2048,768]{1,0:T(8,128)} %all-gather.5.cloned.1.call-done.k_ref, s32[1,128]{1,0:T(1,128)} %bitcast.3), custom_call_target="tpu_custom_call" | custom-call | tf_op jit(solution)/shard_map/pallas_call | solution.py:152
  105.0 3.2 %all-gather.3.cloned.1.call-done.k_ref = f32[2048,256]{1,0:T(8,128)} async-done(((f32[256,256]{1,0:T(8,128)}), f32[2048,256]{1,0:T(8,128)}) %all-gather.3.cloned.1.call-update) | async-done | bytes 2097168 | tf_op jit(solution)/shard_map/all_gather | solution.py:183
  108.2 11.9 %shard_map.47 = f32[128,2048]{1,0:T(8,128)} custom-call(s32[2]{0:T(128)} %pad_add_fusion.nb_ref, f32[128,1024]{1,0:T(8,128)} %slice.38.q_ref, f32[2048,256]{1,0:T(8,128)} %all-gather.3.cloned.1.call-done.k_ref, s32[1,128]{1,0:T(1,128)} %bitcast.4, f32[2048,128]{1,0:T(8,128)} %shard_map.46.refs_0_), custom_call_target="tpu_custom_call" | custom-call | tf_op jit(solution)/shard_map/pallas_call | solution.py:152
  120.1 1.3 slice_select_fusion
  121.4 1.5 %collective-permute-start = (f32[128,1024]{1,0:T(8,128)S(1)}, f32[128,1024]{1,0:T(8,128)S(1)}, u32[]{:S(2)}, u32[]{:S(2)}) collective-permute-start(f32[128,1024]{1,0:T(8,128)S(1)} %slice_select_fusion), channel_id=1, source_target_pairs={{0,2},{2,0},{1,3},{3,1},{4,6},{6,4},{5,7},{7,5},{8,10},{10,8},{9,1... | collective-permute-start | bytes 1572872 | tf_op jit(solution)/shard_map/ppermute | solution.py:168
  122.9 12.9 %collective-permute-done = f32[128,1024]{1,0:T(8,128)S(1)} collective-permute-done((f32[128,1024]{1,0:T(8,128)S(1)}, f32[128,1024]{1,0:T(8,128)S(1)}, u32[]{:S(2)}, u32[]{:S(2)}) %collective-permute-start) | collective-permute-done | bytes 524320 | tf_op jit(solution)/shard_map/ppermute | solution.py:168
  135.9 0.9 select_add_fusion
  (7 shorter events, 0.0 us)
Async XLA Ops:
  6.5 7.6 %copy-start.3 = (s32[128]{0:T(128)S(1)}, s32[128]{0:T(128)}, u32[]{:S(2)}) copy-start(s32[128]{0:T(128)} %param.7) | copy-start | bytes 1540
  6.5 11.5 %copy-start.1 = (f32[128,4096]{1,0:T(8,128)S(1)}, f32[128,4096]{1,0:T(8,128)}, u32[]{:S(2)}) copy-start(f32[128,4096]{1,0:T(8,128)} %param.4) | copy-start | bytes 6291460
  6.5 71.4 %all-gather.5.cloned.1.call-start = ((), (), s32[]{:S(2)}) async-start(), calls=%async_computation.1 | async-start | bytes 7077888 | tf_op jit(solution)/shard_map/all_gather | solution.py:183
  12.4 0.9 copy-start.2
  13.3 94.9 %all-gather.3.cloned.1.call-start = ((), (), s32[]{:S(2)}) async-start(), calls=%async_computation | async-start | bytes 2359296 | tf_op jit(solution)/shard_map/all_gather | solution.py:183
  120.1 15.8 %copy-start = (f32[128,2048]{1,0:T(8,128)S(1)}, f32[128,2048]{1,0:T(8,128)}, u32[]{:S(2)}) copy-start(f32[128,2048]{1,0:T(8,128)} %shard_map.47) | copy-start | bytes 3145732
  121.4 14.5 %collective-permute-start = (f32[128,1024]{1,0:T(8,128)S(1)}, f32[128,1024]{1,0:T(8,128)S(1)}, u32[]{:S(2)}, u32[]{:S(2)}) collective-permute-start(f32[128,1024]{1,0:T(8,128)S(1)} %slice_select_fusion), channel_id=1, source_target_pairs={{0,2},{2,0},{1,3},{3,1},{4,6},{6,4},{5,7},{7,5},{8,10},{10,8},{9,1... | collective-permute-start | bytes 1572872 | tf_op jit(solution)/shard_map/ppermute | solution.py:168
Sparse Core Ops, SparseCore 0:
  13.4 64.4 all-gather.4
  79.5 28.5 all-gather.2

commit v10 on v9

--- a/solution.py
+++ b/solution.py
@@ -22,9 +22,9 @@
 def _mass_kernel(nb_ref, q_ref, k_ref, lim_ref, *refs, chunk_count, score_scale, first, last,
                  pairs_per_kv):
     if first:
-        out_ref, kcat_ref, s_ref, acc_ref = refs
+        out_ref, kcat_ref, s_ref, acc_ref, tops_ref = refs
     else:
-        acc_in_ref, out_ref, kcat_ref, s_ref, acc_ref = refs
+        acc_in_ref, out_ref, kcat_ref, s_ref, acc_ref, tops_ref = refs
     hp = pl.program_id(0)
     nb = nb_ref[0]
     nfull = nb_ref[1]
@@ -62,12 +62,16 @@
         return op(v.reshape(CHUNK // 8, 8, lanes), axis=0)
 
     mm_pages = min(MM_CHUNK, chunk_count * CHUNK)
+    per_mm = mm_pages // CHUNK
     for mc in range(chunk_count * CHUNK // mm_pages):
         @pl.when(mc * mm_pages < nb * CHUNK)
         def _():
-            s_ref[mc * mm_pages:(mc + 1) * mm_pages, :] = jnp.dot(
-                kcat_ref[mc * mm_pages:(mc + 1) * mm_pages, :], wcat,
-                preferred_element_type=jnp.float32)
+            s = jnp.dot(kcat_ref[mc * mm_pages:(mc + 1) * mm_pages, :], wcat,
+                        preferred_element_type=jnp.float32)
+            s_ref[mc * mm_pages:(mc + 1) * mm_pages, :] = s
+            for j in range(per_mm):
+                c = mc * per_mm + j
+                tops_ref[c * 8:(c + 1) * 8, :] = vreg_fold(s[j * CHUNK:(j + 1) * CHUNK, :], jnp.max)
 
     top = jnp.full((8, lanes), -jnp.inf, jnp.float32)
     for c in range(chunk_count):
@@ -75,7 +79,7 @@
             return top
 
         def open_chunk(top, c=c):
-            return jnp.maximum(top, vreg_fold(s_ref[c * CHUNK:(c + 1) * CHUNK, :], jnp.max))
+            return jnp.maximum(top, tops_ref[c * 8:(c + 1) * 8, :])
 
         def masked_chunk(top, c=c):
             s = s_ref[c * CHUNK:(c + 1) * CHUNK, :]
@@ -90,7 +94,7 @@
     total = jnp.zeros((8, lanes), jnp.float32)
     for c in range(chunk_count):
         def pass_exp(total, c=c):
-            e = jnp.exp(s_ref[c * CHUNK:(c + 1) * CHUNK, :] - top)
+            e = jnp.exp2(s_ref[c * CHUNK:(c + 1) * CHUNK, :] - top)
             s_ref[c * CHUNK:(c + 1) * CHUNK, :] = e
             return total + vreg_fold(e, jnp.sum)
         total = lax.cond(c < nb, pass_exp, lambda t: t, total)
@@ -122,7 +126,7 @@
     chunk_count = page_count // CHUNK
     first = acc is None
     kernel = functools.partial(
-        _mass_kernel, chunk_count=chunk_count, score_scale=1.0 / math.sqrt(DH),
+        _mass_kernel, chunk_count=chunk_count, score_scale=math.log2(math.e) / math.sqrt(DH),
         first=first, last=last, pairs_per_kv=pairs_per_kv)
     in_specs = [
         pl.BlockSpec((row_count, 2 * DH), lambda hp, nb: (0, hp)),
@@ -147,6 +151,7 @@
             pltpu.VMEM((page_count, 6 * DH), jnp.bfloat16),
             pltpu.VMEM((page_count, 2 * row_count), jnp.float32),
             pltpu.VMEM((page_count, row_count), jnp.float32),
+            pltpu.VMEM((chunk_count * 8, 2 * row_count), jnp.float32),
         ],
     )
     return pl.pallas_call(

time: 144 us -> 144 us (level)
  transfers between devices with their start and end apart: 3 -> 3, of which waited for: 3 -> 3; matrix products, arithmetic and copies ran while one was open for 3% -> 3% of each run, Pallas kernels for 19% -> 18%
where the time goes in v10:
time: 144 us; the launch traced here: 143 us
  waiting for transfers between devices  74.2 us (52%)
  Pallas kernels  37.7 us (26%)
  between operations  16.7 us (12%)
  local copies, waits for them, and re-layouts  8.84 us (6%)
  other arithmetic  4.24 us (3%)
  starting transfers between devices  1.58 us (1%)
    all_gather x2, waiting for transfers between devices, per_device(): lax.all_gather(jnp.concatenate(parts, axis=1), ('row', 'rep'), axis=0, ti...  61.3 us
    pallas_call x2, Pallas kernels, page_mass_group(): pl.pallas_call(kernel, grid_spec=grid_spec, out_shape=jax.ShapeDtypeStruc...  37.7 us
    ppermute x1, waiting for transfers between devices, head_sum_scatter(): return own + lax.ppermute(other, 'head', [(0, 1), (1, 0)])  12.9 us
    unnamed x13, local copies, waits for them, and re-layouts  5.71 us
  transfers between devices with their start and end apart: 3, of which 3 were waited for; matrix products, arithmetic and copies ran while one was open for 3% of the time, Pallas kernels for 18%

profile of v10, /device:TPU:16, one launch (start us, length us, event | category | flops | bytes accessed | tf_op | source)
XLA Modules:
  0.0 143.2 jit_solution(7692604209321453714)
XLA Ops:
  6.5 1.1 slice_dynamic-update-slice_fusion.5
  7.6 0.9 slice_dynamic-update-slice_fusion.4
  8.5 0.9 slice_dynamic-update-slice_fusion.3
  9.4 0.9 slice_dynamic-update-slice_fusion.2
  10.4 1.0 slice_dynamic-update-slice_fusion.1
  11.4 1.0 slice_dynamic-update-slice_fusion
  12.4 0.0 copy-start.2
  12.4 0.9 copy-done.2
  13.3 0.0 all-gather.5.cloned.1.call-update
  13.3 0.0 all-gather.3.cloned.1.call-start
  13.3 0.7 pad_maximum_fusion
  14.1 0.0 all-gather.3.cloned.1.call-update
  14.1 0.7 fusion
  18.0 1.3 slice.41.q_ref
  19.3 0.8 slice.38.q_ref
  20.1 0.6 pad_add_fusion.nb_ref
  20.8 57.2 %all-gather.5.cloned.1.call-done.k_ref = f32[2048,768]{1,0:T(8,128)} async-done(((f32[256,768]{1,0:T(8,128)}), f32[2048,768]{1,0:T(8,128)}) %all-gather.5.cloned.1.call-update) | async-done | bytes 6291472 | tf_op jit(solution)/shard_map/all_gather | solution.py:188
  77.9 26.1 %shard_map.46.refs_0_ = f32[2048,128]{1,0:T(8,128)} custom-call(s32[2]{0:T(128)} %pad_add_fusion.nb_ref, f32[128,3072]{1,0:T(8,128)} %slice.41.q_ref, f32[2048,768]{1,0:T(8,128)} %all-gather.5.cloned.1.call-done.k_ref, s32[1,128]{1,0:T(1,128)} %bitcast.3), custom_call_target="tpu_custom_call" | custom-call | tf_op jit(solution)/shard_map/pallas_call | solution.py:157
  104.0 4.1 %all-gather.3.cloned.1.call-done.k_ref = f32[2048,256]{1,0:T(8,128)} async-done(((f32[256,256]{1,0:T(8,128)}), f32[2048,256]{1,0:T(8,128)}) %all-gather.3.cloned.1.call-update) | async-done | bytes 2097168 | tf_op jit(solution)/shard_map/all_gather | solution.py:188
  108.2 11.6 %shard_map.47 = f32[128,2048]{1,0:T(8,128)} custom-call(s32[2]{0:T(128)} %pad_add_fusion.nb_ref, f32[128,1024]{1,0:T(8,128)} %slice.38.q_ref, f32[2048,256]{1,0:T(8,128)} %all-gather.3.cloned.1.call-done.k_ref, s32[1,128]{1,0:T(1,128)} %bitcast.4, f32[2048,128]{1,0:T(8,128)} %shard_map.46.refs_0_), custom_call_target="tpu_custom_call" | custom-call | tf_op jit(solution)/shard_map/pallas_call | solution.py:157
  119.8 1.3 slice_select_fusion
  121.1 1.5 %collective-permute-start = (f32[128,1024]{1,0:T(8,128)S(1)}, f32[128,1024]{1,0:T(8,128)S(1)}, u32[]{:S(2)}, u32[]{:S(2)}) collective-permute-start(f32[128,1024]{1,0:T(8,128)S(1)} %slice_select_fusion), channel_id=1, source_target_pairs={{0,2},{2,0},{1,3},{3,1},{4,6},{6,4},{5,7},{7,5},{8,10},{10,8},{9,1... | collective-permute-start | bytes 1572872 | tf_op jit(solution)/shard_map/ppermute | solution.py:173
  122.6 12.9 %collective-permute-done = f32[128,1024]{1,0:T(8,128)S(1)} collective-permute-done((f32[128,1024]{1,0:T(8,128)S(1)}, f32[128,1024]{1,0:T(8,128)S(1)}, u32[]{:S(2)}, u32[]{:S(2)}) %collective-permute-start) | collective-permute-done | bytes 524320 | tf_op jit(solution)/shard_map/ppermute | solution.py:173
  135.5 0.9 select_add_fusion
  (7 shorter events, 0.0 us)
Async XLA Ops:
  6.5 7.6 %copy-start.3 = (s32[128]{0:T(128)S(1)}, s32[128]{0:T(128)}, u32[]{:S(2)}) copy-start(s32[128]{0:T(128)} %param.7) | copy-start | bytes 1540
  6.5 11.5 %copy-start.1 = (f32[128,4096]{1,0:T(8,128)S(1)}, f32[128,4096]{1,0:T(8,128)}, u32[]{:S(2)}) copy-start(f32[128,4096]{1,0:T(8,128)} %param.4) | copy-start | bytes 6291460
  6.5 71.4 %all-gather.5.cloned.1.call-start = ((), (), s32[]{:S(2)}) async-start(), calls=%async_computation.1 | async-start | bytes 7077888 | tf_op jit(solution)/shard_map/all_gather | solution.py:188
  12.4 0.9 copy-start.2
  13.3 94.9 %all-gather.3.cloned.1.call-start = ((), (), s32[]{:S(2)}) async-start(), calls=%async_computation | async-start | bytes 2359296 | tf_op jit(solution)/shard_map/all_gather | solution.py:188
  119.8 15.7 %copy-start = (f32[128,2048]{1,0:T(8,128)S(1)}, f32[128,2048]{1,0:T(8,128)}, u32[]{:S(2)}) copy-start(f32[128,2048]{1,0:T(8,128)} %shard_map.47) | copy-start | bytes 3145732
  121.1 14.4 %collective-permute-start = (f32[128,1024]{1,0:T(8,128)S(1)}, f32[128,1024]{1,0:T(8,128)S(1)}, u32[]{:S(2)}, u32[]{:S(2)}) collective-permute-start(f32[128,1024]{1,0:T(8,128)S(1)} %slice_select_fusion), channel_id=1, source_target_pairs={{0,2},{2,0},{1,3},{3,1},{4,6},{6,4},{5,7},{7,5},{8,10},{10,8},{9,1... | collective-permute-start | bytes 1572872 | tf_op jit(solution)/shard_map/ppermute | solution.py:173
Sparse Core Ops, SparseCore 0:
  13.4 64.4 all-gather.4
  79.5 28.5 all-gather.2

commit v11 on v10

--- a/solution.py
+++ b/solution.py
@@ -173,6 +173,13 @@
     return own + lax.ppermute(other, "head", [(0, 1), (1, 0)])
 
 
+def gather_blocks(block):
+    devices = lax.psum(1, ("row", "rep"))
+    copies = jnp.broadcast_to(block[None], (devices,) + block.shape)
+    got = lax.all_to_all(copies, ("row", "rep"), 0, 0, tiled=True)
+    return got.reshape(devices * block.shape[0], block.shape[1])
+
+
 def per_device(queries, key_max, key_min, limits, head_devices):
     local_pages = key_max.shape[0]
     kv_count = key_max.shape[1] // DH
@@ -185,7 +192,7 @@
         parts = []
         for kv in range(kv0, kv0 + size):
             parts += [key_max[:, kv * DH:(kv + 1) * DH], key_min[:, kv * DH:(kv + 1) * DH]]
-        keys = lax.all_gather(jnp.concatenate(parts, axis=1), ("row", "rep"), axis=0, tiled=True)
+        keys = gather_blocks(jnp.concatenate(parts, axis=1))
         cols = slice(kv0 * head_cols, (kv0 + size) * head_cols)
         acc = page_mass_group(nb, queries[:, cols], keys, limits, acc, last=g == len(sizes) - 1)
         kv0 += size

time: 144 us -> 235 us (1.63)
  waiting for transfers between devices: 74.2 us -> 158 us
  between operations: 16.7 us -> 3.27 us
  starting transfers between devices: 1.58 us -> 13.8 us
  local copies, waits for them, and re-layouts: 8.84 us -> 16.4 us
    all_to_all x0 -> x2, waiting for transfers between devices: none -> 146 us  [gather_blocks(): got = lax.all_to_all(copies, ('row', 'rep'), 0, 0, tiled=True)]
    all_gather x2 -> x0, waiting for transfers between devices: 61.3 us -> none  [per_device(): lax.all_gather(jnp.concatenate(parts, axis=1), ('row', 'rep'), axis=0, ti...]
    all_to_all x0 -> x2, starting transfers between devices: none -> 12.2 us  [gather_blocks(): got = lax.all_to_all(copies, ('row', 'rep'), 0, 0, tiled=True)]
    broadcast_in_dim x0 -> x2, local copies, waits for them, and re-layouts: none -> 4.73 us  [gather_blocks(): copies = jnp.broadcast_to(block[None], (devices,) + block.shape)]
    slice x2, local copies, waits for them, and re-layouts: 2.14 us -> 4.66 us  [per_device(): queries[:, cols]]
    unnamed x13 -> x11, local copies, waits for them, and re-layouts: 5.71 us -> 6 us
  transfers between devices with their start and end apart: 3 -> 3, of which waited for: 3 -> 3; matrix products, arithmetic and copies ran while one was open for 3% -> 3% of each run, Pallas kernels for 18% -> 11%
where the time goes in v11:
time: 235 us; the launch traced here: 233 us
  waiting for transfers between devices  158 us (67%)
  Pallas kernels  37.6 us (16%)
  local copies, waits for them, and re-layouts  16.4 us (7%)
  starting transfers between devices  13.8 us (6%)
  other arithmetic  3.54 us (2%)
  between operations  3.27 us (1%)
    all_to_all x2, waiting for transfers between devices, gather_blocks(): got = lax.all_to_all(copies, ('row', 'rep'), 0, 0, tiled=True)  146 us
    pallas_call x2, Pallas kernels, page_mass_group(): pl.pallas_call(kernel, grid_spec=grid_spec, out_shape=jax.ShapeDtypeStruc...  37.6 us
    all_to_all x2, starting transfers between devices, gather_blocks(): got = lax.all_to_all(copies, ('row', 'rep'), 0, 0, tiled=True)  12.2 us
    ppermute x1, waiting for transfers between devices, head_sum_scatter(): return own + lax.ppermute(other, 'head', [(0, 1), (1, 0)])  12.2 us
    unnamed x11, local copies, waits for them, and re-layouts  6 us
    broadcast_in_dim x2, local copies, waits for them, and re-layouts, gather_blocks(): copies = jnp.broadcast_to(block[None], (devices,) + block.shape)  4.73 us
  transfers between devices with their start and end apart: 3, of which 3 were waited for; matrix products, arithmetic and copies ran while one was open for 3% of the time, Pallas kernels for 11%

profile of v11, /device:TPU:16, one launch (start us, length us, event | category | flops | bytes accessed | tf_op | source)
XLA Modules:
  0.0 233.0 jit_solution(4864459717195593372)
XLA Ops:
  0.0 0.9 slice_dynamic-update-slice_fusion.5
  0.9 0.9 slice_dynamic-update-slice_fusion.4
  1.8 0.9 slice_dynamic-update-slice_fusion.3
  2.8 0.9 slice_dynamic-update-slice_fusion.2
  3.7 1.0 slice_dynamic-update-slice_fusion.1
  4.7 1.0 slice_dynamic-update-slice_fusion
  5.7 3.2 %broadcast_in_dim.5 = f32[8,256,768]{2,1,0:T(8,128)} broadcast(f32[256,768]{1,0:T(8,128)S(1)} %get-tuple-element.7), dimensions={1,2} | broadcast | bytes 7077888 | tf_op jit(solution)/shard_map/broadcast_in_dim | solution.py:178
  8.9 5.2 %all-to-all-start.1 = ((f32[8,256,768]{2,1,0:T(8,128)}), f32[8,256,768]{2,1,0:T(8,128)}, u32[]{:S(2)}, u32[]{:S(2)}) async-start(f32[8,256,768]{2,1,0:T(8,128)} %broadcast_in_dim.5), calls=%async_computation.1 | async-start | bytes 12582912 | tf_op jit(solution)/shard_map/all_to_all | solution.py:179
  14.1 135.7 %all-to-all-done.1 = f32[8,256,768]{2,1,0:T(8,128)} async-done(((f32[8,256,768]{2,1,0:T(8,128)}), f32[8,256,768]{2,1,0:T(8,128)}, u32[]{:S(2)}, u32[]{:S(2)}) %all-to-all-start.1) | async-done | bytes 6291488 | tf_op jit(solution)/shard_map/all_to_all | solution.py:179
  149.8 1.5 broadcast_in_dim.4
  151.3 7.0 %all-to-all-start = ((f32[8,256,256]{2,1,0:T(8,128)}), f32[8,256,256]{2,1,0:T(8,128)S(1)}, u32[]{:S(2)}, u32[]{:S(2)}) async-start(f32[8,256,256]{2,1,0:T(8,128)} %broadcast_in_dim.4), calls=%async_computation | async-start | bytes 4194304 | tf_op jit(solution)/shard_map/all_to_all | solution.py:179
  158.3 0.0 copy-done.2
  158.3 0.7 fusion
  162.2 2.8 %slice.41.q_ref = f32[128,3072]{1,0:T(8,128)} slice(f32[128,4096]{1,0:T(8,128)} %param.4), slice={[0:128], [0:3072]} | slice | bytes 3145728 | tf_op jit(solution)/shard_map/slice | solution.py:197
  165.0 1.9 slice.38.q_ref
  166.9 0.6 pad_add_fusion.nb_ref
  167.5 26.1 %shard_map.46.refs_0_ = f32[2048,128]{1,0:T(8,128)} custom-call(s32[2]{0:T(128)} %pad_add_fusion.nb_ref, f32[128,3072]{1,0:T(8,128)} %slice.41.q_ref, f32[2048,768]{1,0:T(8,128)} %bitcast.4.k_ref, s32[1,128]{1,0:T(1,128)} %bitcast.6), custom_call_target="tpu_custom_call" | custom-call | tf_op jit(solution)/shard_map/pallas_call | solution.py:157
  193.6 10.5 %all-to-all-done = f32[8,256,256]{2,1,0:T(8,128)S(1)} async-done(((f32[8,256,256]{2,1,0:T(8,128)}), f32[8,256,256]{2,1,0:T(8,128)S(1)}, u32[]{:S(2)}, u32[]{:S(2)}) %all-to-all-start) | async-done | bytes 2097184 | tf_op jit(solution)/shard_map/all_to_all | solution.py:179
  204.1 1.3 copy-done.1
  205.5 11.5 %shard_map.47 = f32[128,2048]{1,0:T(8,128)} custom-call(s32[2]{0:T(128)} %pad_add_fusion.nb_ref, f32[128,1024]{1,0:T(8,128)} %slice.38.q_ref, f32[2048,256]{1,0:T(8,128)} %bitcast.5, s32[1,128]{1,0:T(1,128)} %bitcast.7, f32[2048,128]{1,0:T(8,128)} %shard_map.46.refs_0_), custom_call_target="tpu_custom_call" | custom-call | tf_op jit(solution)/shard_map/pallas_call | solution.py:157
  217.0 1.3 slice_select_fusion
  218.3 1.6 collective-permute-start
  219.9 12.2 %collective-permute-done = f32[128,1024]{1,0:T(8,128)S(1)} collective-permute-done((f32[128,1024]{1,0:T(8,128)S(1)}, f32[128,1024]{1,0:T(8,128)S(1)}, u32[]{:S(2)}, u32[]{:S(2)}) %collective-permute-start) | collective-permute-done | bytes 524320 | tf_op jit(solution)/shard_map/ppermute | solution.py:173
  232.1 0.9 select_add_fusion
  (5 shorter events, 0.0 us)
Async XLA Ops:
  8.9 140.9 %all-to-all-start.1 = ((f32[8,256,768]{2,1,0:T(8,128)}), f32[8,256,768]{2,1,0:T(8,128)}, u32[]{:S(2)}, u32[]{:S(2)}) async-start(f32[8,256,768]{2,1,0:T(8,128)} %broadcast_in_dim.5), calls=%async_computation.1 | async-start | bytes 12582912 | tf_op jit(solution)/shard_map/all_to_all | solution.py:179
  151.3 7.0 %copy-start.2 = (s32[128]{0:T(128)S(1)}, s32[128]{0:T(128)}, u32[]{:S(2)}) copy-start(s32[128]{0:T(128)} %param.7) | copy-start | bytes 1540
  151.3 52.8 %all-to-all-start = ((f32[8,256,256]{2,1,0:T(8,128)}), f32[8,256,256]{2,1,0:T(8,128)S(1)}, u32[]{:S(2)}, u32[]{:S(2)}) async-start(f32[8,256,256]{2,1,0:T(8,128)} %broadcast_in_dim.4), calls=%async_computation | async-start | bytes 4194304 | tf_op jit(solution)/shard_map/all_to_all | solution.py:179
  204.1 1.3 copy-start.1
  217.0 15.2 %copy-start = (f32[128,2048]{1,0:T(8,128)S(1)}, f32[128,2048]{1,0:T(8,128)}, u32[]{:S(2)}) copy-start(f32[128,2048]{1,0:T(8,128)} %shard_map.47) | copy-start | bytes 3145732
  218.3 13.8 %collective-permute-start = (f32[128,1024]{1,0:T(8,128)S(1)}, f32[128,1024]{1,0:T(8,128)S(1)}, u32[]{:S(2)}, u32[]{:S(2)}) collective-permute-start(f32[128,1024]{1,0:T(8,128)S(1)} %slice_select_fusion), channel_id=1, source_target_pairs={{0,2},{2,0},{1,3},{3,1},{4,6},{6,4},{5,7},{7,5},{8,10},{10,8},{9,1... | collective-permute-start | bytes 1572872 | tf_op jit(solution)/shard_map/ppermute | solution.py:173

commit v12 on v10

--- a/solution.py
+++ b/solution.py
@@ -11,6 +11,7 @@
 DH = 128
 CHUNK = 256
 MM_CHUNK = 1024
+HEAD_SUM_PIECES = 4
 
 
 def _split(x):
@@ -170,7 +171,9 @@
     first_half = lax.axis_index("head") == 0
     own = jnp.where(first_half, acc[:, :half], acc[:, half:])
     other = jnp.where(first_half, acc[:, half:], acc[:, :half])
-    return own + lax.ppermute(other, "head", [(0, 1), (1, 0)])
+    pieces = jnp.split(other, HEAD_SUM_PIECES, axis=0)
+    sent = [lax.ppermute(p, "head", [(0, 1), (1, 0)]) for p in pieces]
+    return own + jnp.concatenate(sent, axis=0)
 
 
 def per_device(queries, key_max, key_min, limits, head_devices):

time: 144 us -> 144 us (level)
  starting transfers between devices: 1.58 us -> 4.16 us
  waiting for transfers between devices: 74.2 us -> 71.7 us
    ppermute x1 -> x4, waiting for transfers between devices: 12.9 us -> 10.3 us  [head_sum_scatter(): sent = [lax.ppermute(p, 'head', [(0, 1), (1, 0)]) for p in pieces]]
    ppermute x1 -> x4, starting transfers between devices: 1.53 us -> 4.12 us  [head_sum_scatter(): sent = [lax.ppermute(p, 'head', [(0, 1), (1, 0)]) for p in pieces]]
  transfers between devices with their start and end apart: 3 -> 6, of which waited for: 3 -> 6; matrix products, arithmetic and copies ran while one was open for 3% -> 3% of each run, Pallas kernels for 18% -> 18%
where the time goes in v12:
time: 144 us; the launch traced here: 143 us
  waiting for transfers between devices  71.7 us (50%)
  Pallas kernels  37.7 us (26%)
  between operations  16.6 us (12%)
  local copies, waits for them, and re-layouts  8.87 us (6%)
  other arithmetic  4.24 us (3%)
  starting transfers between devices  4.16 us (3%)
    all_gather x2, waiting for transfers between devices, per_device(): lax.all_gather(jnp.concatenate(parts, axis=1), ('row', 'rep'), axis=0, ti...  61.4 us
    pallas_call x2, Pallas kernels, page_mass_group(): pl.pallas_call(kernel, grid_spec=grid_spec, out_shape=jax.ShapeDtypeStruc...  37.7 us
    ppermute x4, waiting for transfers between devices, head_sum_scatter(): sent = [lax.ppermute(p, 'head', [(0, 1), (1, 0)]) for p in pieces]  10.3 us
    unnamed x13, local copies, waits for them, and re-layouts  5.71 us
    ppermute x4, starting transfers between devices, head_sum_scatter(): sent = [lax.ppermute(p, 'head', [(0, 1), (1, 0)]) for p in pieces]  4.12 us
  transfers between devices with their start and end apart: 6, of which 6 were waited for; matrix products, arithmetic and copies ran while one was open for 3% of the time, Pallas kernels for 18%

profile of v12, /device:TPU:16, one launch (start us, length us, event | category | flops | bytes accessed | tf_op | source)
XLA Modules:
  0.0 143.3 jit_solution(16668146936906378119)
XLA Ops:
  6.5 1.1 slice_dynamic-update-slice_fusion.5
  7.6 0.9 slice_dynamic-update-slice_fusion.4
  8.5 0.9 slice_dynamic-update-slice_fusion.3
  9.4 0.9 slice_dynamic-update-slice_fusion.2
  10.4 1.0 slice_dynamic-update-slice_fusion.1
  11.4 1.0 slice_dynamic-update-slice_fusion
  12.4 0.9 copy-done.2
  13.3 0.7 pad_maximum_fusion
  14.1 0.6 fusion
  17.9 1.3 slice.41.q_ref
  19.2 0.8 slice.38.q_ref
  20.0 0.7 pad_add_fusion.nb_ref
  20.7 57.3 %all-gather.5.cloned.1.call-done.k_ref = f32[2048,768]{1,0:T(8,128)} async-done(((f32[256,768]{1,0:T(8,128)}), f32[2048,768]{1,0:T(8,128)}) %all-gather.5.cloned.1.call-update) | async-done | bytes 6291472 | tf_op jit(solution)/shard_map/all_gather | solution.py:191
  77.9 26.1 %shard_map.46.refs_0_ = f32[2048,128]{1,0:T(8,128)} custom-call(s32[2]{0:T(128)} %pad_add_fusion.nb_ref, f32[128,3072]{1,0:T(8,128)} %slice.41.q_ref, f32[2048,768]{1,0:T(8,128)} %all-gather.5.cloned.1.call-done.k_ref, s32[1,128]{1,0:T(1,128)} %bitcast.3), custom_call_target="tpu_custom_call" | custom-call | tf_op jit(solution)/shard_map/pallas_call | solution.py:158
  104.0 4.1 %all-gather.3.cloned.1.call-done.k_ref = f32[2048,256]{1,0:T(8,128)} async-done(((f32[256,256]{1,0:T(8,128)}), f32[2048,256]{1,0:T(8,128)}) %all-gather.3.cloned.1.call-update) | async-done | bytes 2097168 | tf_op jit(solution)/shard_map/all_gather | solution.py:191
  108.2 11.6 %shard_map.47 = f32[128,2048]{1,0:T(8,128)} custom-call(s32[2]{0:T(128)} %pad_add_fusion.nb_ref, f32[128,1024]{1,0:T(8,128)} %slice.38.q_ref, f32[2048,256]{1,0:T(8,128)} %all-gather.3.cloned.1.call-done.k_ref, s32[1,128]{1,0:T(1,128)} %bitcast.4, f32[2048,128]{1,0:T(8,128)} %shard_map.46.refs_0_), custom_call_target="tpu_custom_call" | custom-call | tf_op jit(solution)/shard_map/pallas_call | solution.py:158
  119.8 1.3 slice_select_fusion
  121.2 1.5 %collective-permute-start = (f32[32,1024]{1,0:T(8,128)S(1)}, f32[32,1024]{1,0:T(8,128)S(1)}, u32[]{:S(2)}, u32[]{:S(2)}) collective-permute-start(f32[32,1024]{1,0:T(8,128)S(1)} %get-tuple-element.7), channel_id=1, source_target_pairs={{0,2},{2,0},{1,3},{3,1},{4,6},{6,4},{5,7},{7,5},{8,10},{10,8},{9,1... | collective-permute-start | bytes 393224 | tf_op jit(solution)/shard_map/ppermute | solution.py:175
  123.3 1.5 %collective-permute-start.2 = (f32[32,1024]{1,0:T(8,128)S(1)}, f32[32,1024]{1,0:T(8,128)S(1)}, u32[]{:S(2)}, u32[]{:S(2)}) collective-permute-start(f32[32,1024]{1,0:T(8,128)S(1)} %get-tuple-element.9), channel_id=1, source_target_pairs={{0,2},{2,0},{1,3},{3,1},{4,6},{6,4},{5,7},{7,5},{8,10},{10,8},{9,1... | collective-permute-start | bytes 393224 | tf_op jit(solution)/shard_map/ppermute | solution.py:175
  125.3 2.2 %collective-permute-done = f32[32,1024]{1,0:T(8,128)S(1)} collective-permute-done((f32[32,1024]{1,0:T(8,128)S(1)}, f32[32,1024]{1,0:T(8,128)S(1)}, u32[]{:S(2)}, u32[]{:S(2)}) %collective-permute-start) | collective-permute-done | bytes 131104 | tf_op jit(solution)/shard_map/ppermute | solution.py:175
  127.5 2.8 %collective-permute-done.1 = f32[32,1024]{1,0:T(8,128)S(1)} collective-permute-done((f32[32,1024]{1,0:T(8,128)S(1)}, f32[32,1024]{1,0:T(8,128)S(1)}, u32[]{:S(2)}, u32[]{:S(2)}) %collective-permute-start.1) | collective-permute-done | bytes 131104 | tf_op jit(solution)/shard_map/ppermute | solution.py:175
  130.3 2.8 %collective-permute-done.2 = f32[32,1024]{1,0:T(8,128)S(1)} collective-permute-done((f32[32,1024]{1,0:T(8,128)S(1)}, f32[32,1024]{1,0:T(8,128)S(1)}, u32[]{:S(2)}, u32[]{:S(2)}) %collective-permute-start.2) | collective-permute-done | bytes 131104 | tf_op jit(solution)/shard_map/ppermute | solution.py:175
  133.1 2.4 %collective-permute-done.3 = f32[32,1024]{1,0:T(8,128)S(1)} collective-permute-done((f32[32,1024]{1,0:T(8,128)S(1)}, f32[32,1024]{1,0:T(8,128)S(1)}, u32[]{:S(2)}, u32[]{:S(2)}) %collective-permute-start.3) | collective-permute-done | bytes 131104 | tf_op jit(solution)/shard_map/ppermute | solution.py:175
  135.6 0.9 maximum_add_fusion
  (14 shorter events, 1.2 us)
Async XLA Ops:
  6.5 7.5 %copy-start.3 = (s32[128]{0:T(128)S(1)}, s32[128]{0:T(128)}, u32[]{:S(2)}) copy-start(s32[128]{0:T(128)} %param.7) | copy-start | bytes 1540
  6.5 11.3 %copy-start.1 = (f32[128,4096]{1,0:T(8,128)S(1)}, f32[128,4096]{1,0:T(8,128)}, u32[]{:S(2)}) copy-start(f32[128,4096]{1,0:T(8,128)} %param.4) | copy-start | bytes 6291460
  6.5 71.4 %all-gather.5.cloned.1.call-start = ((), (), s32[]{:S(2)}) async-start(), calls=%async_computation.1 | async-start | bytes 7077888 | tf_op jit(solution)/shard_map/all_gather | solution.py:191
  12.4 0.9 copy-start.2
  13.3 94.9 %all-gather.3.cloned.1.call-start = ((), (), s32[]{:S(2)}) async-start(), calls=%async_computation | async-start | bytes 2359296 | tf_op jit(solution)/shard_map/all_gather | solution.py:191
  119.8 15.8 %copy-start = (f32[128,2048]{1,0:T(8,128)S(1)}, f32[128,2048]{1,0:T(8,128)}, u32[]{:S(2)}) copy-start(f32[128,2048]{1,0:T(8,128)} %shard_map.47) | copy-start | bytes 3145732
  121.2 6.4 %collective-permute-start = (f32[32,1024]{1,0:T(8,128)S(1)}, f32[32,1024]{1,0:T(8,128)S(1)}, u32[]{:S(2)}, u32[]{:S(2)}) collective-permute-start(f32[32,1024]{1,0:T(8,128)S(1)} %get-tuple-element.7), channel_id=1, source_target_pairs={{0,2},{2,0},{1,3},{3,1},{4,6},{6,4},{5,7},{7,5},{8,10},{10,8},{9,1... | collective-permute-start | bytes 393224 | tf_op jit(solution)/shard_map/ppermute | solution.py:175
  122.7 7.6 %collective-permute-start.1 = (f32[32,1024]{1,0:T(8,128)S(1)}, f32[32,1024]{1,0:T(8,128)S(1)}, u32[]{:S(2)}, u32[]{:S(2)}) collective-permute-start(f32[32,1024]{1,0:T(8,128)S(1)} %get-tuple-element.10), channel_id=1, source_target_pairs={{0,2},{2,0},{1,3},{3,1},{4,6},{6,4},{5,7},{7,5},{8,10},{10,8},{9,1... | collective-permute-start | bytes 393224 | tf_op jit(solution)/shard_map/ppermute | solution.py:175
  123.3 9.9 %collective-permute-start.2 = (f32[32,1024]{1,0:T(8,128)S(1)}, f32[32,1024]{1,0:T(8,128)S(1)}, u32[]{:S(2)}, u32[]{:S(2)}) collective-permute-start(f32[32,1024]{1,0:T(8,128)S(1)} %get-tuple-element.9), channel_id=1, source_target_pairs={{0,2},{2,0},{1,3},{3,1},{4,6},{6,4},{5,7},{7,5},{8,10},{10,8},{9,1... | collective-permute-start | bytes 393224 | tf_op jit(solution)/shard_map/ppermute | solution.py:175
  124.7 10.8 %collective-permute-start.3 = (f32[32,1024]{1,0:T(8,128)S(1)}, f32[32,1024]{1,0:T(8,128)S(1)}, u32[]{:S(2)}, u32[]{:S(2)}) collective-permute-start(f32[32,1024]{1,0:T(8,128)S(1)} %get-tuple-element.8), channel_id=1, source_target_pairs={{0,2},{2,0},{1,3},{3,1},{4,6},{6,4},{5,7},{7,5},{8,10},{10,8},{9,1... | collective-permute-start | bytes 393224 | tf_op jit(solution)/shard_map/ppermute | solution.py:175
Sparse Core Ops, SparseCore 0:
  13.4 64.4 all-gather.4
  79.5 28.5 all-gather.2

commit v13 on v10

--- a/solution.py
+++ b/solution.py
@@ -20,7 +20,7 @@
 
 
 def _mass_kernel(nb_ref, q_ref, k_ref, lim_ref, *refs, chunk_count, score_scale, first, last,
-                 pairs_per_kv):
+                 pairs_per_kv, block_of):
     if first:
         out_ref, kcat_ref, s_ref, acc_ref, tops_ref = refs
     else:
@@ -41,7 +41,7 @@
     @pl.when(hp % pairs_per_kv == 0)
     def _():
         for c in range(chunk_count):
-            @pl.when(c < nb)
+            @pl.when(block_of[c] < nb)
             def _():
                 hi, lo = _split(k_ref[c * CHUNK:(c + 1) * CHUNK, :])
                 kcat_ref[c * CHUNK:(c + 1) * CHUNK, :] = jnp.concatenate([hi, hi, lo], axis=1)
@@ -64,7 +64,7 @@
     mm_pages = min(MM_CHUNK, chunk_count * CHUNK)
     per_mm = mm_pages // CHUNK
     for mc in range(chunk_count * CHUNK // mm_pages):
-        @pl.when(mc * mm_pages < nb * CHUNK)
+        @pl.when(min(block_of[mc * per_mm:(mc + 1) * per_mm]) < nb)
         def _():
             s = jnp.dot(kcat_ref[mc * mm_pages:(mc + 1) * mm_pages, :], wcat,
                         preferred_element_type=jnp.float32)
@@ -83,11 +83,11 @@
 
         def masked_chunk(top, c=c):
             s = s_ref[c * CHUNK:(c + 1) * CHUNK, :]
-            s = jnp.where(page_in_chunk <= lim2 - c * CHUNK, s, -1e30)
+            s = jnp.where(page_in_chunk <= lim2 - block_of[c] * CHUNK, s, -1e30)
             s_ref[c * CHUNK:(c + 1) * CHUNK, :] = s
             return jnp.maximum(top, vreg_fold(s, jnp.max))
 
-        branch = jnp.where(c < nb, jnp.where(c < nfull, 1, 2), 0)
+        branch = jnp.where(block_of[c] < nb, jnp.where(block_of[c] < nfull, 1, 2), 0)
         top = lax.switch(branch, [keep, open_chunk, masked_chunk], top)
     top = jnp.max(top, axis=0, keepdims=True)
 
@@ -97,13 +97,13 @@
             e = jnp.exp2(s_ref[c * CHUNK:(c + 1) * CHUNK, :] - top)
             s_ref[c * CHUNK:(c + 1) * CHUNK, :] = e
             return total + vreg_fold(e, jnp.sum)
-        total = lax.cond(c < nb, pass_exp, lambda t: t, total)
+        total = lax.cond(block_of[c] < nb, pass_exp, lambda t: t, total)
     inv = 1.0 / jnp.sum(total, axis=0, keepdims=True)
     inv_a = inv[:, :row_count]
     inv_b = inv[:, row_count:]
 
     for c in range(chunk_count):
-        @pl.when(c < nb)
+        @pl.when(block_of[c] < nb)
         def _():
             e = s_ref[c * CHUNK:(c + 1) * CHUNK, :]
             acc_ref[c * CHUNK:(c + 1) * CHUNK, :] += (
@@ -113,12 +113,12 @@
     def _():
         for c in range(chunk_count):
             if last:
-                out_ref[:, c * CHUNK:(c + 1) * CHUNK] = acc_ref[c * CHUNK:(c + 1) * CHUNK, :].T
+                out_ref[:, block_of[c] * CHUNK:(block_of[c] + 1) * CHUNK] = acc_ref[c * CHUNK:(c + 1) * CHUNK, :].T
             else:
                 out_ref[c * CHUNK:(c + 1) * CHUNK, :] = acc_ref[c * CHUNK:(c + 1) * CHUNK, :]
 
 
-def page_mass_group(nb, queries, keys, limits, acc, last):
+def page_mass_group(nb, queries, keys, limits, acc, last, block_of):
     row_count = queries.shape[0]
     pair_count = queries.shape[1] // (2 * DH)
     pairs_per_kv = pair_count // (keys.shape[1] // (2 * DH))
@@ -127,7 +127,8 @@
     first = acc is None
     kernel = functools.partial(
         _mass_kernel, chunk_count=chunk_count, score_scale=math.log2(math.e) / math.sqrt(DH),
-        first=first, last=last, pairs_per_kv=pairs_per_kv)
+        first=first, last=last, pairs_per_kv=pairs_per_kv,
+        block_of=block_of)
     in_specs = [
         pl.BlockSpec((row_count, 2 * DH), lambda hp, nb: (0, hp)),
         pl.BlockSpec((page_count, 2 * DH), lambda hp, nb: (0, hp // pairs_per_kv)),
@@ -173,10 +174,12 @@
     return own + lax.ppermute(other, "head", [(0, 1), (1, 0)])
 
 
-def per_device(queries, key_max, key_min, limits, head_devices):
+def per_device(queries, key_max, key_min, limits, head_devices, row_devices, rep_devices):
     local_pages = key_max.shape[0]
     kv_count = key_max.shape[1] // DH
     head_cols = queries.shape[1] // kv_count
+    assert local_pages == CHUNK
+    block_of = tuple(z * rep_devices + r for r in range(rep_devices) for z in range(row_devices))
     sizes = [kv_count - 1, 1] if kv_count > 1 else [kv_count]
     nb = jnp.stack([jnp.max(limits) // CHUNK + 1, (jnp.min(limits) + 1) // CHUNK]).astype(jnp.int32)
     acc = None
@@ -185,9 +188,11 @@
         parts = []
         for kv in range(kv0, kv0 + size):
             parts += [key_max[:, kv * DH:(kv + 1) * DH], key_min[:, kv * DH:(kv + 1) * DH]]
-        keys = lax.all_gather(jnp.concatenate(parts, axis=1), ("row", "rep"), axis=0, tiled=True)
+        keys = lax.all_gather(jnp.concatenate(parts, axis=1), "row", axis=0, tiled=True)
+        keys = lax.all_gather(keys, "rep", axis=0, tiled=True)
         cols = slice(kv0 * head_cols, (kv0 + size) * head_cols)
-        acc = page_mass_group(nb, queries[:, cols], keys, limits, acc, last=g == len(sizes) - 1)
+        acc = page_mass_group(nb, queries[:, cols], keys, limits, acc,
+                              last=g == len(sizes) - 1, block_of=block_of)
         kv0 += size
     return head_sum_scatter(acc, head_devices)
 
@@ -200,7 +205,8 @@
         P(("grp", "row", "rep")),
     )
     return jax.shard_map(
-        functools.partial(per_device, head_devices=mesh.shape["head"]),
+        functools.partial(per_device, head_devices=mesh.shape["head"], row_devices=mesh.shape["row"],
+            rep_devices=mesh.shape["rep"]),
         mesh=mesh,
         in_specs=placed,
         out_specs=P(("grp", "row", "rep"), "head"),

time: 144 us -> 188 us (1.31); the launches traced: 143 us -> 185 us
  waiting for transfers between devices: 74.2 us -> 116 us
    all_gather x2 -> x4, waiting for transfers between devices: 61.3 us -> 103 us  [the longest x2 91.5 us: per_device(): lax.all_gather(jnp.concatenate(parts, axis=1), 'row', axis=0, tiled=True)]
  transfers between devices with their start and end apart: 3 -> 5, of which waited for: 3 -> 4; matrix products, arithmetic and copies ran while one was open for 3% -> 2% of each run, Pallas kernels for 18% -> 14%
where the time goes in v13:
time: 188 us; the launch traced here: 185 us
  waiting for transfers between devices  116 us (62%)
  Pallas kernels  37.7 us (20%)
  between operations  16.5 us (9%)
  local copies, waits for them, and re-layouts  8.73 us (5%)
  other arithmetic  4.26 us (2%)
    all_gather x2, waiting for transfers between devices, per_device(): lax.all_gather(jnp.concatenate(parts, axis=1), 'row', axis=0, tiled=True)  91.5 us
    pallas_call x2, Pallas kernels, page_mass_group(): pl.pallas_call(kernel, grid_spec=grid_spec, out_shape=jax.ShapeDtypeStruc...  37.7 us
    ppermute x1, waiting for transfers between devices, head_sum_scatter(): return own + lax.ppermute(other, 'head', [(0, 1), (1, 0)])  13 us
    all_gather x2, waiting for transfers between devices, per_device(): keys = lax.all_gather(keys, 'rep', axis=0, tiled=True)  11.8 us
    unnamed x13, local copies, waits for them, and re-layouts  5.56 us
  transfers between devices with their start and end apart: 5, of which 4 were waited for; matrix products, arithmetic and copies ran while one was open for 2% of the time, Pallas kernels for 14%

profile of v13, /device:TPU:16, one launch (start us, length us, event | category | flops | bytes accessed | tf_op | source)
XLA Modules:
  0.0 185.2 jit_solution(7640373856191434683)
XLA Ops:
  6.5 0.9 slice_dynamic-update-slice_fusion.5
  7.5 0.9 slice_dynamic-update-slice_fusion.4
  8.4 0.9 slice_dynamic-update-slice_fusion.3
  9.3 0.9 slice_dynamic-update-slice_fusion.2
  10.2 1.0 slice_dynamic-update-slice_fusion.1
  11.2 1.0 slice_dynamic-update-slice_fusion
  12.2 0.9 copy-done.2
  13.1 0.0 all-gather.5.cloned.1.call-start
  13.2 0.7 pad_maximum_fusion
  13.9 0.0 all-gather.11.cloned.1.call-start
  14.0 62.5 %all-gather.9.cloned.1.call-done = f32[1024,768]{1,0:T(8,128)} async-done(((f32[256,768]{1,0:T(8,128)}), f32[1024,768]{1,0:T(8,128)}) %all-gather.9.cloned.1.call-update) | async-done | bytes 3145744 | tf_op jit(solution)/shard_map/all_gather | solution.py:191
  76.5 0.0 all-gather.7.cloned.1.call-start
  76.6 28.9 %all-gather.5.cloned.1.call-done = f32[1024,256]{1,0:T(8,128)} async-done(((f32[256,256]{1,0:T(8,128)}), f32[1024,256]{1,0:T(8,128)}) %all-gather.5.cloned.1.call-update) | async-done | bytes 1048592 | tf_op jit(solution)/shard_map/all_gather | solution.py:191
  105.6 0.7 fusion
  109.6 1.3 slice.41.q_ref
  110.9 0.8 slice.38.q_ref
  111.8 0.6 pad_add_fusion.nb_ref
  112.4 11.8 %all-gather.11.cloned.1.call-done.k_ref = f32[2048,768]{1,0:T(8,128)} async-done(((f32[1024,768]{1,0:T(8,128)}), f32[2048,768]{1,0:T(8,128)}) %all-gather.11.cloned.1.call-update) | async-done | bytes 6291472 | tf_op jit(solution)/shard_map/all_gather | solution.py:192
  124.1 26.1 %shard_map.46.refs_0_ = f32[2048,128]{1,0:T(8,128)} custom-call(s32[2]{0:T(128)} %pad_add_fusion.nb_ref, f32[128,3072]{1,0:T(8,128)} %slice.41.q_ref, f32[2048,768]{1,0:T(8,128)} %all-gather.11.cloned.1.call-done.k_ref, s32[1,128]{1,0:T(1,128)} %bitcast.3), custom_call_target="tpu_custom_call" | custom-call | tf_op jit(solution)/shard_map/pallas_call | solution.py:158
  150.3 11.5 %shard_map.47 = f32[128,2048]{1,0:T(8,128)} custom-call(s32[2]{0:T(128)} %pad_add_fusion.nb_ref, f32[128,1024]{1,0:T(8,128)} %slice.38.q_ref, f32[2048,256]{1,0:T(8,128)} %all-gather.7.cloned.1.call-done.k_ref, s32[1,128]{1,0:T(1,128)} %bitcast.4, f32[2048,128]{1,0:T(8,128)} %shard_map.46.refs_0_), custom_call_target="tpu_custom_call" | custom-call | tf_op jit(solution)/shard_map/pallas_call | solution.py:158
  161.8 1.3 slice_select_fusion
  163.2 1.5 collective-permute-start
  164.7 13.0 %collective-permute-done = f32[128,1024]{1,0:T(8,128)S(1)} collective-permute-done((f32[128,1024]{1,0:T(8,128)S(1)}, f32[128,1024]{1,0:T(8,128)S(1)}, u32[]{:S(2)}, u32[]{:S(2)}) %collective-permute-start) | collective-permute-done | bytes 524320 | tf_op jit(solution)/shard_map/ppermute | solution.py:174
  177.7 0.9 select_add_fusion
  (13 shorter events, 0.1 us)
Async XLA Ops:
  6.5 70.0 %all-gather.9.cloned.1.call-start = ((), (), s32[]{:S(2)}) async-start(), calls=%async_computation.2 | async-start | bytes 3932160 | tf_op jit(solution)/shard_map/all_gather | solution.py:191
  12.2 0.9 copy-start.2
  13.1 92.4 %all-gather.5.cloned.1.call-start = ((), (), s32[]{:S(2)}) async-start(), calls=%async_computation | async-start | bytes 1310720 | tf_op jit(solution)/shard_map/all_gather | solution.py:191
  13.9 110.2 %all-gather.11.cloned.1.call-start = ((), (), s32[]{:S(2)}) async-start(), calls=%async_computation.3 | async-start | bytes 9437184 | tf_op jit(solution)/shard_map/all_gather | solution.py:192
  76.5 29.1 %copy-start.3 = (s32[128]{0:T(128)S(1)}, s32[128]{0:T(128)}, u32[]{:S(2)}) copy-start(s32[128]{0:T(128)} %param.7) | copy-start | bytes 1540
  76.5 33.1 %copy-start.1 = (f32[128,4096]{1,0:T(8,128)S(1)}, f32[128,4096]{1,0:T(8,128)}, u32[]{:S(2)}) copy-start(f32[128,4096]{1,0:T(8,128)} %param.4) | copy-start | bytes 6291460
  76.5 73.7 %all-gather.7.cloned.1.call-start = ((), (), s32[]{:S(2)}) async-start(), calls=%async_computation.1 | async-start | bytes 3145728 | tf_op jit(solution)/shard_map/all_gather | solution.py:192
  161.8 15.9 %copy-start = (f32[128,2048]{1,0:T(8,128)S(1)}, f32[128,2048]{1,0:T(8,128)}, u32[]{:S(2)}) copy-start(f32[128,2048]{1,0:T(8,128)} %shard_map.47) | copy-start | bytes 3145732
  163.2 14.6 %collective-permute-start = (f32[128,1024]{1,0:T(8,128)S(1)}, f32[128,1024]{1,0:T(8,128)S(1)}, u32[]{:S(2)}, u32[]{:S(2)}) collective-permute-start(f32[128,1024]{1,0:T(8,128)S(1)} %slice_select_fusion), channel_id=1, source_target_pairs={{0,2},{2,0},{1,3},{3,1},{4,6},{6,4},{5,7},{7,5},{8,10},{10,8},{9,1... | collective-permute-start | bytes 1572872 | tf_op jit(solution)/shard_map/ppermute | solution.py:174
Sparse Core Ops, SparseCore 0:
  13.3 63.2 all-gather.8
  78.1 27.4 all-gather.4
  107.1 16.9 all-gather.10
  125.5 11.7 all-gather.6

commit v14 on v9

v14 whole, which is shorter than its diff:
```python
import functools
import math

import jax
import jax.numpy as jnp
from jax import lax
from jax.experimental import pallas as pl
from jax.experimental.pallas import tpu as pltpu
from jax.sharding import PartitionSpec as P

DH = 128
CHUNK = 256
MM_CHUNK = 1024


def _split(x):
    hi = x.astype(jnp.bfloat16)
    lo = (x - hi.astype(jnp.float32)).astype(jnp.bfloat16)
    return hi, lo


def _mass_kernel(q_ref, k_ref, lim_ref, *refs, chunk_count, score_scale, first, last,
                 pairs_per_kv, pair_count):
    if first:
        out_ref, kcat_ref, s0_ref, s1_ref, top_ref, acc_ref = refs
    else:
        acc_in_ref, out_ref, kcat_ref, s0_ref, s1_ref, top_ref, acc_ref = refs
    j = pl.program_id(0)
    row_count = q_ref.shape[0]
    lanes = 2 * row_count
    mm_pages = min(MM_CHUNK, chunk_count * CHUNK)
    per_mm = mm_pages // CHUNK

    @pl.when(j == 0)
    def _():
        if first:
            acc_ref[...] = jnp.zeros_like(acc_ref)
        else:
            acc_ref[...] = acc_in_ref[...]

    @pl.when((j < pair_count) & (j % pairs_per_kv == 0))
    def _():
        for c in range(chunk_count):
            hi, lo = _split(k_ref[c * CHUNK:(c + 1) * CHUNK, :])
            kcat_ref[c * CHUNK:(c + 1) * CHUNK, :] = jnp.concatenate([hi, hi, lo], axis=1)

    def vreg_fold(v, op):
        return op(v.reshape(CHUNK // 8, 8, lanes), axis=0)

    def step(new, old):
        top_old = None
        total = jnp.zeros((8, lanes), jnp.float32)
        if old is not None:
            s_old, slot_old = old
            top_old = jnp.max(top_ref[slot_old], axis=0, keepdims=True)
        if new is not None:
            s_new, slot_new = new
            q = q_ref[...]
            xs = []
            for h in range(2):
                qh = q[:, h * DH:(h + 1) * DH]
                xs.append(jnp.concatenate([jnp.maximum(qh, 0.0), jnp.minimum(qh, 0.0)], axis=1).T)
            w = jnp.concatenate(xs, axis=1) * score_scale
            whi, wlo = _split(w)
            wcat = jnp.concatenate([whi, wlo, whi], axis=0)
            lim = lim_ref[...]
            lim2 = jnp.concatenate([lim, lim], axis=1)
            page_in_chunk = lax.broadcasted_iota(jnp.int32, (CHUNK, lanes), 0)
            top = jnp.full((8, lanes), -jnp.inf, jnp.float32)
        for mc in range(chunk_count // per_mm):
            if new is not None:
                s = jnp.dot(kcat_ref[mc * mm_pages:(mc + 1) * mm_pages, :], wcat,
                            preferred_element_type=jnp.float32)
            for i in range(per_mm):
                c = mc * per_mm + i
                if new is not None:
                    sc = jnp.where(page_in_chunk <= lim2 - c * CHUNK,
                                   s[i * CHUNK:(i + 1) * CHUNK, :], -1e30)
                    s_new[c * CHUNK:(c + 1) * CHUNK, :] = sc
                    top = jnp.maximum(top, vreg_fold(sc, jnp.max))
                if old is not None:
                    e = jnp.exp2(s_old[c * CHUNK:(c + 1) * CHUNK, :] - top_old)
                    s_old[c * CHUNK:(c + 1) * CHUNK, :] = e
                    total = total + vreg_fold(e, jnp.sum)
        if new is not None:
            top_ref[slot_new] = top
        if old is not None:
            inv = 1.0 / jnp.sum(total, axis=0, keepdims=True)
            inv_a = inv[:, :row_count]
            inv_b = inv[:, row_count:]
            for c in range(chunk_count):
                e = s_old[c * CHUNK:(c + 1) * CHUNK, :]
                acc_ref[c * CHUNK:(c + 1) * CHUNK, :] += (
                    e[:, :row_count] * inv_a + e[:, row_count:] * inv_b)

    middle = (j >= 1) & (j < pair_count)

    @pl.when(j == 0)
    def _():
        step((s0_ref, 0), None)

    @pl.when(middle & (j % 2 == 1))
    def _():
        step((s1_ref, 1), (s0_ref, 0))

    @pl.when(middle & (j % 2 == 0))
    def _():
        step((s0_ref, 0), (s1_ref, 1))

    @pl.when(j == pair_count)
    def _():
        if (pair_count - 1) % 2 == 0:
            step(None, (s0_ref, 0))
        else:
            step(None, (s1_ref, 1))
        for c in range(chunk_count):
            if last:
                out_ref[:, c * CHUNK:(c + 1) * CHUNK] = acc_ref[c * CHUNK:(c + 1) * CHUNK, :].T
            else:
                out_ref[c * CHUNK:(c + 1) * CHUNK, :] = acc_ref[c * CHUNK:(c + 1) * CHUNK, :]


def page_mass_group(queries, keys, limits, acc, last):
    row_count = queries.shape[0]
    pair_count = queries.shape[1] // (2 * DH)
    pairs_per_kv = pair_count // (keys.shape[1] // (2 * DH))
    page_count = keys.shape[0]
    chunk_count = page_count // CHUNK
    first = acc is None
    kernel = functools.partial(
        _mass_kernel, chunk_count=chunk_count, score_scale=math.log2(math.e) / math.sqrt(DH),
        first=first, last=last, pairs_per_kv=pairs_per_kv, pair_count=pair_count)

    def pair_of(j):
        return jnp.minimum(j, pair_count - 1)

    in_specs = [
        pl.BlockSpec((row_count, 2 * DH), lambda j: (0, pair_of(j))),
        pl.BlockSpec((page_count, 2 * DH), lambda j: (0, pair_of(j) // pairs_per_kv)),
        pl.BlockSpec((1, row_count), lambda j: (0, 0)),
    ]
    operands = [queries, keys, limits.reshape(1, row_count)]
    if not first:
        in_specs.append(pl.BlockSpec((page_count, row_count), lambda j: (0, 0)))
        operands.append(acc)
    if last:
        out_shape = (row_count, page_count)
    else:
        out_shape = (page_count, row_count)
    aliases = {3: 0} if (not first and not last) else {}
    return pl.pallas_call(
        kernel,
        grid=(pair_count + 1,),
        in_specs=in_specs,
        out_specs=pl.BlockSpec(out_shape, lambda j: (0, 0)),
        scratch_shapes=[
            pltpu.VMEM((page_count, 6 * DH), jnp.bfloat16),
            pltpu.VMEM((page_count, 2 * row_count), jnp.float32),
            pltpu.VMEM((page_count, 2 * row_count), jnp.float32),
            pltpu.VMEM((2, 8, 2 * row_count), jnp.float32),
            pltpu.VMEM((page_count, row_count), jnp.float32),
        ],
        out_shape=jax.ShapeDtypeStruct(out_shape, jnp.float32),
        input_output_aliases=aliases,
        compiler_params=pltpu.CompilerParams(dimension_semantics=("arbitrary",)),
    )(*operands)


def head_sum_scatter(acc, head_devices):
    if head_devices != 2:
        return lax.psum_scatter(acc, "head", scatter_dimension=1, tiled=True)
    half = acc.shape[1] // 2
    first_half = lax.axis_index("head") == 0
    own = jnp.where(first_half, acc[:, :half], acc[:, half:])
    other = jnp.where(first_half, acc[:, half:], acc[:, :half])
    return own + lax.ppermute(other, "head", [(0, 1), (1, 0)])


def per_device(queries, key_max, key_min, limits, head_devices):
    local_pages = key_max.shape[0]
    kv_count = key_max.shape[1] // DH
    head_cols = queries.shape[1] // kv_count
    sizes = [kv_count - 1, 1] if kv_count > 1 else [kv_count]
    acc = None
    kv0 = 0
    for g, size in enumerate(sizes):
        parts = []
        for kv in range(kv0, kv0 + size):
            parts += [key_max[:, kv * DH:(kv + 1) * DH], key_min[:, kv * DH:(kv + 1) * DH]]
        keys = lax.all_gather(jnp.concatenate(parts, axis=1), ("row", "rep"), axis=0, tiled=True)
        cols = slice(kv0 * head_cols, (kv0 + size) * head_cols)
        acc = page_mass_group(queries[:, cols], keys, limits, acc, last=g == len(sizes) - 1)
        kv0 += size
    return head_sum_scatter(acc, head_devices)


def solution(mesh):
    placed = (
        P(("grp", "row", "rep"), "head"),
        P(("grp", "row", "rep"), "head"),
        P(("grp", "row", "rep"), "head"),
        P(("grp", "row", "rep")),
    )
    return jax.shard_map(
        functools.partial(per_device, head_devices=mesh.shape["head"]),
        mesh=mesh,
        in_specs=placed,
        out_specs=P(("grp", "row", "rep"), "head"),
        check_vma=False,
    )
```

time: 144 us -> 144 us (level); the launches traced: 144 us -> 141 us
  waiting for transfers between devices: 73.3 us -> 82.3 us
  Pallas kernels: 38.9 us -> 32 us
  between operations: 16.7 us -> 13.4 us
    all_gather x2, waiting for transfers between devices: 60.4 us -> 69.7 us  [per_device(): lax.all_gather(jnp.concatenate(parts, axis=1), ('row', 'rep'), axis=0, ti...]
    pallas_call x2, Pallas kernels: 38.9 us -> 32 us  [page_mass_group(): pl.pallas_call(kernel, grid=(pair_count + 1,), in_specs=in_specs, out_spe...]
    unnamed x13 -> x11, local copies, waits for them, and re-layouts: 5.71 us -> 5.71 us
  transfers between devices with their start and end apart: 3 -> 3, of which waited for: 3 -> 3; matrix products, arithmetic and copies ran while one was open for 3% -> 2% of each run, Pallas kernels for 19% -> 16%
where the time goes in v14:
time: 144 us; the launch traced here: 141 us
  waiting for transfers between devices  82.3 us (57%)
  Pallas kernels  32 us (22%)
  between operations  13.4 us (9%)
  local copies, waits for them, and re-layouts  8.83 us (6%)
  other arithmetic  2.96 us (2%)
  starting transfers between devices  1.58 us (1%)
    all_gather x2, waiting for transfers between devices, per_device(): lax.all_gather(jnp.concatenate(parts, axis=1), ('row', 'rep'), axis=0, ti...  69.7 us
    pallas_call x2, Pallas kernels, page_mass_group(): pl.pallas_call(kernel, grid=(pair_count + 1,), in_specs=in_specs, out_spe...  32 us
    ppermute x1, waiting for transfers between devices, head_sum_scatter(): return own + lax.ppermute(other, 'head', [(0, 1), (1, 0)])  12.6 us
    unnamed x11, local copies, waits for them, and re-layouts  5.71 us
  transfers between devices with their start and end apart: 3, of which 3 were waited for; matrix products, arithmetic and copies ran while one was open for 2% of the time, Pallas kernels for 16%

profile of v14, /device:TPU:16, one launch (start us, length us, event | category | flops | bytes accessed | tf_op | source)
XLA Modules:
  0.0 141.1 jit_solution(308427697414242306)
XLA Ops:
  6.5 0.0 all-gather.5.cloned.1.call-start
  6.5 1.1 slice_dynamic-update-slice_fusion.5
  7.6 0.9 slice_dynamic-update-slice_fusion.4
  8.5 0.9 slice_dynamic-update-slice_fusion.3
  9.4 0.9 slice_dynamic-update-slice_fusion.2
  10.4 1.0 slice_dynamic-update-slice_fusion.1
  11.4 1.0 slice_dynamic-update-slice_fusion
  12.4 0.0 copy-start.2
  12.4 0.9 copy-done.2
  13.3 0.0 all-gather.5.cloned.1.call-update
  13.3 0.0 all-gather.3.cloned.1.call-start
  13.3 0.7 pad_maximum_fusion
  14.1 0.0 all-gather.3.cloned.1.call-update
  14.1 0.0 copy-done.1
  14.1 1.3 slice.41.q_ref
  15.4 0.8 slice.38.q_ref
  16.2 61.7 %all-gather.5.cloned.1.call-done.k_ref = f32[2048,768]{1,0:T(8,128)} async-done(((f32[256,768]{1,0:T(8,128)}), f32[2048,768]{1,0:T(8,128)}) %all-gather.5.cloned.1.call-update) | async-done | bytes 6291472 | tf_op jit(solution)/shard_map/all_gather | solution.py:190
  77.9 22.2 %shard_map.46.refs_0_ = f32[2048,128]{1,0:T(8,128)} custom-call(f32[128,3072]{1,0:T(8,128)} %slice.41.q_ref, f32[2048,768]{1,0:T(8,128)} %all-gather.5.cloned.1.call-done.k_ref, s32[1,128]{1,0:T(1,128)} %bitcast.1), custom_call_target="tpu_custom_call" | custom-call | tf_op jit(solution)/shard_map/pallas_call | solution.py:151
  100.2 8.0 %all-gather.3.cloned.1.call-done.k_ref = f32[2048,256]{1,0:T(8,128)} async-done(((f32[256,256]{1,0:T(8,128)}), f32[2048,256]{1,0:T(8,128)}) %all-gather.3.cloned.1.call-update) | async-done | bytes 2097168 | tf_op jit(solution)/shard_map/all_gather | solution.py:190
  108.2 9.7 %shard_map.47 = f32[128,2048]{1,0:T(8,128)} custom-call(f32[128,1024]{1,0:T(8,128)} %slice.38.q_ref, f32[2048,256]{1,0:T(8,128)} %all-gather.3.cloned.1.call-done.k_ref, s32[1,128]{1,0:T(1,128)} %bitcast.2, f32[2048,128]{1,0:T(8,128)} %shard_map.46.refs_0_), custom_call_target="tpu_custom_call" | custom-call | tf_op jit(solution)/shard_map/pallas_call | solution.py:151
  117.9 1.3 slice_select_fusion
  119.3 1.5 %collective-permute-start = (f32[128,1024]{1,0:T(8,128)S(1)}, f32[128,1024]{1,0:T(8,128)S(1)}, u32[]{:S(2)}, u32[]{:S(2)}) collective-permute-start(f32[128,1024]{1,0:T(8,128)S(1)} %slice_select_fusion), channel_id=1, source_target_pairs={{0,2},{2,0},{1,3},{3,1},{4,6},{6,4},{5,7},{7,5},{8,10},{10,8},{9,1... | collective-permute-start | bytes 1572872 | tf_op jit(solution)/shard_map/ppermute | solution.py:176
  120.8 12.6 %collective-permute-done = f32[128,1024]{1,0:T(8,128)S(1)} collective-permute-done((f32[128,1024]{1,0:T(8,128)S(1)}, f32[128,1024]{1,0:T(8,128)S(1)}, u32[]{:S(2)}, u32[]{:S(2)}) %collective-permute-start) | collective-permute-done | bytes 524320 | tf_op jit(solution)/shard_map/ppermute | solution.py:176
  133.4 0.9 select_add_fusion
  (3 shorter events, 0.0 us)
Async XLA Ops:
  6.5 7.6 %copy-start.1 = (f32[128,4096]{1,0:T(8,128)S(1)}, f32[128,4096]{1,0:T(8,128)}, u32[]{:S(2)}) copy-start(f32[128,4096]{1,0:T(8,128)} %param.4) | copy-start | bytes 6291460
  6.5 71.4 %all-gather.5.cloned.1.call-start = ((), (), s32[]{:S(2)}) async-start(), calls=%async_computation.1 | async-start | bytes 7077888 | tf_op jit(solution)/shard_map/all_gather | solution.py:190
  12.4 0.9 copy-start.2
  13.3 94.9 %all-gather.3.cloned.1.call-start = ((), (), s32[]{:S(2)}) async-start(), calls=%async_computation | async-start | bytes 2359296 | tf_op jit(solution)/shard_map/all_gather | solution.py:190
  117.9 15.5 %copy-start = (f32[128,2048]{1,0:T(8,128)S(1)}, f32[128,2048]{1,0:T(8,128)}, u32[]{:S(2)}) copy-start(f32[128,2048]{1,0:T(8,128)} %shard_map.47) | copy-start | bytes 3145732
  119.3 14.1 %collective-permute-start = (f32[128,1024]{1,0:T(8,128)S(1)}, f32[128,1024]{1,0:T(8,128)S(1)}, u32[]{:S(2)}, u32[]{:S(2)}) collective-permute-start(f32[128,1024]{1,0:T(8,128)S(1)} %slice_select_fusion), channel_id=1, source_target_pairs={{0,2},{2,0},{1,3},{3,1},{4,6},{6,4},{5,7},{7,5},{8,10},{10,8},{9,1... | collective-permute-start | bytes 1572872 | tf_op jit(solution)/shard_map/ppermute | solution.py:176
Sparse Core Ops, SparseCore 0:
  13.4 64.4 all-gather.4
  79.5 28.5 all-gather.2

commit v15 on v14

--- a/solution.py
+++ b/solution.py
@@ -20,11 +20,12 @@
 
 
 def _mass_kernel(q_ref, k_ref, lim_ref, *refs, chunk_count, score_scale, first, last,
-                 pairs_per_kv, pair_count):
-    if first:
-        out_ref, kcat_ref, s0_ref, s1_ref, top_ref, acc_ref = refs
-    else:
-        acc_in_ref, out_ref, kcat_ref, s0_ref, s1_ref, top_ref, acc_ref = refs
+                 pairs_per_kv, pair_count, halves):
+    refs = list(refs)
+    acc_in_ref = None if first else refs.pop(0)
+    out_refs = [refs.pop(0) for _ in range(2 if halves else 1)]
+    kcat_ref, s0_ref, s1_ref, top_ref, acc_ref = refs
+    out_ref = out_refs[0]
     j = pl.program_id(0)
     row_count = q_ref.shape[0]
     lanes = 2 * row_count
@@ -113,14 +114,23 @@
             step(None, (s0_ref, 0))
         else:
             step(None, (s1_ref, 1))
-        for c in range(chunk_count):
+        if halves:
+            half = chunk_count // 2
+            for own_first in (True, False):
+                @pl.when((lax.axis_index("head") == 0) == own_first)
+                def _():
+                    for c in range(chunk_count):
+                        ref = out_refs[0 if (c < half) == own_first else 1]
+                        k = c % half
+                        ref[:, k * CHUNK:(k + 1) * CHUNK] = acc_ref[c * CHUNK:(c + 1) * CHUNK, :].T
+        for c in range(chunk_count if not halves else 0):
             if last:
                 out_ref[:, c * CHUNK:(c + 1) * CHUNK] = acc_ref[c * CHUNK:(c + 1) * CHUNK, :].T
             else:
                 out_ref[c * CHUNK:(c + 1) * CHUNK, :] = acc_ref[c * CHUNK:(c + 1) * CHUNK, :]
 
 
-def page_mass_group(queries, keys, limits, acc, last):
+def page_mass_group(queries, keys, limits, acc, last, halves=False):
     row_count = queries.shape[0]
     pair_count = queries.shape[1] // (2 * DH)
     pairs_per_kv = pair_count // (keys.shape[1] // (2 * DH))
@@ -129,7 +139,8 @@
     first = acc is None
     kernel = functools.partial(
         _mass_kernel, chunk_count=chunk_count, score_scale=math.log2(math.e) / math.sqrt(DH),
-        first=first, last=last, pairs_per_kv=pairs_per_kv, pair_count=pair_count)
+        first=first, last=last, pairs_per_kv=pairs_per_kv, pair_count=pair_count,
+        halves=halves)
 
     def pair_of(j):
         return jnp.minimum(j, pair_count - 1)
@@ -148,11 +159,18 @@
     else:
         out_shape = (page_count, row_count)
     aliases = {3: 0} if (not first and not last) else {}
+    if halves:
+        out_shape = (row_count, page_count // 2)
+    out_specs = pl.BlockSpec(out_shape, lambda j: (0, 0))
+    out_struct = jax.ShapeDtypeStruct(out_shape, jnp.float32)
+    if halves:
+        out_specs = [out_specs, out_specs]
+        out_struct = [out_struct, out_struct]
     return pl.pallas_call(
         kernel,
         grid=(pair_count + 1,),
         in_specs=in_specs,
-        out_specs=pl.BlockSpec(out_shape, lambda j: (0, 0)),
+        out_specs=out_specs,
         scratch_shapes=[
             pltpu.VMEM((page_count, 6 * DH), jnp.bfloat16),
             pltpu.VMEM((page_count, 2 * row_count), jnp.float32),
@@ -160,7 +178,7 @@
             pltpu.VMEM((2, 8, 2 * row_count), jnp.float32),
             pltpu.VMEM((page_count, row_count), jnp.float32),
         ],
-        out_shape=jax.ShapeDtypeStruct(out_shape, jnp.float32),
+        out_shape=out_struct,
         input_output_aliases=aliases,
         compiler_params=pltpu.CompilerParams(dimension_semantics=("arbitrary",)),
     )(*operands)
@@ -169,10 +187,7 @@
 def head_sum_scatter(acc, head_devices):
     if head_devices != 2:
         return lax.psum_scatter(acc, "head", scatter_dimension=1, tiled=True)
-    half = acc.shape[1] // 2
-    first_half = lax.axis_index("head") == 0
-    own = jnp.where(first_half, acc[:, :half], acc[:, half:])
-    other = jnp.where(first_half, acc[:, half:], acc[:, :half])
+    own, other = acc
     return own + lax.ppermute(other, "head", [(0, 1), (1, 0)])
 
 
@@ -189,7 +204,9 @@
             parts += [key_max[:, kv * DH:(kv + 1) * DH], key_min[:, kv * DH:(kv + 1) * DH]]
         keys = lax.all_gather(jnp.concatenate(parts, axis=1), ("row", "rep"), axis=0, tiled=True)
         cols = slice(kv0 * head_cols, (kv0 + size) * head_cols)
-        acc = page_mass_group(queries[:, cols], keys, limits, acc, last=g == len(sizes) - 1)
+        last = g == len(sizes) - 1
+        acc = page_mass_group(queries[:, cols], keys, limits, acc, last=last,
+                              halves=last and head_devices == 2)
         kv0 += size
     return head_sum_scatter(acc, head_devices)
 

time: 144 us -> 144 us (level)
    unnamed x11 -> x9, local copies, waits for them, and re-layouts: 5.71 us -> 5.7 us
where the time goes in v15:
time: 144 us; the launch traced here: 141 us
  waiting for transfers between devices  82.5 us (57%)
  Pallas kernels  32.2 us (22%)
  between operations  13.4 us (9%)
  local copies, waits for them, and re-layouts  8.82 us (6%)
  other arithmetic  2.64 us (2%)
  starting transfers between devices  1.51 us (1%)
    all_gather x2, waiting for transfers between devices, per_device(): lax.all_gather(jnp.concatenate(parts, axis=1), ('row', 'rep'), axis=0, ti...  69.7 us
    pallas_call x2, Pallas kernels, page_mass_group(): pl.pallas_call(kernel, grid=(pair_count + 1,), in_specs=in_specs, out_spe...  32.2 us
    ppermute x1, waiting for transfers between devices, head_sum_scatter(): return own + lax.ppermute(other, 'head', [(0, 1), (1, 0)])  12.8 us
    unnamed x9, local copies, waits for them, and re-layouts  5.7 us
  transfers between devices with their start and end apart: 3, of which 3 were waited for; matrix products, arithmetic and copies ran while one was open for 2% of the time, Pallas kernels for 16%

profile of v15, /device:TPU:16, one launch (start us, length us, event | category | flops | bytes accessed | tf_op | source)
XLA Modules:
  0.0 141.2 jit_solution(18047475333346110773)
XLA Ops:
  6.5 0.0 copy-start
  6.5 0.0 all-gather.5.cloned.1.call-start
  6.5 1.1 slice_dynamic-update-slice_fusion.5
  7.6 0.9 slice_dynamic-update-slice_fusion.4
  8.5 0.9 slice_dynamic-update-slice_fusion.3
  9.4 0.9 slice_dynamic-update-slice_fusion.2
  10.4 1.0 slice_dynamic-update-slice_fusion.1
  11.4 1.0 slice_dynamic-update-slice_fusion
  12.4 0.0 copy-start.1
  12.4 0.9 copy-done.1
  13.3 0.0 all-gather.5.cloned.1.call-update
  13.3 0.0 all-gather.3.cloned.1.call-start
  13.3 0.7 pad_maximum_fusion
  14.1 0.0 all-gather.3.cloned.1.call-update
  14.1 0.0 copy-done
  14.1 1.3 slice.33.q_ref
  15.4 0.8 slice.30.q_ref
  16.2 61.7 %all-gather.5.cloned.1.call-done.k_ref = f32[2048,768]{1,0:T(8,128)} async-done(((f32[256,768]{1,0:T(8,128)}), f32[2048,768]{1,0:T(8,128)}) %all-gather.5.cloned.1.call-update) | async-done | bytes 6291472 | tf_op jit(solution)/shard_map/all_gather | solution.py:205
  77.9 22.2 %shard_map.46.refs_0_ = f32[2048,128]{1,0:T(8,128)} custom-call(f32[128,3072]{1,0:T(8,128)} %slice.33.q_ref, f32[2048,768]{1,0:T(8,128)} %all-gather.5.cloned.1.call-done.k_ref, s32[1,128]{1,0:T(1,128)} %bitcast.1), custom_call_target="tpu_custom_call" | custom-call | tf_op jit(solution)/shard_map/pallas_call | solution.py:169
  100.2 8.0 %all-gather.3.cloned.1.call-done.k_ref = f32[2048,256]{1,0:T(8,128)} async-done(((f32[256,256]{1,0:T(8,128)}), f32[2048,256]{1,0:T(8,128)}) %all-gather.3.cloned.1.call-update) | async-done | bytes 2097168 | tf_op jit(solution)/shard_map/all_gather | solution.py:205
  108.2 10.0 %shard_map.47 = (f32[128,1024]{1,0:T(8,128)}, f32[128,1024]{1,0:T(8,128)}) custom-call(f32[128,1024]{1,0:T(8,128)} %slice.30.q_ref, f32[2048,256]{1,0:T(8,128)} %all-gather.3.cloned.1.call-done.k_ref, s32[1,128]{1,0:T(1,128)} %bitcast.2, f32[2048,128]{1,0:T(8,128)} %shard_map.46.refs_0_), custom_call_target="tpu_custom_call" | custom-call | tf_op jit(solution)/shard_map/pallas_call | solution.py:169
  118.1 1.5 %collective-permute-start = (f32[128,1024]{1,0:T(8,128)}, f32[128,1024]{1,0:T(8,128)S(1)}, u32[]{:S(2)}, u32[]{:S(2)}) collective-permute-start(f32[128,1024]{1,0:T(8,128)} %get-tuple-element.8), channel_id=1, source_target_pairs={{0,2},{2,0},{1,3},{3,1},{4,6},{6,4},{5,7},{7,5},{8,10},{10,8},{9,1... | collective-permute-start | bytes 1572872 | tf_op jit(solution)/shard_map/ppermute | solution.py:191
  119.6 12.8 %collective-permute-done = f32[128,1024]{1,0:T(8,128)S(1)} collective-permute-done((f32[128,1024]{1,0:T(8,128)}, f32[128,1024]{1,0:T(8,128)S(1)}, u32[]{:S(2)}, u32[]{:S(2)}) %collective-permute-start) | collective-permute-done | bytes 524320 | tf_op jit(solution)/shard_map/ppermute | solution.py:191
  132.4 1.9 %add.3 = f32[128,1024]{1,0:T(8,128)} add(f32[128,1024]{1,0:T(8,128)} %get-tuple-element.7, f32[128,1024]{1,0:T(8,128)S(1)} %collective-permute-done) | non-fusion elementwise | flops 131072 | bytes 1572864 | tf_op jit(solution)/shard_map/add | solution.py:191
Async XLA Ops:
  6.5 7.6 %copy-start = (f32[128,4096]{1,0:T(8,128)S(1)}, f32[128,4096]{1,0:T(8,128)}, u32[]{:S(2)}) copy-start(f32[128,4096]{1,0:T(8,128)} %param.4) | copy-start | bytes 6291460
  6.5 71.4 %all-gather.5.cloned.1.call-start = ((), (), s32[]{:S(2)}) async-start(), calls=%async_computation.1 | async-start | bytes 7077888 | tf_op jit(solution)/shard_map/all_gather | solution.py:205
  12.4 0.9 copy-start.1
  13.3 94.9 %all-gather.3.cloned.1.call-start = ((), (), s32[]{:S(2)}) async-start(), calls=%async_computation | async-start | bytes 2359296 | tf_op jit(solution)/shard_map/all_gather | solution.py:205
  118.1 14.3 %collective-permute-start = (f32[128,1024]{1,0:T(8,128)}, f32[128,1024]{1,0:T(8,128)S(1)}, u32[]{:S(2)}, u32[]{:S(2)}) collective-permute-start(f32[128,1024]{1,0:T(8,128)} %get-tuple-element.8), channel_id=1, source_target_pairs={{0,2},{2,0},{1,3},{3,1},{4,6},{6,4},{5,7},{7,5},{8,10},{10,8},{9,1... | collective-permute-start | bytes 1572872 | tf_op jit(solution)/shard_map/ppermute | solution.py:191
Sparse Core Ops, SparseCore 0:
  13.4 64.4 all-gather.4
  79.5 28.5 all-gather.2

commit v16 on v15

--- a/solution.py
+++ b/solution.py
@@ -199,10 +199,12 @@
     acc = None
     kv0 = 0
     for g, size in enumerate(sizes):
-        parts = []
-        for kv in range(kv0, kv0 + size):
-            parts += [key_max[:, kv * DH:(kv + 1) * DH], key_min[:, kv * DH:(kv + 1) * DH]]
-        keys = lax.all_gather(jnp.concatenate(parts, axis=1), ("row", "rep"), axis=0, tiled=True)
+        span = slice(kv0 * DH, (kv0 + size) * DH)
+        bounds = jnp.stack(
+            (key_max[:, span].reshape(local_pages, size, DH),
+             key_min[:, span].reshape(local_pages, size, DH)), axis=2,
+        ).reshape(local_pages, size * 2 * DH)
+        keys = lax.all_gather(bounds, ("row", "rep"), axis=0, tiled=True)
         cols = slice(kv0 * head_cols, (kv0 + size) * head_cols)
         last = g == len(sizes) - 1
         acc = page_mass_group(queries[:, cols], keys, limits, acc, last=last,

time: 144 us -> 141 us (0.979)
    unnamed x9 -> x7, local copies, waits for them, and re-layouts: 5.7 us -> 1.06 us
    another operation x0 -> x3, local copies, waits for them, and re-layouts: none -> 1.88 us  [per_device(): jnp.stack((key_max[:, span].reshape(local_pages, size, DH), key_min[:, sp...]
    reshape x0 -> x1, local copies, waits for them, and re-layouts: none -> 1.53 us  [per_device(): bounds = jnp.stack((key_max[:, span].reshape(local_pages, size, DH), key_...]
  transfers between devices with their start and end apart: 3 -> 3, of which waited for: 3 -> 3; matrix products, arithmetic and copies ran while one was open for 2% -> 3% of each run, Pallas kernels for 16% -> 16%
where the time goes in v16:
time: 141 us; the launch traced here: 138 us
  waiting for transfers between devices  81.2 us (58%)
  Pallas kernels  32.2 us (23%)
  between operations  13.5 us (10%)
  local copies, waits for them, and re-layouts  7.66 us (5%)
  other arithmetic  2.01 us (1%)
  starting transfers between devices  1.52 us (1%)
    all_gather x2, waiting for transfers between devices, per_device(): keys = lax.all_gather(bounds, ('row', 'rep'), axis=0, tiled=True)  68.4 us
    pallas_call x2, Pallas kernels, page_mass_group(): pl.pallas_call(kernel, grid=(pair_count + 1,), in_specs=in_specs, out_spe...  32.2 us
    ppermute x1, waiting for transfers between devices, head_sum_scatter(): return own + lax.ppermute(other, 'head', [(0, 1), (1, 0)])  12.8 us
  transfers between devices with their start and end apart: 3, of which 3 were waited for; matrix products, arithmetic and copies ran while one was open for 3% of the time, Pallas kernels for 16%

profile of v16, /device:TPU:16, one launch (start us, length us, event | category | flops | bytes accessed | tf_op | source)
XLA Modules:
  0.0 138.1 jit_solution(11617812374860389415)
XLA Ops:
  6.5 0.0 all-gather.5.cloned.1.call-start
  6.5 1.1 slice.22
  7.6 0.2 copy.12
  7.8 0.0 slice-done
  7.8 0.2 copy.13
  8.0 0.1 pad_maximum_fusion
  8.0 0.0 copy-start.1
  8.1 0.6 copy.11
  8.7 1.5 %reshape.12 = f32[256,768]{1,0:T(8,128)} reshape(f32[256,3,2,128]{3,2,1,0:T(2,128)S(1)} %copy.11) | data formatting | bytes 1572864 | tf_op jit(solution)/shard_map/reshape | solution.py:206
  10.2 0.0 all-gather.5.cloned.1.call-update
  10.2 0.0 all-gather.3.cloned.1.call-start
  10.3 1.1 slice_bitcast_fusion
  11.4 0.2 copy.8
  11.6 0.7 copy.16
  12.3 0.0 all-gather.3.cloned.1.call-update
  12.4 1.3 slice.21.q_ref
  13.7 0.8 slice.18.q_ref
  14.5 60.4 %all-gather.5.cloned.1.call-done.k_ref = f32[2048,768]{1,0:T(8,128)} async-done(((f32[256,768]{1,0:T(8,128)}), f32[2048,768]{1,0:T(8,128)}) %all-gather.5.cloned.1.call-update) | async-done | bytes 6291472 | tf_op jit(solution)/shard_map/all_gather | solution.py:207
  74.9 22.2 %shard_map.46.refs_0_ = f32[2048,128]{1,0:T(8,128)} custom-call(f32[128,3072]{1,0:T(8,128)} %slice.21.q_ref, f32[2048,768]{1,0:T(8,128)} %all-gather.5.cloned.1.call-done.k_ref, s32[1,128]{1,0:T(1,128)} %bitcast.17), custom_call_target="tpu_custom_call" | custom-call | tf_op jit(solution)/shard_map/pallas_call | solution.py:169
  97.1 8.0 %all-gather.3.cloned.1.call-done.k_ref = f32[2048,256]{1,0:T(8,128)} async-done(((f32[256,256]{1,0:T(8,128)}), f32[2048,256]{1,0:T(8,128)}) %all-gather.3.cloned.1.call-update) | async-done | bytes 2097168 | tf_op jit(solution)/shard_map/all_gather | solution.py:207
  105.1 10.0 %shard_map.47 = (f32[128,1024]{1,0:T(8,128)}, f32[128,1024]{1,0:T(8,128)}) custom-call(f32[128,1024]{1,0:T(8,128)} %slice.18.q_ref, f32[2048,256]{1,0:T(8,128)} %all-gather.3.cloned.1.call-done.k_ref, s32[1,128]{1,0:T(1,128)} %bitcast.18, f32[2048,128]{1,0:T(8,128)} %shard_map.46.refs_0_), custom_call_target="tpu_custom_call" | custom-call | tf_op jit(solution)/shard_map/pallas_call | solution.py:169
  115.1 1.5 %collective-permute-start = (f32[128,1024]{1,0:T(8,128)}, f32[128,1024]{1,0:T(8,128)S(1)}, u32[]{:S(2)}, u32[]{:S(2)}) collective-permute-start(f32[128,1024]{1,0:T(8,128)} %get-tuple-element.8), channel_id=1, source_target_pairs={{0,2},{2,0},{1,3},{3,1},{4,6},{6,4},{5,7},{7,5},{8,10},{10,8},{9,1... | collective-permute-start | bytes 1572872 | tf_op jit(solution)/shard_map/ppermute | solution.py:191
  116.6 12.8 %collective-permute-done = f32[128,1024]{1,0:T(8,128)S(1)} collective-permute-done((f32[128,1024]{1,0:T(8,128)}, f32[128,1024]{1,0:T(8,128)S(1)}, u32[]{:S(2)}, u32[]{:S(2)}) %collective-permute-start) | collective-permute-done | bytes 524320 | tf_op jit(solution)/shard_map/ppermute | solution.py:191
  129.3 1.9 %add.3 = f32[128,1024]{1,0:T(8,128)} add(f32[128,1024]{1,0:T(8,128)} %get-tuple-element.7, f32[128,1024]{1,0:T(8,128)S(1)} %collective-permute-done) | non-fusion elementwise | flops 131072 | bytes 1572864 | tf_op jit(solution)/shard_map/add | solution.py:191
  (5 shorter events, 0.0 us)
Async XLA Ops:
  6.5 1.3 slice-start
  6.5 68.3 %all-gather.5.cloned.1.call-start = ((), (), s32[]{:S(2)}) async-start(), calls=%async_computation.1 | async-start | bytes 7077888 | tf_op jit(solution)/shard_map/all_gather | solution.py:207
  8.0 2.2 %copy-start.1 = (f32[256,512]{1,0:T(8,128)S(1)}, f32[256,512]{1,0:T(8,128)}, u32[]{:S(2)}) copy-start(f32[256,512]{1,0:T(8,128)} %param.6) | copy-start | bytes 1572868
  10.2 2.1 %copy-start = (f32[128,4096]{1,0:T(8,128)S(1)}, f32[128,4096]{1,0:T(8,128)}, u32[]{:S(2)}) copy-start(f32[128,4096]{1,0:T(8,128)} %param.4) | copy-start | bytes 6291460
  10.2 94.9 %all-gather.3.cloned.1.call-start = ((), (), s32[]{:S(2)}) async-start(), calls=%async_computation | async-start | bytes 2359296 | tf_op jit(solution)/shard_map/all_gather | solution.py:207
  115.1 14.3 %collective-permute-start = (f32[128,1024]{1,0:T(8,128)}, f32[128,1024]{1,0:T(8,128)S(1)}, u32[]{:S(2)}, u32[]{:S(2)}) collective-permute-start(f32[128,1024]{1,0:T(8,128)} %get-tuple-element.8), channel_id=1, source_target_pairs={{0,2},{2,0},{1,3},{3,1},{4,6},{6,4},{5,7},{7,5},{8,10},{10,8},{9,1... | collective-permute-start | bytes 1572872 | tf_op jit(solution)/shard_map/ppermute | solution.py:191
Sparse Core Ops, SparseCore 0:
  10.4 64.4 all-gather.4
  76.5 28.5 all-gather.2

commit v17 on v16

--- a/solution.py
+++ b/solution.py
@@ -19,7 +19,7 @@
     return hi, lo
 
 
-def _mass_kernel(q_ref, k_ref, lim_ref, *refs, chunk_count, score_scale, first, last,
+def _mass_kernel(q_ref, kmax_ref, kmin_ref, lim_ref, *refs, chunk_count, score_scale, first, last,
                  pairs_per_kv, pair_count, halves):
     refs = list(refs)
     acc_in_ref = None if first else refs.pop(0)
@@ -42,8 +42,10 @@
     @pl.when((j < pair_count) & (j % pairs_per_kv == 0))
     def _():
         for c in range(chunk_count):
-            hi, lo = _split(k_ref[c * CHUNK:(c + 1) * CHUNK, :])
-            kcat_ref[c * CHUNK:(c + 1) * CHUNK, :] = jnp.concatenate([hi, hi, lo], axis=1)
+            hmax, lmax = _split(kmax_ref[c * CHUNK:(c + 1) * CHUNK, :])
+            hmin, lmin = _split(kmin_ref[c * CHUNK:(c + 1) * CHUNK, :])
+            kcat_ref[c * CHUNK:(c + 1) * CHUNK, :] = jnp.concatenate(
+                [hmax, hmin, hmax, hmin, lmax, lmin], axis=1)
 
     def vreg_fold(v, op):
         return op(v.reshape(CHUNK // 8, 8, lanes), axis=0)
@@ -130,11 +132,12 @@
                 out_ref[c * CHUNK:(c + 1) * CHUNK, :] = acc_ref[c * CHUNK:(c + 1) * CHUNK, :]
 
 
-def page_mass_group(queries, keys, limits, acc, last, halves=False):
+def page_mass_group(queries, kmax, kmin, limits, acc, last, halves=False):
     row_count = queries.shape[0]
     pair_count = queries.shape[1] // (2 * DH)
-    pairs_per_kv = pair_count // (keys.shape[1] // (2 * DH))
-    page_count = keys.shape[0]
+    kv_in_group = kmax.shape[1] // (2 * DH)
+    pairs_per_kv = pair_count // kv_in_group
+    page_count = kmax.shape[0]
     chunk_count = page_count // CHUNK
     first = acc is None
     kernel = functools.partial(
@@ -147,10 +150,11 @@
 
     in_specs = [
         pl.BlockSpec((row_count, 2 * DH), lambda j: (0, pair_of(j))),
-        pl.BlockSpec((page_count, 2 * DH), lambda j: (0, pair_of(j) // pairs_per_kv)),
+        pl.BlockSpec((page_count, DH), lambda j: (0, pair_of(j) // pairs_per_kv)),
+        pl.BlockSpec((page_count, DH), lambda j: (0, kv_in_group + pair_of(j) // pairs_per_kv)),
         pl.BlockSpec((1, row_count), lambda j: (0, 0)),
     ]
-    operands = [queries, keys, limits.reshape(1, row_count)]
+    operands = [queries, kmax, kmin, limits.reshape(1, row_count)]
     if not first:
         in_specs.append(pl.BlockSpec((page_count, row_count), lambda j: (0, 0)))
         operands.append(acc)
@@ -158,7 +162,7 @@
         out_shape = (row_count, page_count)
     else:
         out_shape = (page_count, row_count)
-    aliases = {3: 0} if (not first and not last) else {}
+    aliases = {4: 0} if (not first and not last) else {}
     if halves:
         out_shape = (row_count, page_count // 2)
     out_specs = pl.BlockSpec(out_shape, lambda j: (0, 0))
@@ -200,14 +204,11 @@
     kv0 = 0
     for g, size in enumerate(sizes):
         span = slice(kv0 * DH, (kv0 + size) * DH)
-        bounds = jnp.stack(
-            (key_max[:, span].reshape(local_pages, size, DH),
-             key_min[:, span].reshape(local_pages, size, DH)), axis=2,
-        ).reshape(local_pages, size * 2 * DH)
-        keys = lax.all_gather(bounds, ("row", "rep"), axis=0, tiled=True)
+        keys = lax.all_gather(jnp.concatenate((key_max[:, span], key_min[:, span]), axis=1),
+                              ("row", "rep"), axis=0, tiled=True)
         cols = slice(kv0 * head_cols, (kv0 + size) * head_cols)
         last = g == len(sizes) - 1
-        acc = page_mass_group(queries[:, cols], keys, limits, acc, last=last,
+        acc = page_mass_group(queries[:, cols], keys, keys, limits, acc, last=last,
                               halves=last and head_devices == 2)
         kv0 += size
     return head_sum_scatter(acc, head_devices)

time: 141 us -> 140 us (level)
  local copies, waits for them, and re-layouts: 7.66 us -> 4.37 us
  other arithmetic: 2.01 us -> 3.59 us
    another operation x3 -> x0, local copies, waits for them, and re-layouts: 1.88 us -> none  [per_device(): jnp.stack((key_max[:, span].reshape(local_pages, size, DH), key_min[:, sp...]
    concatenate x0 -> x2, other arithmetic: none -> 1.67 us  [per_device(): jnp.concatenate((key_max[:, span], key_min[:, span]), axis=1)]
    reshape x1 -> x0, local copies, waits for them, and re-layouts: 1.53 us -> none  [per_device(): bounds = jnp.stack((key_max[:, span].reshape(local_pages, size, DH), key_...]
    all_gather x2, waiting for transfers between devices: 68.4 us -> 69.8 us  [per_device(): lax.all_gather(jnp.concatenate((key_max[:, span], key_min[:, span]), axis...]
  transfers between devices with their start and end apart: 3 -> 3, of which waited for: 3 -> 3; matrix products, arithmetic and copies ran while one was open for 3% -> 2% of each run, Pallas kernels for 16% -> 16%
where the time goes in v17:
time: 140 us; the launch traced here: 138 us
  waiting for transfers between devices  82.6 us (59%)
  Pallas kernels  32.1 us (23%)
  between operations  13.4 us (10%)
  local copies, waits for them, and re-layouts  4.37 us (3%)
  other arithmetic  3.59 us (3%)
  starting transfers between devices  1.52 us (1%)
    all_gather x2, waiting for transfers between devices, per_device(): lax.all_gather(jnp.concatenate((key_max[:, span], key_min[:, span]), axis...  69.8 us
    pallas_call x2, Pallas kernels, page_mass_group(): pl.pallas_call(kernel, grid=(pair_count + 1,), in_specs=in_specs, out_spe...  32.1 us
    ppermute x1, waiting for transfers between devices, head_sum_scatter(): return own + lax.ppermute(other, 'head', [(0, 1), (1, 0)])  12.8 us
  transfers between devices with their start and end apart: 3, of which 3 were waited for; matrix products, arithmetic and copies ran while one was open for 2% of the time, Pallas kernels for 16%

profile of v17, /device:TPU:16, one launch (start us, length us, event | category | flops | bytes accessed | tf_op | source)
XLA Modules:
  0.0 137.6 jit_solution(16927652940097421695)
XLA Ops:
  6.5 0.0 slice-start
  6.5 0.0 slice-start.1
  6.5 0.0 all-gather.5.cloned.1.call-start
  6.5 1.1 slice.22
  7.6 0.0 copy-start
  7.6 1.2 slice.23
  8.8 1.0 pad_maximum_fusion
  9.7 0.0 all-gather.5.cloned.1.call-update
  9.8 0.0 all-gather.3.cloned.1.call-start
  9.8 0.0 slice-done
  9.8 0.0 slice-done.1
  9.8 0.7 pad_maximum_fusion.1
  10.6 0.0 all-gather.3.cloned.1.call-update
  10.6 0.0 copy-done
  10.6 1.3 slice.21.q_ref
  11.9 0.8 slice.18.q_ref
  12.7 61.7 %all-gather.5.cloned.1.call-done.kmax_ref.kmin_ref = f32[2048,768]{1,0:T(8,128)} async-done(((f32[256,768]{1,0:T(8,128)}), f32[2048,768]{1,0:T(8,128)}) %all-gather.5.cloned.1.call-update) | async-done | bytes 6291472 | tf_op jit(solution)/shard_map/all_gather | solution.py:207
  74.4 22.1 %shard_map.46.refs_0_ = f32[2048,128]{1,0:T(8,128)} custom-call(f32[128,3072]{1,0:T(8,128)} %slice.21.q_ref, f32[2048,768]{1,0:T(8,128)} %all-gather.5.cloned.1.call-done.kmax_ref.kmin_ref, f32[2048,768]{1,0:T(8,128)} %all-gather.5.cloned.1.call-done.kmax_ref.kmin_ref, s32[1,128]{1,0:T(1,128)} %bitcast.1), custom_call_target="tpu_custom_call" | custom-call | tf_op jit(solution)/shard_map/pallas_call | solution.py:173
  96.5 8.1 %all-gather.3.cloned.1.call-done.kmax_ref.kmin_ref = f32[2048,256]{1,0:T(8,128)} async-done(((f32[256,256]{1,0:T(8,128)}), f32[2048,256]{1,0:T(8,128)}) %all-gather.3.cloned.1.call-update) | async-done | bytes 2097168 | tf_op jit(solution)/shard_map/all_gather | solution.py:207
  104.6 10.0 %shard_map.47 = (f32[128,1024]{1,0:T(8,128)}, f32[128,1024]{1,0:T(8,128)}) custom-call(f32[128,1024]{1,0:T(8,128)} %slice.18.q_ref, f32[2048,256]{1,0:T(8,128)} %all-gather.3.cloned.1.call-done.kmax_ref.kmin_ref, f32[2048,256]{1,0:T(8,128)} %all-gather.3.cloned.1.call-done.kmax_ref.kmin_ref, s32[1,128]{1,0:T(1,128)} %bitcast.2, f32[2048,128]{1,0:T(8,128)} %shard_map.46.refs_0_), custom_call_target="tpu_custom_call" | custom-call | tf_op jit(solution)/shard_map/pallas_call | solution.py:173
  114.6 1.5 %collective-permute-start = (f32[128,1024]{1,0:T(8,128)}, f32[128,1024]{1,0:T(8,128)S(1)}, u32[]{:S(2)}, u32[]{:S(2)}) collective-permute-start(f32[128,1024]{1,0:T(8,128)} %get-tuple-element.8), channel_id=1, source_target_pairs={{0,2},{2,0},{1,3},{3,1},{4,6},{6,4},{5,7},{7,5},{8,10},{10,8},{9,1... | collective-permute-start | bytes 1572872 | tf_op jit(solution)/shard_map/ppermute | solution.py:195
  116.1 12.8 %collective-permute-done = f32[128,1024]{1,0:T(8,128)S(1)} collective-permute-done((f32[128,1024]{1,0:T(8,128)}, f32[128,1024]{1,0:T(8,128)S(1)}, u32[]{:S(2)}, u32[]{:S(2)}) %collective-permute-start) | collective-permute-done | bytes 524320 | tf_op jit(solution)/shard_map/ppermute | solution.py:195
  128.9 1.9 %add.3 = f32[128,1024]{1,0:T(8,128)} add(f32[128,1024]{1,0:T(8,128)} %get-tuple-element.7, f32[128,1024]{1,0:T(8,128)S(1)} %collective-permute-done) | non-fusion elementwise | flops 131072 | bytes 1572864 | tf_op jit(solution)/shard_map/add | solution.py:195
Async XLA Ops:
  6.5 3.3 %slice-start = ((f32[256,512]{1,0:T(8,128)}), f32[256,128]{1,0:T(8,128)S(1)}, s32[]{:S(2)}) async-start(f32[256,512]{1,0:T(8,128)} %param.5), calls=%async_computation.2 | async-start | bytes 262144 | tf_op jit(solution)/shard_map/slice | solution.py:207
  6.5 3.3 %slice-start.1 = ((f32[256,512]{1,0:T(8,128)}), f32[256,128]{1,0:T(8,128)S(1)}, s32[]{:S(2)}) async-start(f32[256,512]{1,0:T(8,128)} %param.6), calls=%async_computation.3 | async-start | bytes 262144 | tf_op jit(solution)/shard_map/slice | solution.py:207
  6.5 67.9 %all-gather.5.cloned.1.call-start = ((), (), s32[]{:S(2)}) async-start(), calls=%async_computation.1 | async-start | bytes 7077888 | tf_op jit(solution)/shard_map/all_gather | solution.py:207
  7.6 3.0 %copy-start = (f32[128,4096]{1,0:T(8,128)S(1)}, f32[128,4096]{1,0:T(8,128)}, u32[]{:S(2)}) copy-start(f32[128,4096]{1,0:T(8,128)} %param.4) | copy-start | bytes 6291460
  9.8 94.9 %all-gather.3.cloned.1.call-start = ((), (), s32[]{:S(2)}) async-start(), calls=%async_computation | async-start | bytes 2359296 | tf_op jit(solution)/shard_map/all_gather | solution.py:207
  114.6 14.3 %collective-permute-start = (f32[128,1024]{1,0:T(8,128)}, f32[128,1024]{1,0:T(8,128)S(1)}, u32[]{:S(2)}, u32[]{:S(2)}) collective-permute-start(f32[128,1024]{1,0:T(8,128)} %get-tuple-element.8), channel_id=1, source_target_pairs={{0,2},{2,0},{1,3},{3,1},{4,6},{6,4},{5,7},{7,5},{8,10},{10,8},{9,1... | collective-permute-start | bytes 1572872 | tf_op jit(solution)/shard_map/ppermute | solution.py:195
Sparse Core Ops, SparseCore 0:
  9.9 64.4 all-gather.4
  76.0 28.5 all-gather.2

commit v18 on v17

--- a/solution.py
+++ b/solution.py
@@ -10,7 +10,7 @@
 
 DH = 128
 CHUNK = 256
-MM_CHUNK = 1024
+MM_CHUNK = 2048
 
 
 def _split(x):

time: 140 us -> 140 us (level)
  no operation moved by 1% of the time
where the time goes in v18:
time: 140 us; the launch traced here: 138 us
  waiting for transfers between devices  82.1 us (59%)
  Pallas kernels  32.9 us (24%)
  between operations  13.4 us (10%)
  local copies, waits for them, and re-layouts  4.37 us (3%)
  other arithmetic  3.59 us (3%)
  starting transfers between devices  1.51 us (1%)
    all_gather x2, waiting for transfers between devices, per_device(): lax.all_gather(jnp.concatenate((key_max[:, span], key_min[:, span]), axis...  69.2 us
    pallas_call x2, Pallas kernels, page_mass_group(): pl.pallas_call(kernel, grid=(pair_count + 1,), in_specs=in_specs, out_spe...  32.9 us
    ppermute x1, waiting for transfers between devices, head_sum_scatter(): return own + lax.ppermute(other, 'head', [(0, 1), (1, 0)])  12.8 us
  transfers between devices with their start and end apart: 3, of which 3 were waited for; matrix products, arithmetic and copies ran while one was open for 2% of the time, Pallas kernels for 16%

profile of v18, /device:TPU:16, one launch (start us, length us, event | category | flops | bytes accessed | tf_op | source)
XLA Modules:
  0.0 137.8 jit_solution(15049383934877071632)
XLA Ops:
  6.5 0.0 slice-start
  6.5 0.0 slice-start.1
  6.5 0.0 all-gather.5.cloned.1.call-start
  6.5 1.1 slice.22
  7.6 0.0 copy-start
  7.6 1.2 slice.23
  8.8 1.0 pad_maximum_fusion
  9.7 0.0 all-gather.5.cloned.1.call-update
  9.8 0.0 all-gather.3.cloned.1.call-start
  9.8 0.0 slice-done
  9.8 0.0 slice-done.1
  9.8 0.7 pad_maximum_fusion.1
  10.6 0.0 all-gather.3.cloned.1.call-update
  10.6 0.0 copy-done
  10.6 1.3 slice.21.q_ref
  11.9 0.8 slice.18.q_ref
  12.7 61.7 %all-gather.5.cloned.1.call-done.kmax_ref.kmin_ref = f32[2048,768]{1,0:T(8,128)} async-done(((f32[256,768]{1,0:T(8,128)}), f32[2048,768]{1,0:T(8,128)}) %all-gather.5.cloned.1.call-update) | async-done | bytes 6291472 | tf_op jit(solution)/shard_map/all_gather | solution.py:207
  74.4 22.7 %shard_map.46.refs_0_ = f32[2048,128]{1,0:T(8,128)} custom-call(f32[128,3072]{1,0:T(8,128)} %slice.21.q_ref, f32[2048,768]{1,0:T(8,128)} %all-gather.5.cloned.1.call-done.kmax_ref.kmin_ref, f32[2048,768]{1,0:T(8,128)} %all-gather.5.cloned.1.call-done.kmax_ref.kmin_ref, s32[1,128]{1,0:T(1,128)} %bitcast.1), custom_call_target="tpu_custom_call" | custom-call | tf_op jit(solution)/shard_map/pallas_call | solution.py:173
  97.1 7.5 %all-gather.3.cloned.1.call-done.kmax_ref.kmin_ref = f32[2048,256]{1,0:T(8,128)} async-done(((f32[256,256]{1,0:T(8,128)}), f32[2048,256]{1,0:T(8,128)}) %all-gather.3.cloned.1.call-update) | async-done | bytes 2097168 | tf_op jit(solution)/shard_map/all_gather | solution.py:207
  104.6 10.1 %shard_map.47 = (f32[128,1024]{1,0:T(8,128)}, f32[128,1024]{1,0:T(8,128)}) custom-call(f32[128,1024]{1,0:T(8,128)} %slice.18.q_ref, f32[2048,256]{1,0:T(8,128)} %all-gather.3.cloned.1.call-done.kmax_ref.kmin_ref, f32[2048,256]{1,0:T(8,128)} %all-gather.3.cloned.1.call-done.kmax_ref.kmin_ref, s32[1,128]{1,0:T(1,128)} %bitcast.2, f32[2048,128]{1,0:T(8,128)} %shard_map.46.refs_0_), custom_call_target="tpu_custom_call" | custom-call | tf_op jit(solution)/shard_map/pallas_call | solution.py:173
  114.8 1.5 %collective-permute-start = (f32[128,1024]{1,0:T(8,128)}, f32[128,1024]{1,0:T(8,128)S(1)}, u32[]{:S(2)}, u32[]{:S(2)}) collective-permute-start(f32[128,1024]{1,0:T(8,128)} %get-tuple-element.8), channel_id=1, source_target_pairs={{0,2},{2,0},{1,3},{3,1},{4,6},{6,4},{5,7},{7,5},{8,10},{10,8},{9,1... | collective-permute-start | bytes 1572872 | tf_op jit(solution)/shard_map/ppermute | solution.py:195
  116.3 12.8 %collective-permute-done = f32[128,1024]{1,0:T(8,128)S(1)} collective-permute-done((f32[128,1024]{1,0:T(8,128)}, f32[128,1024]{1,0:T(8,128)S(1)}, u32[]{:S(2)}, u32[]{:S(2)}) %collective-permute-start) | collective-permute-done | bytes 524320 | tf_op jit(solution)/shard_map/ppermute | solution.py:195
  129.1 1.9 %add.3 = f32[128,1024]{1,0:T(8,128)} add(f32[128,1024]{1,0:T(8,128)} %get-tuple-element.7, f32[128,1024]{1,0:T(8,128)S(1)} %collective-permute-done) | non-fusion elementwise | flops 131072 | bytes 1572864 | tf_op jit(solution)/shard_map/add | solution.py:195
Async XLA Ops:
  6.5 3.3 %slice-start = ((f32[256,512]{1,0:T(8,128)}), f32[256,128]{1,0:T(8,128)S(1)}, s32[]{:S(2)}) async-start(f32[256,512]{1,0:T(8,128)} %param.5), calls=%async_computation.2 | async-start | bytes 262144 | tf_op jit(solution)/shard_map/slice | solution.py:207
  6.5 3.3 %slice-start.1 = ((f32[256,512]{1,0:T(8,128)}), f32[256,128]{1,0:T(8,128)S(1)}, s32[]{:S(2)}) async-start(f32[256,512]{1,0:T(8,128)} %param.6), calls=%async_computation.3 | async-start | bytes 262144 | tf_op jit(solution)/shard_map/slice | solution.py:207
  6.5 67.9 %all-gather.5.cloned.1.call-start = ((), (), s32[]{:S(2)}) async-start(), calls=%async_computation.1 | async-start | bytes 7077888 | tf_op jit(solution)/shard_map/all_gather | solution.py:207
  7.6 3.0 %copy-start = (f32[128,4096]{1,0:T(8,128)S(1)}, f32[128,4096]{1,0:T(8,128)}, u32[]{:S(2)}) copy-start(f32[128,4096]{1,0:T(8,128)} %param.4) | copy-start | bytes 6291460
  9.8 94.9 %all-gather.3.cloned.1.call-start = ((), (), s32[]{:S(2)}) async-start(), calls=%async_computation | async-start | bytes 2359296 | tf_op jit(solution)/shard_map/all_gather | solution.py:207
  114.8 14.3 %collective-permute-start = (f32[128,1024]{1,0:T(8,128)}, f32[128,1024]{1,0:T(8,128)S(1)}, u32[]{:S(2)}, u32[]{:S(2)}) collective-permute-start(f32[128,1024]{1,0:T(8,128)} %get-tuple-element.8), channel_id=1, source_target_pairs={{0,2},{2,0},{1,3},{3,1},{4,6},{6,4},{5,7},{7,5},{8,10},{10,8},{9,1... | collective-permute-start | bytes 1572872 | tf_op jit(solution)/shard_map/ppermute | solution.py:195
Sparse Core Ops, SparseCore 0:
  9.9 64.4 all-gather.4
  76.0 28.5 all-gather.2

commit v19 on v17

--- a/solution.py
+++ b/solution.py
@@ -135,9 +135,9 @@
 def page_mass_group(queries, kmax, kmin, limits, acc, last, halves=False):
     row_count = queries.shape[0]
     pair_count = queries.shape[1] // (2 * DH)
-    kv_in_group = kmax.shape[1] // (2 * DH)
+    kv_in_group = kmax.shape[2] // DH
     pairs_per_kv = pair_count // kv_in_group
-    page_count = kmax.shape[0]
+    page_count = kmax.shape[1]
     chunk_count = page_count // CHUNK
     first = acc is None
     kernel = functools.partial(
@@ -150,8 +150,8 @@
 
     in_specs = [
         pl.BlockSpec((row_count, 2 * DH), lambda j: (0, pair_of(j))),
-        pl.BlockSpec((page_count, DH), lambda j: (0, pair_of(j) // pairs_per_kv)),
-        pl.BlockSpec((page_count, DH), lambda j: (0, kv_in_group + pair_of(j) // pairs_per_kv)),
+        pl.BlockSpec((None, page_count, DH), lambda j: (0, 0, pair_of(j) // pairs_per_kv)),
+        pl.BlockSpec((None, page_count, DH), lambda j: (1, 0, pair_of(j) // pairs_per_kv)),
         pl.BlockSpec((1, row_count), lambda j: (0, 0)),
     ]
     operands = [queries, kmax, kmin, limits.reshape(1, row_count)]
@@ -204,8 +204,8 @@
     kv0 = 0
     for g, size in enumerate(sizes):
         span = slice(kv0 * DH, (kv0 + size) * DH)
-        keys = lax.all_gather(jnp.concatenate((key_max[:, span], key_min[:, span]), axis=1),
-                              ("row", "rep"), axis=0, tiled=True)
+        keys = lax.all_gather(jnp.stack((key_max[:, span], key_min[:, span])),
+                              ("row", "rep"), axis=1, tiled=True)
         cols = slice(kv0 * head_cols, (kv0 + size) * head_cols)
         last = g == len(sizes) - 1
         acc = page_mass_group(queries[:, cols], keys, keys, limits, acc, last=last,

time: 140 us -> 139 us (level)
    slice x6 -> x0, local copies, waits for them, and re-layouts: 2.24 us -> none  [the longest x3 1.18 us: per_device(): key_min[:, span]]
    another operation x0 -> x2, local copies, waits for them, and re-layouts: none -> 2.16 us  [per_device(): jnp.stack((key_max[:, span], key_min[:, span]))]
    another operation x0 -> x2, other arithmetic: none -> 1.7 us  [per_device(): jnp.stack((key_max[:, span], key_min[:, span]))]
    concatenate x2 -> x0, other arithmetic: 1.67 us -> none  [per_device(): jnp.concatenate((key_max[:, span], key_min[:, span]), axis=1)]
  transfers between devices with their start and end apart: 3 -> 3, of which waited for: 3 -> 3; matrix products, arithmetic and copies ran while one was open for 2% -> 3% of each run, Pallas kernels for 16% -> 16%
where the time goes in v19:
time: 139 us; the launch traced here: 137 us
  waiting for transfers between devices  81.8 us (59%)
  Pallas kernels  32.1 us (23%)
  between operations  13.4 us (10%)
  local copies, waits for them, and re-layouts  4.3 us (3%)
  other arithmetic  3.62 us (3%)
  starting transfers between devices  1.52 us (1%)
    all_gather x2, waiting for transfers between devices, per_device(): lax.all_gather(jnp.stack((key_max[:, span], key_min[:, span])), ('row', '...  69 us
    pallas_call x2, Pallas kernels, page_mass_group(): pl.pallas_call(kernel, grid=(pair_count + 1,), in_specs=in_specs, out_spe...  32.1 us
    ppermute x1, waiting for transfers between devices, head_sum_scatter(): return own + lax.ppermute(other, 'head', [(0, 1), (1, 0)])  12.8 us
  transfers between devices with their start and end apart: 3, of which 3 were waited for; matrix products, arithmetic and copies ran while one was open for 3% of the time, Pallas kernels for 16%

profile of v19, /device:TPU:16, one launch (start us, length us, event | category | flops | bytes accessed | tf_op | source)
XLA Modules:
  0.0 136.8 jit_solution(15992290681525187316)
XLA Ops:
  6.5 0.0 all-gather.5.cloned.1.call-start
  6.5 1.2 slice_bitcast_fusion
  7.7 0.0 copy-start
  7.7 1.0 pad_maximum_fusion
  8.7 0.0 all-gather.5.cloned.1.call-update
  8.7 0.0 all-gather.3.cloned.1.call-start
  8.8 1.0 slice_bitcast_fusion.2
  9.7 0.7 pad_maximum_fusion.1
  10.5 0.0 all-gather.3.cloned.1.call-update
  10.5 0.0 copy-done
  10.5 1.3 slice.21.q_ref
  11.8 0.8 slice.18.q_ref
  12.7 60.8 %all-gather.5.cloned.1.call-done.kmax_ref.kmin_ref = f32[2,2048,384]{2,1,0:T(8,128)} async-done(((f32[2,256,384]{2,1,0:T(8,128)}), f32[2,2048,384]{2,1,0:T(8,128)}) %all-gather.5.cloned.1.call-update) | async-done | bytes 6291472 | tf_op jit(solution)/shard_map/all_gather | solution.py:207
  73.5 22.1 %shard_map.46.refs_0_ = f32[2048,128]{1,0:T(8,128)} custom-call(f32[128,3072]{1,0:T(8,128)} %slice.21.q_ref, f32[2,2048,384]{2,1,0:T(8,128)} %all-gather.5.cloned.1.call-done.kmax_ref.kmin_ref, f32[2,2048,384]{2,1,0:T(8,128)} %all-gather.5.cloned.1.call-done.kmax_ref.kmin_ref, s32[1,128]{1,0:T(1,128)} %bitcast.9), custom_call_target="tpu_custom_call" | custom-call | tf_op jit(solution)/shard_map/pallas_call | solution.py:173
  95.5 8.2 %all-gather.3.cloned.1.call-done.kmax_ref.kmin_ref = f32[2,2048,128]{2,1,0:T(8,128)} async-done(((f32[2,256,128]{2,1,0:T(8,128)}), f32[2,2048,128]{2,1,0:T(8,128)}) %all-gather.3.cloned.1.call-update) | async-done | bytes 2097168 | tf_op jit(solution)/shard_map/all_gather | solution.py:207
  103.7 10.0 %shard_map.47 = (f32[128,1024]{1,0:T(8,128)}, f32[128,1024]{1,0:T(8,128)}) custom-call(f32[128,1024]{1,0:T(8,128)} %slice.18.q_ref, f32[2,2048,128]{2,1,0:T(8,128)} %all-gather.3.cloned.1.call-done.kmax_ref.kmin_ref, f32[2,2048,128]{2,1,0:T(8,128)} %all-gather.3.cloned.1.call-done.kmax_ref.kmin_ref, s32[1,128]{1,0:T(1,128)} %bitcast.10, ...), custom_call_target="tpu_custom_call" | custom-call | tf_op jit(solution)/shard_map/pallas_call | solution.py:173
  113.7 1.5 %collective-permute-start = (f32[128,1024]{1,0:T(8,128)}, f32[128,1024]{1,0:T(8,128)S(1)}, u32[]{:S(2)}, u32[]{:S(2)}) collective-permute-start(f32[128,1024]{1,0:T(8,128)} %get-tuple-element.8), channel_id=1, source_target_pairs={{0,2},{2,0},{1,3},{3,1},{4,6},{6,4},{5,7},{7,5},{8,10},{10,8},{9,1... | collective-permute-start | bytes 1572872 | tf_op jit(solution)/shard_map/ppermute | solution.py:195
  115.2 12.8 %collective-permute-done = f32[128,1024]{1,0:T(8,128)S(1)} collective-permute-done((f32[128,1024]{1,0:T(8,128)}, f32[128,1024]{1,0:T(8,128)S(1)}, u32[]{:S(2)}, u32[]{:S(2)}) %collective-permute-start) | collective-permute-done | bytes 524320 | tf_op jit(solution)/shard_map/ppermute | solution.py:195
  128.0 1.9 %add.3 = f32[128,1024]{1,0:T(8,128)} add(f32[128,1024]{1,0:T(8,128)} %get-tuple-element.7, f32[128,1024]{1,0:T(8,128)S(1)} %collective-permute-done) | non-fusion elementwise | flops 131072 | bytes 1572864 | tf_op jit(solution)/shard_map/add | solution.py:195
Async XLA Ops:
  6.5 66.9 %all-gather.5.cloned.1.call-start = ((), (), s32[]{:S(2)}) async-start(), calls=%async_computation.1 | async-start | bytes 7077888 | tf_op jit(solution)/shard_map/all_gather | solution.py:207
  7.7 2.8 %copy-start = (f32[128,4096]{1,0:T(8,128)S(1)}, f32[128,4096]{1,0:T(8,128)}, u32[]{:S(2)}) copy-start(f32[128,4096]{1,0:T(8,128)} %param.4) | copy-start | bytes 6291460
  8.7 95.0 %all-gather.3.cloned.1.call-start = ((), (), s32[]{:S(2)}) async-start(), calls=%async_computation | async-start | bytes 2359296 | tf_op jit(solution)/shard_map/all_gather | solution.py:207
  113.7 14.3 %collective-permute-start = (f32[128,1024]{1,0:T(8,128)}, f32[128,1024]{1,0:T(8,128)S(1)}, u32[]{:S(2)}, u32[]{:S(2)}) collective-permute-start(f32[128,1024]{1,0:T(8,128)} %get-tuple-element.8), channel_id=1, source_target_pairs={{0,2},{2,0},{1,3},{3,1},{4,6},{6,4},{5,7},{7,5},{8,10},{10,8},{9,1... | collective-permute-start | bytes 1572872 | tf_op jit(solution)/shard_map/ppermute | solution.py:195
Sparse Core Ops, SparseCore 0:
  9.0 64.4 all-gather.4
  75.1 28.5 all-gather.2

commit v20 on v19

--- a/solution.py
+++ b/solution.py
@@ -10,7 +10,7 @@
 
 DH = 128
 CHUNK = 256
-MM_CHUNK = 1024
+MM_CHUNK = 512
 
 
 def _split(x):

time: 139 us -> 139 us (level)
  transfers between devices with their start and end apart: 3 -> 3, of which waited for: 3 -> 3; matrix products, arithmetic and copies ran while one was open for 3% -> 3% of each run, Pallas kernels for 16% -> 15%
where the time goes in v20:
time: 139 us; the launch traced here: 136 us
  waiting for transfers between devices  82.8 us (60%)
  Pallas kernels  30.8 us (22%)
  between operations  13.4 us (10%)
  local copies, waits for them, and re-layouts  4.3 us (3%)
  other arithmetic  3.62 us (3%)
  starting transfers between devices  1.51 us (1%)
    all_gather x2, waiting for transfers between devices, per_device(): lax.all_gather(jnp.stack((key_max[:, span], key_min[:, span])), ('row', '...  70 us
    pallas_call x2, Pallas kernels, page_mass_group(): pl.pallas_call(kernel, grid=(pair_count + 1,), in_specs=in_specs, out_spe...  30.8 us
    ppermute x1, waiting for transfers between devices, head_sum_scatter(): return own + lax.ppermute(other, 'head', [(0, 1), (1, 0)])  12.8 us
  transfers between devices with their start and end apart: 3, of which 3 were waited for; matrix products, arithmetic and copies ran while one was open for 3% of the time, Pallas kernels for 15%

profile of v20, /device:TPU:16, one launch (start us, length us, event | category | flops | bytes accessed | tf_op | source)
XLA Modules:
  0.0 136.4 jit_solution(13059538387645475707)
XLA Ops:
  6.5 0.0 all-gather.5.cloned.1.call-start
  6.5 1.2 slice_bitcast_fusion
  7.7 0.0 copy-start
  7.7 1.0 pad_maximum_fusion
  8.7 0.0 all-gather.5.cloned.1.call-update
  8.7 0.0 all-gather.3.cloned.1.call-start
  8.8 1.0 slice_bitcast_fusion.2
  9.7 0.7 pad_maximum_fusion.1
  10.5 0.0 all-gather.3.cloned.1.call-update
  10.5 0.0 copy-done
  10.5 1.3 slice.21.q_ref
  11.8 0.8 slice.18.q_ref
  12.7 60.8 %all-gather.5.cloned.1.call-done.kmax_ref.kmin_ref = f32[2,2048,384]{2,1,0:T(8,128)} async-done(((f32[2,256,384]{2,1,0:T(8,128)}), f32[2,2048,384]{2,1,0:T(8,128)}) %all-gather.5.cloned.1.call-update) | async-done | bytes 6291472 | tf_op jit(solution)/shard_map/all_gather | solution.py:207
  73.5 21.1 %shard_map.46.refs_0_ = f32[2048,128]{1,0:T(8,128)} custom-call(f32[128,3072]{1,0:T(8,128)} %slice.21.q_ref, f32[2,2048,384]{2,1,0:T(8,128)} %all-gather.5.cloned.1.call-done.kmax_ref.kmin_ref, f32[2,2048,384]{2,1,0:T(8,128)} %all-gather.5.cloned.1.call-done.kmax_ref.kmin_ref, s32[1,128]{1,0:T(1,128)} %bitcast.9), custom_call_target="tpu_custom_call" | custom-call | tf_op jit(solution)/shard_map/pallas_call | solution.py:173
  94.6 9.1 %all-gather.3.cloned.1.call-done.kmax_ref.kmin_ref = f32[2,2048,128]{2,1,0:T(8,128)} async-done(((f32[2,256,128]{2,1,0:T(8,128)}), f32[2,2048,128]{2,1,0:T(8,128)}) %all-gather.3.cloned.1.call-update) | async-done | bytes 2097168 | tf_op jit(solution)/shard_map/all_gather | solution.py:207
  103.7 9.7 %shard_map.47 = (f32[128,1024]{1,0:T(8,128)}, f32[128,1024]{1,0:T(8,128)}) custom-call(f32[128,1024]{1,0:T(8,128)} %slice.18.q_ref, f32[2,2048,128]{2,1,0:T(8,128)} %all-gather.3.cloned.1.call-done.kmax_ref.kmin_ref, f32[2,2048,128]{2,1,0:T(8,128)} %all-gather.3.cloned.1.call-done.kmax_ref.kmin_ref, s32[1,128]{1,0:T(1,128)} %bitcast.10, ...), custom_call_target="tpu_custom_call" | custom-call | tf_op jit(solution)/shard_map/pallas_call | solution.py:173
  113.4 1.5 %collective-permute-start = (f32[128,1024]{1,0:T(8,128)}, f32[128,1024]{1,0:T(8,128)S(1)}, u32[]{:S(2)}, u32[]{:S(2)}) collective-permute-start(f32[128,1024]{1,0:T(8,128)} %get-tuple-element.8), channel_id=1, source_target_pairs={{0,2},{2,0},{1,3},{3,1},{4,6},{6,4},{5,7},{7,5},{8,10},{10,8},{9,1... | collective-permute-start | bytes 1572872 | tf_op jit(solution)/shard_map/ppermute | solution.py:195
  114.9 12.8 %collective-permute-done = f32[128,1024]{1,0:T(8,128)S(1)} collective-permute-done((f32[128,1024]{1,0:T(8,128)}, f32[128,1024]{1,0:T(8,128)S(1)}, u32[]{:S(2)}, u32[]{:S(2)}) %collective-permute-start) | collective-permute-done | bytes 524320 | tf_op jit(solution)/shard_map/ppermute | solution.py:195
  127.7 1.9 %add.3 = f32[128,1024]{1,0:T(8,128)} add(f32[128,1024]{1,0:T(8,128)} %get-tuple-element.7, f32[128,1024]{1,0:T(8,128)S(1)} %collective-permute-done) | non-fusion elementwise | flops 131072 | bytes 1572864 | tf_op jit(solution)/shard_map/add | solution.py:195
Async XLA Ops:
  6.5 66.9 %all-gather.5.cloned.1.call-start = ((), (), s32[]{:S(2)}) async-start(), calls=%async_computation.1 | async-start | bytes 7077888 | tf_op jit(solution)/shard_map/all_gather | solution.py:207
  7.7 2.8 %copy-start = (f32[128,4096]{1,0:T(8,128)S(1)}, f32[128,4096]{1,0:T(8,128)}, u32[]{:S(2)}) copy-start(f32[128,4096]{1,0:T(8,128)} %param.4) | copy-start | bytes 6291460
  8.7 95.0 %all-gather.3.cloned.1.call-start = ((), (), s32[]{:S(2)}) async-start(), calls=%async_computation | async-start | bytes 2359296 | tf_op jit(solution)/shard_map/all_gather | solution.py:207
  113.4 14.3 %collective-permute-start = (f32[128,1024]{1,0:T(8,128)}, f32[128,1024]{1,0:T(8,128)S(1)}, u32[]{:S(2)}, u32[]{:S(2)}) collective-permute-start(f32[128,1024]{1,0:T(8,128)} %get-tuple-element.8), channel_id=1, source_target_pairs={{0,2},{2,0},{1,3},{3,1},{4,6},{6,4},{5,7},{7,5},{8,10},{10,8},{9,1... | collective-permute-start | bytes 1572872 | tf_op jit(solution)/shard_map/ppermute | solution.py:195
Sparse Core Ops, SparseCore 0:
  9.0 64.4 all-gather.4
  75.1 28.5 all-gather.2
